TPU v7x, 256 devices: a whole 4x4x8 slice. The times are simulated.
256 devices in a mesh: seq: 64 (over y, z, core), head: 4 (over x).
Axes of the slice: x: 4, y: 4, z: 8, core: 2. Of those that a mesh axis runs over, the one named last changes fastest.
Arguments:
- queries: bfloat16 [32768, 4096], P(('seq', 'head')), may hold values from -6 to 6
- keys: bfloat16 [32768, 4096], P(('seq', 'head')), may hold values from -6 to 6
- values: bfloat16 [32768, 4096], P(('seq', 'head')), may hold values from -6 to 6
- cluster_ids: int32 [32, 32768, 1], P(None, 'seq'), may hold values from 0 to 127; in each aligned block of 128 rows (0 to 127, 128 to 255, ..., all dimensions but the last counted through in order) at most 2 rows name the same one
- out_weight: bfloat16 [4096, 4096], P('head', 'seq'), may hold values from -0.09375 to 0.09375
Outputs:
- projected: bfloat16 [32768, 4096], P('seq', 'head')
Inputs may be any that keep to these rules, and one draw needn't show every extreme that they name: `cluster_ids`: in each aligned block of 128 tokens of one head (the rows of one device), no cluster id appears more than 2 times, and some cluster appears exactly 2 times.
All inputs are finite; a program needn't handle non-finite values.
Results may differ from a plain program's by a relative error of at most 0.014.
Values may be sent and summed in bfloat16 or wider, within the bound.
No kernel may reach another device: no remote copies, remote signals or barrier semaphores. Data moves between devices by JAX's collectives and lax.ppermute only.
A program may use at most 128 MiB of HBM per device.

v0:
```python
import jax
import jax.numpy as jnp
from jax import lax
from jax.sharding import PartitionSpec as P

HEADS = 32
HD = 128
CLUSTERS = 128


def slot_table(block_ids, slot_depth):
    sub_rows = block_ids.shape[-1]
    onehot = (block_ids[..., None] == jnp.arange(CLUSTERS, dtype=jnp.int32)).astype(jnp.float32)
    lower = (jnp.arange(sub_rows)[:, None] >= jnp.arange(sub_rows)[None, :]).astype(jnp.float32)
    running = jnp.einsum("ts,abse->abte", lower, onehot)
    ranking = (jnp.sum(running * onehot, axis=-1) - 1.0).astype(jnp.int32)
    depth_hit = (ranking[..., None] == jnp.arange(slot_depth, dtype=jnp.int32)).astype(jnp.bfloat16)
    return onehot.astype(jnp.bfloat16)[..., :, None] * depth_hit[..., None, :]


def attend_blocks(packed, validity):
    scores = jnp.einsum(
        "cqd,ckd->cqk", packed[0], packed[1], preferred_element_type=jnp.float32
    ) * HD ** (-0.5)
    scores = jnp.where(validity[:, None, :] > 0, scores, -1e30)
    row_max = jnp.max(scores, axis=-1, keepdims=True)
    raised = jnp.exp(scores - row_max)
    weights = (raised / jnp.sum(raised, axis=-1, keepdims=True)).astype(jnp.bfloat16)
    return jnp.einsum(
        "cqk,ckd->cqd", weights, packed[2], preferred_element_type=jnp.float32
    ).astype(jnp.bfloat16)


def attend_and_return(arrived):
    packed, markers = arrived
    item_count = packed.shape[1]
    n_seq = packed.shape[2]
    lane_count = packed.shape[3]
    result_block = attend_blocks(
        packed.reshape(3, item_count, n_seq * lane_count, HD),
        markers.reshape(item_count, n_seq * lane_count),
    )
    result_block = result_block.reshape(item_count, n_seq, lane_count, HD)
    return lax.all_to_all(result_block, "seq", split_axis=1, concat_axis=1, tiled=True)


def body(queries, keys, values, cluster_ids, out_weight):
    n_seq = lax.axis_size("seq")
    n_head = lax.axis_size("head")
    head_group = lax.axis_index("head")
    tok_dev = cluster_ids.shape[1]
    sub_rows = tok_dev // n_head
    group_heads = HEADS // n_head
    slot_depth = max(2, 2 * tok_dev // (n_head * CLUSTERS))
    lane_count = n_head * slot_depth
    per_owner = group_heads * CLUSTERS // n_seq
    all_ids = cluster_ids[:, :, 0]
    group_ids = lax.dynamic_slice_in_dim(all_ids, head_group * group_heads, group_heads, 0)
    group_ids = group_ids.reshape(group_heads, n_head, sub_rows)
    home_table = slot_table(group_ids, slot_depth)
    relaid = (
        lax.all_to_all(queries, "head", split_axis=1, concat_axis=0, tiled=True),
        lax.all_to_all(keys, "head", split_axis=1, concat_axis=0, tiled=True),
        lax.all_to_all(values, "head", split_axis=1, concat_axis=0, tiled=True),
    )
    stacked = jnp.stack([tensor.reshape(n_head, sub_rows, group_heads, HD) for tensor in relaid])
    packed = jnp.einsum(
        "hltcr,xlthd->xhclrd", home_table, stacked, preferred_element_type=jnp.float32
    ).astype(jnp.bfloat16)
    packed = packed.reshape(3, per_owner, n_seq, lane_count, HD)
    markers = (
        jnp.sum(home_table.astype(jnp.float32), axis=2).transpose(0, 2, 1, 3).astype(jnp.bfloat16)
    )
    markers = markers.reshape(1, per_owner, n_seq, lane_count)
    returned = attend_and_return(
        (
            lax.all_to_all(packed, "seq", split_axis=2, concat_axis=2, tiled=True),
            lax.all_to_all(markers, "seq", split_axis=2, concat_axis=2, tiled=True),
        )
    )
    returned = returned.reshape(group_heads, CLUSTERS, n_head, slot_depth, HD)
    gathered = jnp.einsum(
        "hltcr,hclrd->lthd", home_table, returned, preferred_element_type=jnp.float32
    ).astype(jnp.bfloat16)
    gathered = gathered.reshape(tok_dev, group_heads * HD)
    partial_value = jnp.dot(
        gathered,
        lax.all_gather(out_weight, "seq", axis=1, tiled=True),
        preferred_element_type=jnp.float32,
    )
    return lax.psum_scatter(
        partial_value.astype(jnp.bfloat16), "head", scatter_dimension=1, tiled=True
    )


def solution(mesh):
    in_specs = (
        P(("seq", "head"), None),
        P(("seq", "head"), None),
        P(("seq", "head"), None),
        P(None, "seq", None),
        P("head", "seq"),
    )
    out_specs = P("seq", "head")
    return jax.shard_map(body, mesh=mesh, in_specs=in_specs, out_specs=out_specs, check_vma=False)
```

profile of v0, /device:TPU:1, one launch (start us, length us, event | category | flops | bytes accessed | tf_op | source)
XLA Modules:
  0.0 417.8 jit_solution(13506348038587240276)
XLA Ops:
  6.5 0.0 copy-start
  6.5 0.0 copy-start.2
  6.5 2.4 copy.54
  8.9 4.8 %all-to-all-start.1 = ((bf16[128,4,1024]{0,2,1:T(8,128)(2,1)}), bf16[128,4,1024]{0,2,1:T(8,128)(2,1)S(1)}, u32[]{:S(2)}, u32[]{:S(2)}) async-start(bf16[128,4,1024]{0,2,1:T(8,128)(2,1)} %bitcast.6), calls=%async_computation.1 | async-start | bytes 2097152 | tf_op jit(solution)/shard_map/all_to_all | solution.py:62
  13.7 0.0 copy-done.2
  13.7 1.3 copy.55
  15.1 11.9 %all-to-all-done.1 = bf16[128,4,1024]{0,2,1:T(8,128)(2,1)S(1)} async-done(((bf16[128,4,1024]{0,2,1:T(8,128)(2,1)}), bf16[128,4,1024]{0,2,1:T(8,128)(2,1)S(1)}, u32[]{:S(2)}, u32[]{:S(2)}) %all-to-all-start.1) | async-done | bytes 1048608 | tf_op jit(solution)/shard_map/all_to_all | solution.py:62
  27.0 3.5 all-to-all-start.2
  30.5 2.3 copy.56
  32.8 0.0 copy-done
  32.8 1.2 convert_convert_fusion
  34.0 8.5 %all-to-all-done.2 = bf16[128,4,1024]{0,2,1:T(8,128)(2,1)S(1)} async-done(((bf16[128,4,1024]{0,2,1:T(8,128)(2,1)}), bf16[128,4,1024]{0,2,1:T(8,128)(2,1)S(1)}, u32[]{:S(2)}, u32[]{:S(2)}) %all-to-all-start.2) | async-done | bytes 1048608 | tf_op jit(solution)/shard_map/all_to_all | solution.py:63
  42.5 4.2 %all-to-all-start.3 = ((bf16[128,4,1024]{0,2,1:T(8,128)(2,1)}), bf16[128,4,1024]{0,2,1:T(8,128)(2,1)}, u32[]{:S(2)}, u32[]{:S(2)}) async-start(bf16[128,4,1024]{0,2,1:T(8,128)(2,1)} %bitcast.12), calls=%async_computation.3 | async-start | bytes 2097152 | tf_op jit(solution)/shard_map/all_to_all | solution.py:64
  46.7 0.7 fusion.18
  47.4 1.6 copy.49
  49.1 2.5 multiply_reduce_fusion
  51.6 0.1 reshape.61
  51.7 0.8 copy.52
  52.5 1.3 copy.57
  53.8 0.0 copy-start.3
  53.8 1.3 copy.58
  55.1 2.5 all-to-all-done.3
  57.6 19.1 %all-to-all-start = ((bf16[1,16,64,8]{1,3,0,2:T(8,128)(2,1)}), bf16[1,16,64,8]{1,3,0,2:T(8,128)(2,1)S(1)}, u32[]{:S(2)}, u32[]{:S(2)}) async-start(bf16[1,16,64,8]{1,3,0,2:T(8,128)(2,1)} %copy.52), calls=%async_computation | async-start | bytes 262144 | tf_op jit(solution)/shard_map/all_to_all | solution.py:78
  76.7 1.6 copy.59
  78.3 0.0 copy-done.3
  78.4 3.8 convert_bitcast_fusion
  82.1 2.6 copy.61
  84.8 6.7 %copy.62 = bf16[3,16,64,8,128]{4,1,3,0,2:T(8,128)(2,1)} copy(bf16[3,16,64,8,128]{4,2,1,3,0:T(8,128)(2,1)S(1)} %bitcast.66) | data formatting | bytes 12582912 | tf_op jit(solution)/shard_map/reshape | solution.py:70
  91.4 0.0 all-to-all-done
  91.4 10.5 %all-to-all-start.4 = ((bf16[3,16,64,8,128]{4,1,3,0,2:T(8,128)(2,1)}), bf16[3,16,64,8,128]{4,1,3,0,2:T(8,128)(2,1)}, u32[]{:S(2)}, u32[]{:S(2)}) async-start(bf16[3,16,64,8,128]{4,1,3,0,2:T(8,128)(2,1)} %copy.62), calls=%async_computation.4 | async-start | bytes 12582912 | tf_op jit(solution)/shard_map/all_to_all | solution.py:77
  101.9 0.0 all-gather.2.cloned.1.call-start
  102.0 0.7 all-gather.2.cloned.1.call-update
  102.7 0.3 reduce-scatter.2.cloned.1.call-start
  103.0 0.1 copy.53
  103.1 164.3 %all-to-all-done.4 = bf16[3,16,64,8,128]{4,1,3,0,2:T(8,128)(2,1)} async-done(((bf16[3,16,64,8,128]{4,1,3,0,2:T(8,128)(2,1)}), bf16[3,16,64,8,128]{4,1,3,0,2:T(8,128)(2,1)}, u32[]{:S(2)}, u32[]{:S(2)}) %all-to-all-start.4) | async-done | bytes 6291488 | tf_op jit(solution)/shard_map/all_to_all | solution.py:77
  267.4 6.0 %fusion.45 = (bf16[1,16,64,8,128]{4,1,3,0,2:T(8,128)(2,1)S(1)}, bf16[1,16,64,8,128]{4,1,3,0,2:T(8,128)(2,1)}, bf16[1,16,64,8,128]{4,1,3,0,2:T(8,128)(2,1)S(1)}) fusion(bf16[3,16,64,8,128]{4,1,3,0,2:T(8,128)(2,1)} %all-to-all-done.4), kind=kLoop, calls=%fused_computation.52 | loop fusion | bytes 12582912 | tf_op jit(solution)/shard_map/slice | solution.py:23
  273.4 2.4 fusion.14
  275.8 8.1 %fusion.46 = (f32[16,512]{1,0:T(8,128)S(1)}, f32[16,512,512]{1,2,0:T(8,128)}) fusion(f32[16,512,512]{1,2,0:T(8,128)S(1)} %fusion.14, pred[16,512]{1,0:T(8,128)(4,1)S(1)} %copy.53), kind=kOutput, calls=%fused_computation.53 | output fusion | flops 25166336 | bytes 33595392 | tf_op jit(solution)/shard_map/sub | solution.py:27
  283.9 9.4 %convert_bitcast_fusion.1 = bf16[16,64,8,128]{3,2,1,0:T(8,128)(2,1)S(1)} fusion(bf16[1,16,64,8,128]{4,1,3,0,2:T(8,128)(2,1)} %get-tuple-element.6, f32[16,512,512]{1,2,0:T(8,128)} %get-tuple-element.11, f32[16,512]{1,0:T(8,128)S(1)} %get-tuple-element.10), kind=kOutput, calls=%fused_computation.32 | convolution fusion | flops 1083179008 | bytes 21004288 | tf_op jit(solution)/shard_map/cqk,ckd->cqd/dot_general | solution.py:29
  293.3 2.4 copy.67
  295.8 56.8 %all_to_all.63 = bf16[16,64,8,128]{3,0,2,1:T(8,128)(2,1)S(1)} all-to-all(bf16[16,64,8,128]{3,0,2,1:T(8,128)(2,1)S(1)} %copy.67), channel_id=1, replica_groups=mesh['seq'=64,'head'=4] {'seq'}, dimensions={1} | all-to-all | bytes 4194304 | tf_op jit(solution)/shard_map/all_to_all | solution.py:44
  352.6 1.4 copy.68
  354.0 2.6 fusion.29
  356.5 0.7 copy.70
  357.3 0.0 all-gather.2.cloned.1.call-done
  357.3 0.0 copy-start.1
  357.3 9.5 %convolution_convert_fusion = bf16[512,4096]{1,0:T(8,128)(2,1)} fusion(bf16[1024,4096]{0,1:T(8,128)(2,1)} %all-gather.2.cloned.1.call-done, bf16[64,8,8,128]{3,2,1,0:T(8,128)(2,1)S(1)} %bitcast.70), kind=kOutput, calls=%fused_computation.10 | convolution fusion | flops 4297064448 | bytes 13631488 | tf_op jit(solution)/shard_map/dot_general | solution.py:86
  366.8 0.0 reduce-scatter.2.cloned.1.call-update
  366.8 44.2 %reduce-scatter.2.cloned.1.call-done = bf16[512,1024]{1,0:T(8,128)(2,1)} async-done(((bf16[512,4096]{1,0:T(8,128)(2,1)}), bf16[512,1024]{1,0:T(8,128)(2,1)}) %reduce-scatter.2.cloned.1.call-update) | async-done | bytes 1048592 | tf_op jit(solution)/shard_map/reduce_scatter | solution.py:91
  411.0 0.0 copy-done.1
  (5 shorter events, 0.1 us)
Async XLA Ops:
  6.5 26.2 %copy-start = (s32[32,512,1]{1,2,0:T(1,128)S(1)}, s32[32,512,1]{1,2,0:T(1,128)}, u32[]{:S(2)}) copy-start(s32[32,512,1]{1,2,0:T(1,128)} %param.8) | copy-start | bytes 196612
  6.5 7.2 %copy-start.2 = (bf16[128,4096]{1,0:T(8,128)(2,1)S(1)}, bf16[128,4096]{1,0:T(8,128)(2,1)}, u32[]{:S(2)}) copy-start(bf16[128,4096]{1,0:T(8,128)(2,1)} %param.6) | copy-start | bytes 3145732
  8.9 18.1 %all-to-all-start.1 = ((bf16[128,4,1024]{0,2,1:T(8,128)(2,1)}), bf16[128,4,1024]{0,2,1:T(8,128)(2,1)S(1)}, u32[]{:S(2)}, u32[]{:S(2)}) async-start(bf16[128,4,1024]{0,2,1:T(8,128)(2,1)} %bitcast.6), calls=%async_computation.1 | async-start | bytes 2097152 | tf_op jit(solution)/shard_map/all_to_all | solution.py:62
  27.0 15.5 %all-to-all-start.2 = ((bf16[128,4,1024]{0,2,1:T(8,128)(2,1)}), bf16[128,4,1024]{0,2,1:T(8,128)(2,1)S(1)}, u32[]{:S(2)}, u32[]{:S(2)}) async-start(bf16[128,4,1024]{0,2,1:T(8,128)(2,1)} %bitcast.9), calls=%async_computation.2 | async-start | bytes 2097152 | tf_op jit(solution)/shard_map/all_to_all | solution.py:63
  42.5 15.1 %all-to-all-start.3 = ((bf16[128,4,1024]{0,2,1:T(8,128)(2,1)}), bf16[128,4,1024]{0,2,1:T(8,128)(2,1)}, u32[]{:S(2)}, u32[]{:S(2)}) async-start(bf16[128,4,1024]{0,2,1:T(8,128)(2,1)} %bitcast.12), calls=%async_computation.3 | async-start | bytes 2097152 | tf_op jit(solution)/shard_map/all_to_all | solution.py:64
  53.8 24.6 %copy-start.3 = (bf16[1,4,128,8,128]{4,2,0,1,3:T(8,128)(2,1)S(1)}, bf16[1,4,128,8,128]{4,2,0,1,3:T(8,128)(2,1)}, u32[]{:S(2)}) copy-start(bf16[1,4,128,8,128]{4,2,0,1,3:T(8,128)(2,1)} %copy.57) | copy-start | bytes 3145732
  57.6 33.8 %all-to-all-start = ((bf16[1,16,64,8]{1,3,0,2:T(8,128)(2,1)}), bf16[1,16,64,8]{1,3,0,2:T(8,128)(2,1)S(1)}, u32[]{:S(2)}, u32[]{:S(2)}) async-start(bf16[1,16,64,8]{1,3,0,2:T(8,128)(2,1)} %copy.52), calls=%async_computation | async-start | bytes 262144 | tf_op jit(solution)/shard_map/all_to_all | solution.py:78
  91.4 175.9 %all-to-all-start.4 = ((bf16[3,16,64,8,128]{4,1,3,0,2:T(8,128)(2,1)}), bf16[3,16,64,8,128]{4,1,3,0,2:T(8,128)(2,1)}, u32[]{:S(2)}, u32[]{:S(2)}) async-start(bf16[3,16,64,8,128]{4,1,3,0,2:T(8,128)(2,1)} %copy.62), calls=%async_computation.4 | async-start | bytes 12582912 | tf_op jit(solution)/shard_map/all_to_all | solution.py:77
  101.9 255.3 %all-gather.2.cloned.1.call-start = ((), (), s32[]{:S(2)}) async-start(), calls=%async_computation.7 | async-start | bytes 8519680 | tf_op jit(solution)/shard_map/all_gather | solution.py:88
  102.7 308.3 %reduce-scatter.2.cloned.1.call-start = ((), (), s32[]{:S(2)}) async-start(), calls=%async_computation.8 | async-start | bytes 5242880 | tf_op jit(solution)/shard_map/reduce_scatter | solution.py:91
  357.3 53.7 %copy-start.1 = (s32[32,512,1]{1,2,0:T(1,128)S(1)}, s32[32,512,1]{1,2,0:T(1,128)}, u32[]{:S(2)}) copy-start(s32[32,512,1]{1,2,0:T(1,128)} %param.8) | copy-start | bytes 196612
Sparse Core Ops, SparseCore 0:
  105.6 134.2 all-gather.1
  366.9 43.9 reduce-scatter.1
where the time goes:
time: 418 us
  waiting for transfers between devices  232 us (56%)
  blocking collectives  56.8 us (14%)
  starting transfers between devices  42.5 us (10%)
  local copies, waits for them, and re-layouts  32.7 us (8%)
  matrix products  28.3 us (7%)
  between operations  13.6 us (3%)
  other arithmetic  11.9 us (3%)
    all_to_all x1, waiting for transfers between devices, body(): lax.all_to_all(packed, 'seq', split_axis=2, concat_axis=2, tiled=True)  164 us
    all_to_all x1, blocking collectives, attend_and_return(): lax.all_to_all(result_block, 'seq', split_axis=1, concat_axis=1, tiled=True)  56.8 us
    reduce_scatter x1, waiting for transfers between devices, body(): lax.psum_scatter(partial_value.astype(jnp.bfloat16), 'head', scatter_dime...  44.2 us
    all_to_all x1, starting transfers between devices, body(): lax.all_to_all(markers, 'seq', split_axis=2, concat_axis=2, tiled=True)  19.1 us
    all_to_all x1, waiting for transfers between devices, body(): lax.all_to_all(queries, 'head', split_axis=1, concat_axis=0, tiled=True)  11.9 us
    all_to_all x1, starting transfers between devices, body(): lax.all_to_all(packed, 'seq', split_axis=2, concat_axis=2, tiled=True)  10.5 us
    dot_general x1, matrix products, body(): jnp.dot(gathered, lax.all_gather(out_weight, 'seq', axis=1, tiled=True),...  9.49 us
    dot_general x1, matrix products, attend_blocks(): jnp.einsum('cqk,ckd->cqd', weights, packed[2], preferred_element_type=jnp...  9.4 us
  transfers between devices with their start and end apart: 7, of which 5 were waited for; matrix products, arithmetic and copies ran while one was open for 15% of the time, Pallas kernels for 0%

commit v1 on v0

--- a/solution.py
+++ b/solution.py
@@ -31,19 +31,6 @@
     ).astype(jnp.bfloat16)
 
 
-def attend_and_return(arrived):
-    packed, markers = arrived
-    item_count = packed.shape[1]
-    n_seq = packed.shape[2]
-    lane_count = packed.shape[3]
-    result_block = attend_blocks(
-        packed.reshape(3, item_count, n_seq * lane_count, HD),
-        markers.reshape(item_count, n_seq * lane_count),
-    )
-    result_block = result_block.reshape(item_count, n_seq, lane_count, HD)
-    return lax.all_to_all(result_block, "seq", split_axis=1, concat_axis=1, tiled=True)
-
-
 def body(queries, keys, values, cluster_ids, out_weight):
     n_seq = lax.axis_size("seq")
     n_head = lax.axis_size("head")
@@ -52,33 +39,34 @@
     sub_rows = tok_dev // n_head
     group_heads = HEADS // n_head
     slot_depth = max(2, 2 * tok_dev // (n_head * CLUSTERS))
-    lane_count = n_head * slot_depth
     per_owner = group_heads * CLUSTERS // n_seq
+    n_src = n_seq * n_head
     all_ids = cluster_ids[:, :, 0]
+
+    own_ids = lax.dynamic_slice_in_dim(all_ids, head_group * sub_rows, sub_rows, 1)
+    own_table = slot_table(own_ids[:, None, :], slot_depth)[:, 0]
+    stacked = jnp.stack([t.reshape(sub_rows, HEADS, HD) for t in (queries, keys, values)])
+    packed = jnp.einsum(
+        "htcr,xthd->xhcrd", own_table, stacked, preferred_element_type=jnp.float32
+    ).astype(jnp.bfloat16)
+    packed = packed.reshape(3, n_head, per_owner, n_seq, slot_depth, HD)
+    packed = packed.transpose(0, 3, 1, 2, 4, 5).reshape(3, n_src, per_owner, slot_depth, HD)
+    markers = jnp.sum(own_table.astype(jnp.float32), axis=1).astype(jnp.bfloat16)
+    markers = markers.reshape(n_head, per_owner, n_seq, slot_depth)
+    markers = markers.transpose(2, 0, 1, 3).reshape(n_src, per_owner, slot_depth)
+
+    arrived = lax.all_to_all(packed, ("seq", "head"), split_axis=1, concat_axis=1, tiled=True)
+    valid = lax.all_to_all(markers, ("seq", "head"), split_axis=0, concat_axis=0, tiled=True)
+    arrived = arrived.transpose(0, 2, 1, 3, 4).reshape(3, per_owner, n_src * slot_depth, HD)
+    valid = valid.transpose(1, 0, 2).reshape(per_owner, n_src * slot_depth)
+    result_block = attend_blocks(arrived, valid)
+    result_block = result_block.reshape(per_owner, n_seq, n_head * slot_depth, HD)
+    returned = lax.all_to_all(result_block, "seq", split_axis=1, concat_axis=1, tiled=True)
+    returned = returned.reshape(group_heads, CLUSTERS, n_head, slot_depth, HD)
+
     group_ids = lax.dynamic_slice_in_dim(all_ids, head_group * group_heads, group_heads, 0)
     group_ids = group_ids.reshape(group_heads, n_head, sub_rows)
     home_table = slot_table(group_ids, slot_depth)
-    relaid = (
-        lax.all_to_all(queries, "head", split_axis=1, concat_axis=0, tiled=True),
-        lax.all_to_all(keys, "head", split_axis=1, concat_axis=0, tiled=True),
-        lax.all_to_all(values, "head", split_axis=1, concat_axis=0, tiled=True),
-    )
-    stacked = jnp.stack([tensor.reshape(n_head, sub_rows, group_heads, HD) for tensor in relaid])
-    packed = jnp.einsum(
-        "hltcr,xlthd->xhclrd", home_table, stacked, preferred_element_type=jnp.float32
-    ).astype(jnp.bfloat16)
-    packed = packed.reshape(3, per_owner, n_seq, lane_count, HD)
-    markers = (
-        jnp.sum(home_table.astype(jnp.float32), axis=2).transpose(0, 2, 1, 3).astype(jnp.bfloat16)
-    )
-    markers = markers.reshape(1, per_owner, n_seq, lane_count)
-    returned = attend_and_return(
-        (
-            lax.all_to_all(packed, "seq", split_axis=2, concat_axis=2, tiled=True),
-            lax.all_to_all(markers, "seq", split_axis=2, concat_axis=2, tiled=True),
-        )
-    )
-    returned = returned.reshape(group_heads, CLUSTERS, n_head, slot_depth, HD)
     gathered = jnp.einsum(
         "hltcr,hclrd->lthd", home_table, returned, preferred_element_type=jnp.float32
     ).astype(jnp.bfloat16)

time: 418 us -> 386 us (0.923)
  blocking collectives: 56.8 us -> 0 us
  waiting for transfers between devices: 232 us -> 260 us
  other arithmetic: 11.9 us -> 1.93 us
  matrix products: 28.3 us -> 35.4 us
  starting transfers between devices: 42.5 us -> 35.8 us
  local copies, waits for them, and re-layouts: 32.7 us -> 38.6 us
    all_to_all x1 -> x0, blocking collectives: 56.8 us -> none  [attend_and_return(): lax.all_to_all(result_block, 'seq', split_axis=1, concat_axis=1, tiled=True)]
    all_to_all x5 -> x3, waiting for transfers between devices: 187 us -> 216 us  [the longest x1 167 us: body(): lax.all_to_all(packed, ('seq', 'head'), split_axis=1, concat_axis=1, tile...]
    slice x0 -> x3, local copies, waits for them, and re-layouts: none -> 10.6 us  [the longest x2 7.36 us: attend_blocks(): packed[1]]
    sub x0 -> x1, matrix products: none -> 9.84 us  [attend_blocks(): raised = jnp.exp(scores - row_max)]
    sub x1 -> x0, other arithmetic: 8.12 us -> none  [attend_blocks(): raised = jnp.exp(scores - row_max)]
    all_to_all x5 -> x3, starting transfers between devices: 42.2 us -> 35.5 us  [the longest x1 15.7 us: body(): lax.all_to_all(markers, ('seq', 'head'), split_axis=0, concat_axis=0, til...]
    transpose x0 -> x2, local copies, waits for them, and re-layouts: none -> 4.19 us  [the longest x1 4.05 us: body(): packed.transpose(0, 3, 1, 2, 4, 5)]
  transfers between devices with their start and end apart: 7 -> 5, of which waited for: 5 -> 3; matrix products, arithmetic and copies ran while one was open for 15% -> 16% of each run, Pallas kernels for 0% -> 0%
where the time goes in v1:
time: 386 us; the launch traced here: 385 us
  waiting for transfers between devices  260 us (67%)
  local copies, waits for them, and re-layouts  38.6 us (10%)
  starting transfers between devices  35.8 us (9%)
  matrix products  35.4 us (9%)
  between operations  13.7 us (4%)
    all_to_all x1, waiting for transfers between devices, body(): lax.all_to_all(packed, ('seq', 'head'), split_axis=1, concat_axis=1, tile...  167 us
    all_to_all x1, waiting for transfers between devices, body(): lax.all_to_all(result_block, 'seq', split_axis=1, concat_axis=1, tiled=True)  48.7 us
    reduce_scatter x1, waiting for transfers between devices, body(): lax.psum_scatter(partial_value.astype(jnp.bfloat16), 'head', scatter_dime...  43.6 us
    all_to_all x1, starting transfers between devices, body(): lax.all_to_all(markers, ('seq', 'head'), split_axis=0, concat_axis=0, til...  15.7 us
    all_to_all x1, starting transfers between devices, body(): lax.all_to_all(packed, ('seq', 'head'), split_axis=1, concat_axis=1, tile...  14.6 us
    sub x1, matrix products, attend_blocks(): raised = jnp.exp(scores - row_max)  9.84 us
    dot_general x1, matrix products, body(): jnp.dot(gathered, lax.all_gather(out_weight, 'seq', axis=1, tiled=True),...  9.49 us
    dot_general x1, matrix products, attend_blocks(): jnp.einsum('cqk,ckd->cqd', weights, packed[2], preferred_element_type=jnp...  8.9 us
  transfers between devices with their start and end apart: 5, of which 3 were waited for; matrix products, arithmetic and copies ran while one was open for 16% of the time, Pallas kernels for 0%

profile of v1, /device:TPU:1, one launch (start us, length us, event | category | flops | bytes accessed | tf_op | source)
XLA Modules:
  0.0 385.3 jit_solution(9638940476264557998)
XLA Ops:
  6.5 0.0 copy-start
  6.5 0.8 copy-done
  7.4 0.3 convert_convert_fusion.1
  7.7 0.0 copy-start.1
  7.7 0.7 fusion.10
  8.4 1.2 multiply_reduce_fusion
  9.6 0.1 reshape.102
  9.7 0.1 copy.41
  9.8 0.8 copy.42
  10.6 15.7 %all-to-all-start = ((bf16[256,16,2]{1,2,0:T(2,128)(2,1)}), bf16[256,16,2]{1,2,0:T(2,128)(2,1)S(1)}, u32[]{:S(2)}, u32[]{:S(2)}) async-start(bf16[256,16,2]{1,2,0:T(2,128)(2,1)} %copy.42), calls=%async_computation | async-start | bytes 262144 | tf_op jit(solution)/shard_map/all_to_all | solution.py:59
  26.3 0.0 copy-done.1
  26.3 0.7 copy.44
  27.0 0.0 copy-start.2
  27.0 1.3 copy.47
  28.3 0.0 copy-done.2
  28.3 0.7 copy.45
  29.0 0.0 copy-start.3
  29.0 1.3 copy.48
  30.3 0.0 copy-done.3
  30.3 0.7 copy.46
  31.0 0.0 copy-start.5
  31.0 1.3 copy.49
  32.3 0.0 copy-done.5
  32.3 3.3 convert_bitcast_fusion
  35.6 2.6 copy.50
  38.3 4.0 %copy.51 = bf16[3,64,4,16,2,128]{5,3,4,2,1,0:T(8,128)(2,1)S(1)} copy(bf16[3,64,4,16,2,128]{5,1,3,2,4,0:T(8,128)(2,1)S(1)} %bitcast.72) | data formatting | bytes 12582912 | tf_op jit(solution)/shard_map/transpose | solution.py:53
  42.3 3.7 copy.52
  46.0 0.0 all-to-all-done
  46.0 14.6 %all-to-all-start.1 = ((bf16[3,256,16,2,128]{4,2,3,0,1:T(8,128)(2,1)}), bf16[3,256,16,2,128]{4,2,3,0,1:T(8,128)(2,1)}, u32[]{:S(2)}, u32[]{:S(2)}) async-start(bf16[3,256,16,2,128]{4,2,3,0,1:T(8,128)(2,1)} %copy.52), calls=%async_computation.1 | async-start | bytes 12582912 | tf_op jit(solution)/shard_map/all_to_all | solution.py:58
  60.6 0.3 all-gather.2.cloned.1.call-start
  60.9 0.5 all-gather.2.cloned.1.call-update
  61.4 0.2 compare_bitcast_fusion
  61.5 0.2 gt.20
  61.7 0.1 copy.43
  61.8 167.1 %all-to-all-done.1 = bf16[3,256,16,2,128]{4,2,3,0,1:T(8,128)(2,1)} async-done(((bf16[3,256,16,2,128]{4,2,3,0,1:T(8,128)(2,1)}), bf16[3,256,16,2,128]{4,2,3,0,1:T(8,128)(2,1)}, u32[]{:S(2)}, u32[]{:S(2)}) %all-to-all-start.1) | async-done | bytes 6291488 | tf_op jit(solution)/shard_map/all_to_all | solution.py:58
  229.0 4.2 %fusion.43 = (bf16[1,16,256,2,128]{4,1,3,0,2:T(8,128)(2,1)S(1)}, bf16[1,16,256,2,128]{4,1,3,0,2:T(8,128)(2,1)S(1)}, bf16[1,16,256,2,128]{4,1,3,0,2:T(8,128)(2,1)S(1)}) fusion(bf16[3,16,256,2,128]{4,1,3,0,2:T(8,128)(2,1)} %bitcast.18), kind=kLoop, calls=%fused_computation.58 | loop fusion | bytes 12582912 | tf_op jit(solution)/shard_map/slice | solution.py:23
  233.1 2.0 copy.53
  235.2 3.2 copy.54
  238.4 3.3 copy.55
  241.6 9.8 %fusion.44 = (f32[16,512]{1,0:T(8,128)S(1)}, f32[16,512,512]{1,2,0:T(8,128)}) fusion(pred[16,512]{1,0:T(8,128)(4,1)S(1)} %copy.43, bf16[16,512,128]{2,1,0:T(8,128)(2,1)S(1)} %bitcast.77, bf16[16,512,128]{2,1,0:T(8,128)(2,1)} %bitcast.78), kind=kOutput, calls=%fused_computation.59 | convolution fusion | flops 1090519552 | bytes 21012480 | tf_op jit(solution)/shard_map/sub | solution.py:27
  251.5 8.9 %convert_bitcast_fusion.1 = bf16[16,64,8,128]{3,2,1,0:T(8,128)(2,1)S(1)} fusion(bf16[16,512,128]{2,1,0:T(8,128)(2,1)} %bitcast.79, f32[16,512,512]{1,2,0:T(8,128)} %get-tuple-element.9, f32[16,512]{1,0:T(8,128)S(1)} %get-tuple-element.8), kind=kOutput, calls=%fused_computation.29 | convolution fusion | flops 1083179008 | bytes 21004288 | tf_op jit(solution)/shard_map/cqk,ckd->cqd/dot_general | solution.py:29
  260.4 3.8 copy.57
  264.1 5.2 %all-to-all-start.2 = ((bf16[16,64,8,128]{3,0,2,1:T(8,128)(2,1)}), bf16[16,64,8,128]{3,0,2,1:T(8,128)(2,1)S(1)}, u32[]{:S(2)}, u32[]{:S(2)}) async-start(bf16[16,64,8,128]{3,0,2,1:T(8,128)(2,1)} %copy.57), calls=%async_computation.2 | async-start | bytes 4194304 | tf_op jit(solution)/shard_map/all_to_all | solution.py:64
  269.3 0.0 reduce-scatter.2.cloned.1.call-start
  269.4 0.3 convert_convert_fusion
  269.7 1.6 copy.60
  271.3 0.7 fusion.11
  272.0 0.0 copy-start.4
  272.0 48.7 %all-to-all-done.2 = bf16[16,64,8,128]{3,0,2,1:T(8,128)(2,1)S(1)} async-done(((bf16[16,64,8,128]{3,0,2,1:T(8,128)(2,1)}), bf16[16,64,8,128]{3,0,2,1:T(8,128)(2,1)S(1)}, u32[]{:S(2)}, u32[]{:S(2)}) %all-to-all-start.2) | async-done | bytes 2097184 | tf_op jit(solution)/shard_map/all_to_all | solution.py:64
  320.7 1.4 copy.58
  322.1 0.0 copy-done.4
  322.1 2.6 fusion.23
  324.6 0.7 copy.62
  325.4 0.0 all-gather.2.cloned.1.call-done
  325.4 9.5 %convolution_convert_fusion = bf16[512,4096]{1,0:T(8,128)(2,1)} fusion(bf16[1024,4096]{0,1:T(8,128)(2,1)} %all-gather.2.cloned.1.call-done, bf16[64,8,8,128]{3,2,1,0:T(8,128)(2,1)S(1)} %bitcast.81), kind=kOutput, calls=%fused_computation.10 | convolution fusion | flops 4297064448 | bytes 13631488 | tf_op jit(solution)/shard_map/dot_general | solution.py:74
  334.9 0.0 reduce-scatter.2.cloned.1.call-update
  334.9 43.6 %reduce-scatter.2.cloned.1.call-done = bf16[512,1024]{1,0:T(8,128)(2,1)} async-done(((bf16[512,4096]{1,0:T(8,128)(2,1)}), bf16[512,1024]{1,0:T(8,128)(2,1)}) %reduce-scatter.2.cloned.1.call-update) | async-done | bytes 1048592 | tf_op jit(solution)/shard_map/reduce_scatter | solution.py:79
  (8 shorter events, 0.1 us)
Async XLA Ops:
  6.5 0.8 copy-start
  7.7 18.6 %copy-start.1 = (bf16[128,4096]{1,0:T(8,128)(2,1)S(1)}, bf16[128,4096]{1,0:T(8,128)(2,1)}, u32[]{:S(2)}) copy-start(bf16[128,4096]{1,0:T(8,128)(2,1)} %param.5) | copy-start | bytes 3145732
  10.6 35.4 %all-to-all-start = ((bf16[256,16,2]{1,2,0:T(2,128)(2,1)}), bf16[256,16,2]{1,2,0:T(2,128)(2,1)S(1)}, u32[]{:S(2)}, u32[]{:S(2)}) async-start(bf16[256,16,2]{1,2,0:T(2,128)(2,1)} %copy.42), calls=%async_computation | async-start | bytes 262144 | tf_op jit(solution)/shard_map/all_to_all | solution.py:59
  27.0 1.3 copy-start.2
  29.0 1.3 copy-start.3
  31.0 1.3 copy-start.5
  46.0 182.9 %all-to-all-start.1 = ((bf16[3,256,16,2,128]{4,2,3,0,1:T(8,128)(2,1)}), bf16[3,256,16,2,128]{4,2,3,0,1:T(8,128)(2,1)}, u32[]{:S(2)}, u32[]{:S(2)}) async-start(bf16[3,256,16,2,128]{4,2,3,0,1:T(8,128)(2,1)} %copy.52), calls=%async_computation.1 | async-start | bytes 12582912 | tf_op jit(solution)/shard_map/all_to_all | solution.py:58
  60.6 264.7 %all-gather.2.cloned.1.call-start = ((), (), s32[]{:S(2)}) async-start(), calls=%async_computation.4 | async-start | bytes 8519680 | tf_op jit(solution)/shard_map/all_gather | solution.py:76
  264.1 56.6 %all-to-all-start.2 = ((bf16[16,64,8,128]{3,0,2,1:T(8,128)(2,1)}), bf16[16,64,8,128]{3,0,2,1:T(8,128)(2,1)S(1)}, u32[]{:S(2)}, u32[]{:S(2)}) async-start(bf16[16,64,8,128]{3,0,2,1:T(8,128)(2,1)} %copy.57), calls=%async_computation.2 | async-start | bytes 4194304 | tf_op jit(solution)/shard_map/all_to_all | solution.py:64
  269.3 109.1 %reduce-scatter.2.cloned.1.call-start = ((), (), s32[]{:S(2)}) async-start(), calls=%async_computation.5 | async-start | bytes 5242880 | tf_op jit(solution)/shard_map/reduce_scatter | solution.py:79
  272.0 50.1 %copy-start.4 = (bf16[8,4,128,128]{3,2,0,1:T(8,128)(2,1)S(1)}, bf16[8,4,128,128]{3,2,0,1:T(8,128)(2,1)}, u32[]{:S(2)}) copy-start(bf16[8,4,128,128]{3,2,0,1:T(8,128)(2,1)} %copy.60) | copy-start | bytes 3145732
Sparse Core Ops, SparseCore 0:
  64.3 139.8 all-gather.1
  335.0 43.4 reduce-scatter.1

commit v2 on v1

--- a/solution.py
+++ b/solution.py
@@ -59,23 +59,36 @@
     valid = lax.all_to_all(markers, ("seq", "head"), split_axis=0, concat_axis=0, tiled=True)
     arrived = arrived.transpose(0, 2, 1, 3, 4).reshape(3, per_owner, n_src * slot_depth, HD)
     valid = valid.transpose(1, 0, 2).reshape(per_owner, n_src * slot_depth)
-    result_block = attend_blocks(arrived, valid)
-    result_block = result_block.reshape(per_owner, n_seq, n_head * slot_depth, HD)
-    returned = lax.all_to_all(result_block, "seq", split_axis=1, concat_axis=1, tiled=True)
-    returned = returned.reshape(group_heads, CLUSTERS, n_head, slot_depth, HD)
-
     group_ids = lax.dynamic_slice_in_dim(all_ids, head_group * group_heads, group_heads, 0)
     group_ids = group_ids.reshape(group_heads, n_head, sub_rows)
     home_table = slot_table(group_ids, slot_depth)
-    gathered = jnp.einsum(
-        "hltcr,hclrd->lthd", home_table, returned, preferred_element_type=jnp.float32
-    ).astype(jnp.bfloat16)
-    gathered = gathered.reshape(tok_dev, group_heads * HD)
-    partial_value = jnp.dot(
-        gathered,
-        lax.all_gather(out_weight, "seq", axis=1, tiled=True),
-        preferred_element_type=jnp.float32,
-    )
+    weight = lax.all_gather(out_weight, "seq", axis=1, tiled=True)
+
+    halves = 2
+    part_items = per_owner // halves
+    part_heads = group_heads // halves
+    projected = []
+    for half in range(halves):
+        items = slice(half * part_items, (half + 1) * part_items)
+        result_block = attend_blocks(arrived[:, items], valid[items])
+        result_block = result_block.reshape(part_items, n_seq, n_head * slot_depth, HD)
+        returned = lax.all_to_all(result_block, "seq", split_axis=1, concat_axis=1, tiled=True)
+        returned = returned.reshape(part_heads, CLUSTERS, n_head, slot_depth, HD)
+        gathered = jnp.einsum(
+            "hltcr,hclrd->lthd",
+            home_table[half * part_heads:(half + 1) * part_heads],
+            returned,
+            preferred_element_type=jnp.float32,
+        ).astype(jnp.bfloat16)
+        gathered = gathered.reshape(tok_dev, part_heads * HD)
+        projected.append(jnp.dot(
+            gathered,
+            weight[half * part_heads * HD:(half + 1) * part_heads * HD],
+            preferred_element_type=jnp.float32,
+        ))
+    partial_value = projected[0]
+    for part in projected[1:]:
+        partial_value = partial_value + part
     return lax.psum_scatter(
         partial_value.astype(jnp.bfloat16), "head", scatter_dimension=1, tiled=True
     )

time: 386 us -> 391 us (1.013)
  other arithmetic: 1.93 us -> 14.5 us
  waiting for transfers between devices: 260 us -> 250 us
  matrix products: 35.4 us -> 27.6 us
  starting transfers between devices: 35.8 us -> 42.3 us
    slice x4 -> x0, local copies, waits for them, and re-layouts: 12.6 us -> none  [the longest x2 7.36 us: attend_blocks(): packed[1]]
    sub x0 -> x2, other arithmetic: none -> 10.1 us  [attend_blocks(): raised = jnp.exp(scores - row_max)]
    all_to_all x1 -> x2, waiting for transfers between devices: 48.7 us -> 38.7 us  [body(): lax.all_to_all(result_block, 'seq', split_axis=1, concat_axis=1, tiled=True)]
    sub x1 -> x0, matrix products: 9.84 us -> none  [attend_blocks(): raised = jnp.exp(scores - row_max)]
    transpose x0 -> x1, local copies, waits for them, and re-layouts: none -> 9.57 us  [body(): arrived.transpose(0, 2, 1, 3, 4)]
    all_to_all x1 -> x2, starting transfers between devices: 5.2 us -> 11.5 us  [body(): lax.all_to_all(result_block, 'seq', split_axis=1, concat_axis=1, tiled=True)]
    dot_general x2 -> x6, matrix products: 12.1 us -> 15.3 us  [the longest x2 9.07 us: body(): jnp.dot(gathered, weight[half * part_heads * HD:(half + 1) * part_heads *...]
    dot_general x1 -> x2, matrix products: 8.9 us -> 7.62 us  [attend_blocks(): jnp.einsum('cqk,ckd->cqd', weights, packed[2], preferred_element_type=jnp...]
  transfers between devices with their start and end apart: 5 -> 6, of which waited for: 3 -> 4; matrix products, arithmetic and copies ran while one was open for 16% -> 17% of each run, Pallas kernels for 0% -> 0%
where the time goes in v2:
time: 391 us; the launch traced here: 387 us
  waiting for transfers between devices  250 us (64%)
  starting transfers between devices  42.3 us (11%)
  local copies, waits for them, and re-layouts  39 us (10%)
  matrix products  27.6 us (7%)
  other arithmetic  14.5 us (4%)
  between operations  14.2 us (4%)
    all_to_all x1, waiting for transfers between devices, body(): lax.all_to_all(packed, ('seq', 'head'), split_axis=1, concat_axis=1, tile...  167 us
    reduce_scatter x1, waiting for transfers between devices, body(): lax.psum_scatter(partial_value.astype(jnp.bfloat16), 'head', scatter_dime...  43.9 us
    all_to_all x2, waiting for transfers between devices, body(): lax.all_to_all(result_block, 'seq', split_axis=1, concat_axis=1, tiled=True)  38.7 us
    all_to_all x1, starting transfers between devices, body(): lax.all_to_all(markers, ('seq', 'head'), split_axis=0, concat_axis=0, til...  15.9 us
    all_to_all x1, starting transfers between devices, body(): lax.all_to_all(packed, ('seq', 'head'), split_axis=1, concat_axis=1, tile...  14.6 us
    all_to_all x2, starting transfers between devices, body(): lax.all_to_all(result_block, 'seq', split_axis=1, concat_axis=1, tiled=True)  11.5 us
    sub x2, other arithmetic, attend_blocks(): raised = jnp.exp(scores - row_max)  10.1 us
    transpose x1, local copies, waits for them, and re-layouts, body(): arrived.transpose(0, 2, 1, 3, 4)  9.57 us
  transfers between devices with their start and end apart: 6, of which 4 were waited for; matrix products, arithmetic and copies ran while one was open for 17% of the time, Pallas kernels for 0%

profile of v2, /device:TPU:1, one launch (start us, length us, event | category | flops | bytes accessed | tf_op | source)
XLA Modules:
  0.0 387.3 jit_solution(3742600096769343205)
XLA Ops:
  6.5 0.0 copy-start
  6.5 0.8 copy-done
  7.4 0.3 convert_convert_fusion.1
  7.7 0.7 fusion.19
  8.4 1.2 multiply_reduce_fusion
  9.6 0.1 reshape.123
  9.7 0.1 copy.78
  9.8 0.8 copy.79
  10.6 15.9 %all-to-all-start = ((bf16[256,16,2]{1,2,0:T(2,128)(2,1)}), bf16[256,16,2]{1,2,0:T(2,128)(2,1)S(1)}, u32[]{:S(2)}, u32[]{:S(2)}) async-start(bf16[256,16,2]{1,2,0:T(2,128)(2,1)} %copy.79), calls=%async_computation | async-start | bytes 262144 | tf_op jit(solution)/shard_map/all_to_all | solution.py:59
  26.6 1.6 copy.81
  28.2 1.3 copy.84
  29.5 0.0 copy-done.4
  29.5 0.7 copy.82
  30.2 0.0 copy-start.5
  30.2 1.3 copy.85
  31.5 1.6 copy.83
  33.1 1.3 copy.86
  34.5 0.0 copy-done.5
  34.5 3.3 convert_bitcast_fusion
  37.8 2.6 copy.87
  40.4 4.0 %copy.88 = bf16[3,64,4,16,2,128]{5,3,4,2,1,0:T(8,128)(2,1)S(1)} copy(bf16[3,64,4,16,2,128]{5,1,3,2,4,0:T(8,128)(2,1)S(1)} %bitcast.102) | data formatting | bytes 12582912 | tf_op jit(solution)/shard_map/transpose | solution.py:53
  44.5 3.8 copy.89
  48.3 0.0 all-to-all-done
  48.3 14.6 %all-to-all-start.1 = ((bf16[3,256,16,2,128]{4,2,3,0,1:T(8,128)(2,1)}), bf16[3,256,16,2,128]{4,2,3,0,1:T(8,128)(2,1)}, u32[]{:S(2)}, u32[]{:S(2)}) async-start(bf16[3,256,16,2,128]{4,2,3,0,1:T(8,128)(2,1)} %copy.89), calls=%async_computation.1 | async-start | bytes 12582912 | tf_op jit(solution)/shard_map/all_to_all | solution.py:58
  62.9 0.3 all-gather.2.cloned.1.call-start
  63.1 0.5 all-gather.2.cloned.1.call-update
  63.6 0.4 slice_compare_fusion
  64.0 0.2 gt.25
  64.2 0.1 copy.98
  64.3 0.2 gt.23
  64.5 0.1 copy.80
  64.6 166.6 %all-to-all-done.1 = bf16[3,256,16,2,128]{4,2,3,0,1:T(8,128)(2,1)} async-done(((bf16[3,256,16,2,128]{4,2,3,0,1:T(8,128)(2,1)}), bf16[3,256,16,2,128]{4,2,3,0,1:T(8,128)(2,1)}, u32[]{:S(2)}, u32[]{:S(2)}) %all-to-all-start.1) | async-done | bytes 6291488 | tf_op jit(solution)/shard_map/all_to_all | solution.py:58
  231.2 9.6 %copy.90 = bf16[3,16,256,2,128]{4,3,2,1,0:T(2,128)(2,1)S(1)} copy(bf16[3,16,256,2,128]{4,1,3,0,2:T(8,128)(2,1)} %bitcast.18) | data formatting | bytes 12582912 | tf_op jit(solution)/shard_map/transpose | solution.py:60
  240.8 0.0 copy-start.1
  240.8 1.3 fusion.32
  242.0 6.6 %fusion.56 = (f32[8,512]{1,0:T(8,128)S(1)}, f32[8,512,512]{1,2,0:T(8,128)}) fusion(f32[8,512,512]{1,2,0:T(8,128)S(1)} %fusion.32, pred[8,512]{1,0:T(8,128)(4,1)S(1)} %copy.98), kind=kOutput, calls=%fused_computation.90 | output fusion | flops 12583423 | bytes 16797696 | tf_op jit(solution)/shard_map/sub | solution.py:27
  248.6 0.0 copy-done.1
  248.6 4.8 %fusion.26 = bf16[8,64,8,128]{3,2,1,0:T(8,128)(2,1)S(1)} fusion(f32[8,512,512]{1,2,0:T(8,128)} %get-tuple-element.10, f32[8,512]{1,0:T(8,128)S(1)} %get-tuple-element.9, bf16[3,16,512,128]{3,2,1,0:T(8,128)(2,1)S(1)} %bitcast.105), kind=kOutput, calls=%fused_computation.44 | convolution fusion | flops 541589504 | bytes 10502144 | tf_op jit(solution)/shard_map/cqk,ckd->cqd/dot_general | solution.py:29
  253.4 2.2 copy.100
  255.6 5.2 %all-to-all-start.3 = ((bf16[8,64,8,128]{3,0,2,1:T(8,128)(2,1)}), bf16[8,64,8,128]{3,0,2,1:T(8,128)(2,1)S(1)}, u32[]{:S(2)}, u32[]{:S(2)}) async-start(bf16[8,64,8,128]{3,0,2,1:T(8,128)(2,1)} %copy.100), calls=%async_computation.3 | async-start | bytes 2097152 | tf_op jit(solution)/shard_map/all_to_all | solution.py:75
  260.8 2.8 fusion.34
  263.6 3.5 fusion.55
  267.1 2.8 fusion.25
  269.9 2.2 copy.92
  272.1 17.3 %all-to-all-done.3 = bf16[8,64,8,128]{3,0,2,1:T(8,128)(2,1)S(1)} async-done(((bf16[8,64,8,128]{3,0,2,1:T(8,128)(2,1)}), bf16[8,64,8,128]{3,0,2,1:T(8,128)(2,1)S(1)}, u32[]{:S(2)}, u32[]{:S(2)}) %all-to-all-start.3) | async-done | bytes 1048608 | tf_op jit(solution)/shard_map/all_to_all | solution.py:75
  289.4 6.3 %all-to-all-start.2 = ((bf16[8,64,8,128]{3,0,2,1:T(8,128)(2,1)}), bf16[8,64,8,128]{3,0,2,1:T(8,128)(2,1)S(1)}, u32[]{:S(2)}, u32[]{:S(2)}) async-start(bf16[8,64,8,128]{3,0,2,1:T(8,128)(2,1)} %copy.92), calls=%async_computation.2 | async-start | bytes 2097152 | tf_op jit(solution)/shard_map/all_to_all | solution.py:75
  295.7 0.0 reduce-scatter.2.cloned.1.call-start
  295.7 1.2 convert_convert_fusion
  297.0 1.6 copy.94
  298.6 0.7 fusion.20
  299.3 1.2 broadcast_multiply_fusion
  300.6 0.7 copy.101
  301.3 0.7 copy-done.3
  302.0 0.5 fusion.29
  302.4 0.3 copy.103
  302.8 21.5 %all-to-all-done.2 = bf16[8,64,8,128]{3,0,2,1:T(8,128)(2,1)S(1)} async-done(((bf16[8,64,8,128]{3,0,2,1:T(8,128)(2,1)}), bf16[8,64,8,128]{3,0,2,1:T(8,128)(2,1)S(1)}, u32[]{:S(2)}, u32[]{:S(2)}) %all-to-all-start.2) | async-done | bytes 1048608 | tf_op jit(solution)/shard_map/all_to_all | solution.py:75
  324.2 0.7 copy.93
  324.9 1.7 fusion.30
  326.6 0.3 copy.97
  326.9 0.0 all-gather.2.cloned.1.call-done
  327.0 4.7 %fusion.5 = f32[512,4096]{1,0:T(8,128)S(1)} fusion(bf16[1024,4096]{0,1:T(8,128)(2,1)} %all-gather.2.cloned.1.call-done, bf16[64,8,4,128]{3,2,1,0:T(4,128)(2,1)S(1)} %bitcast.112), kind=kOutput, calls=%fused_computation.13 | convolution fusion | flops 2147483648 | bytes 13107200 | tf_op jit(solution)/shard_map/dot_general | solution.py:84
  331.7 4.3 %add_convert_fusion = bf16[512,4096]{1,0:T(8,128)(2,1)} fusion(f32[512,4096]{1,0:T(8,128)S(1)} %fusion.5, bf16[1024,4096]{0,1:T(8,128)(2,1)S(1)} %copy-done.2, bf16[64,8,4,128]{3,2,1,0:T(4,128)(2,1)S(1)} %bitcast.111), kind=kOutput, calls=%fused_computation.2 | convolution fusion | flops 2151677952 | bytes 17301504 | tf_op jit(solution)/shard_map/dot_general | solution.py:84
  336.1 0.0 reduce-scatter.2.cloned.1.call-update
  336.1 43.9 %reduce-scatter.2.cloned.1.call-done = bf16[512,1024]{1,0:T(8,128)(2,1)} async-done(((bf16[512,4096]{1,0:T(8,128)(2,1)}), bf16[512,1024]{1,0:T(8,128)(2,1)}) %reduce-scatter.2.cloned.1.call-update) | async-done | bytes 1048592 | tf_op jit(solution)/shard_map/reduce_scatter | solution.py:92
  (11 shorter events, 0.1 us)
Async XLA Ops:
  6.5 0.8 copy-start
  6.5 23.0 %copy-start.4 = (bf16[128,4096]{1,0:T(8,128)(2,1)S(1)}, bf16[128,4096]{1,0:T(8,128)(2,1)}, u32[]{:S(2)}) copy-start(bf16[128,4096]{1,0:T(8,128)(2,1)} %param.6) | copy-start | bytes 3145732
  10.6 37.7 %all-to-all-start = ((bf16[256,16,2]{1,2,0:T(2,128)(2,1)}), bf16[256,16,2]{1,2,0:T(2,128)(2,1)S(1)}, u32[]{:S(2)}, u32[]{:S(2)}) async-start(bf16[256,16,2]{1,2,0:T(2,128)(2,1)} %copy.79), calls=%async_computation | async-start | bytes 262144 | tf_op jit(solution)/shard_map/all_to_all | solution.py:59
  30.2 4.3 %copy-start.5 = (bf16[1,128,32,128]{3,1,0,2:T(8,128)(2,1)S(1)}, bf16[1,128,32,128]{3,1,0,2:T(8,128)(2,1)}, u32[]{:S(2)}) copy-start(bf16[1,128,32,128]{3,1,0,2:T(8,128)(2,1)} %copy.84) | copy-start | bytes 3145732
  48.3 182.9 %all-to-all-start.1 = ((bf16[3,256,16,2,128]{4,2,3,0,1:T(8,128)(2,1)}), bf16[3,256,16,2,128]{4,2,3,0,1:T(8,128)(2,1)}, u32[]{:S(2)}, u32[]{:S(2)}) async-start(bf16[3,256,16,2,128]{4,2,3,0,1:T(8,128)(2,1)} %copy.89), calls=%async_computation.1 | async-start | bytes 12582912 | tf_op jit(solution)/shard_map/all_to_all | solution.py:58
  62.9 264.1 %all-gather.2.cloned.1.call-start = ((), (), s32[]{:S(2)}) async-start(), calls=%async_computation.5 | async-start | bytes 8519680 | tf_op jit(solution)/shard_map/all_gather | solution.py:65
  240.8 7.8 %copy-start.1 = (bf16[3,16,256,2,128]{4,3,2,1,0:T(2,128)(2,1)}, bf16[3,16,256,2,128]{4,3,2,1,0:T(2,128)(2,1)S(1)}, u32[]{:S(2)}) copy-start(bf16[3,16,256,2,128]{4,3,2,1,0:T(2,128)(2,1)S(1)} %copy.90) | copy-start | bytes 18874372
  255.6 33.7 %all-to-all-start.3 = ((bf16[8,64,8,128]{3,0,2,1:T(8,128)(2,1)}), bf16[8,64,8,128]{3,0,2,1:T(8,128)(2,1)S(1)}, u32[]{:S(2)}, u32[]{:S(2)}) async-start(bf16[8,64,8,128]{3,0,2,1:T(8,128)(2,1)} %copy.100), calls=%async_computation.3 | async-start | bytes 2097152 | tf_op jit(solution)/shard_map/all_to_all | solution.py:75
  289.4 34.8 %all-to-all-start.2 = ((bf16[8,64,8,128]{3,0,2,1:T(8,128)(2,1)}), bf16[8,64,8,128]{3,0,2,1:T(8,128)(2,1)S(1)}, u32[]{:S(2)}, u32[]{:S(2)}) async-start(bf16[8,64,8,128]{3,0,2,1:T(8,128)(2,1)} %copy.92), calls=%async_computation.2 | async-start | bytes 2097152 | tf_op jit(solution)/shard_map/all_to_all | solution.py:75
  295.7 84.4 %reduce-scatter.2.cloned.1.call-start = ((), (), s32[]{:S(2)}) async-start(), calls=%async_computation.6 | async-start | bytes 5242880 | tf_op jit(solution)/shard_map/reduce_scatter | solution.py:92
  300.6 1.4 copy-start.3
  327.0 4.7 %copy-start.2 = (bf16[1024,4096]{0,1:T(8,128)(2,1)S(1)}, bf16[1024,4096]{0,1:T(8,128)(2,1)}, u32[]{:S(2)}) copy-start(bf16[1024,4096]{0,1:T(8,128)(2,1)} %all-gather.2.cloned.1.call-done) | copy-start | bytes 25165828
Sparse Core Ops, SparseCore 0:
  66.5 139.8 all-gather.1
  336.2 43.7 reduce-scatter.1

commit v3 on v2

--- a/solution.py
+++ b/solution.py
@@ -18,16 +18,16 @@
     return onehot.astype(jnp.bfloat16)[..., :, None] * depth_hit[..., None, :]
 
 
-def attend_blocks(packed, validity):
+def attend_blocks(query, key, value, validity):
     scores = jnp.einsum(
-        "cqd,ckd->cqk", packed[0], packed[1], preferred_element_type=jnp.float32
+        "cqd,ckd->cqk", query, key, preferred_element_type=jnp.float32
     ) * HD ** (-0.5)
     scores = jnp.where(validity[:, None, :] > 0, scores, -1e30)
     row_max = jnp.max(scores, axis=-1, keepdims=True)
     raised = jnp.exp(scores - row_max)
     weights = (raised / jnp.sum(raised, axis=-1, keepdims=True)).astype(jnp.bfloat16)
     return jnp.einsum(
-        "cqk,ckd->cqd", weights, packed[2], preferred_element_type=jnp.float32
+        "cqk,ckd->cqd", weights, value, preferred_element_type=jnp.float32
     ).astype(jnp.bfloat16)
 
 
@@ -65,33 +65,25 @@
     weight = lax.all_gather(out_weight, "seq", axis=1, tiled=True)
 
     halves = 2
-    part_items = per_owner // halves
-    part_heads = group_heads // halves
-    projected = []
+    part_blocks = n_head // halves
+    by_block = arrived.reshape(3, per_owner, n_seq, n_head, slot_depth, HD)
+    outputs = []
     for half in range(halves):
-        items = slice(half * part_items, (half + 1) * part_items)
-        result_block = attend_blocks(arrived[:, items], valid[items])
-        result_block = result_block.reshape(part_items, n_seq, n_head * slot_depth, HD)
+        blocks = slice(half * part_blocks, (half + 1) * part_blocks)
+        query = by_block[0, :, :, blocks].reshape(per_owner, -1, HD)
+        result_block = attend_blocks(query, arrived[1], arrived[2], valid)
+        result_block = result_block.reshape(per_owner, n_seq, part_blocks * slot_depth, HD)
         returned = lax.all_to_all(result_block, "seq", split_axis=1, concat_axis=1, tiled=True)
-        returned = returned.reshape(part_heads, CLUSTERS, n_head, slot_depth, HD)
+        returned = returned.reshape(group_heads, CLUSTERS, part_blocks, slot_depth, HD)
         gathered = jnp.einsum(
-            "hltcr,hclrd->lthd",
-            home_table[half * part_heads:(half + 1) * part_heads],
-            returned,
-            preferred_element_type=jnp.float32,
+            "hltcr,hclrd->lthd", home_table[:, blocks], returned, preferred_element_type=jnp.float32
         ).astype(jnp.bfloat16)
-        gathered = gathered.reshape(tok_dev, part_heads * HD)
-        projected.append(jnp.dot(
-            gathered,
-            weight[half * part_heads * HD:(half + 1) * part_heads * HD],
-            preferred_element_type=jnp.float32,
+        gathered = gathered.reshape(part_blocks * sub_rows, group_heads * HD)
+        partial_value = jnp.dot(gathered, weight, preferred_element_type=jnp.float32)
+        outputs.append(lax.psum_scatter(
+            partial_value.astype(jnp.bfloat16), "head", scatter_dimension=1, tiled=True
         ))
-    partial_value = projected[0]
-    for part in projected[1:]:
-        partial_value = partial_value + part
-    return lax.psum_scatter(
-        partial_value.astype(jnp.bfloat16), "head", scatter_dimension=1, tiled=True
-    )
+    return jnp.concatenate(outputs, axis=0)
 
 
 def solution(mesh):

time: 391 us -> 391 us (level)
  waiting for transfers between devices: 250 us -> 210 us
  blocking collectives: 0 us -> 35.1 us
  matrix products: 27.6 us -> 45.1 us
  other arithmetic: 14.5 us -> 6.4 us
  starting transfers between devices: 42.3 us -> 36.4 us
    all_to_all x0 -> x1, blocking collectives: none -> 35.1 us  [body(): lax.all_to_all(result_block, 'seq', split_axis=1, concat_axis=1, tiled=True)]
    all_to_all x2 -> x1, waiting for transfers between devices: 38.7 us -> 15.3 us  [body(): lax.all_to_all(result_block, 'seq', split_axis=1, concat_axis=1, tiled=True)]
    reduce_scatter x1 -> x2, waiting for transfers between devices: 43.9 us -> 26.8 us  [body(): lax.psum_scatter(partial_value.astype(jnp.bfloat16), 'head', scatter_dime...]
    sub x0 -> x2, matrix products: none -> 15.9 us  [attend_blocks(): raised = jnp.exp(scores - row_max)]
    slice x0 -> x4, local copies, waits for them, and re-layouts: none -> 11.2 us  [the longest x3 8.21 us: body(): result_block = attend_blocks(query, arrived[1], arrived[2], valid)]
    sub x2 -> x0, other arithmetic: 10.1 us -> none  [attend_blocks(): raised = jnp.exp(scores - row_max)]
    transpose x1 -> x0, local copies, waits for them, and re-layouts: 9.57 us -> none  [body(): arrived.transpose(0, 2, 1, 3, 4)]
    all_to_all x2 -> x1, starting transfers between devices: 11.5 us -> 5.57 us  [body(): lax.all_to_all(result_block, 'seq', split_axis=1, concat_axis=1, tiled=True)]
  transfers between devices with their start and end apart: 6 -> 6, of which waited for: 4 -> 3; matrix products, arithmetic and copies ran while one was open for 17% -> 20% of each run, Pallas kernels for 0% -> 0%
where the time goes in v3:
time: 391 us; the launch traced here: 387 us
  waiting for transfers between devices  210 us (54%)
  matrix products  45.1 us (12%)
  local copies, waits for them, and re-layouts  41 us (10%)
  starting transfers between devices  36.4 us (9%)
  blocking collectives  35.1 us (9%)
  between operations  13.6 us (3%)
  other arithmetic  6.4 us (2%)
    all_to_all x1, waiting for transfers between devices, body(): lax.all_to_all(packed, ('seq', 'head'), split_axis=1, concat_axis=1, tile...  167 us
    all_to_all x1, blocking collectives, body(): lax.all_to_all(result_block, 'seq', split_axis=1, concat_axis=1, tiled=True)  35.1 us
    reduce_scatter x2, waiting for transfers between devices, body(): lax.psum_scatter(partial_value.astype(jnp.bfloat16), 'head', scatter_dime...  26.8 us
    all_to_all x1, starting transfers between devices, body(): lax.all_to_all(markers, ('seq', 'head'), split_axis=0, concat_axis=0, til...  15.9 us
    sub x2, matrix products, attend_blocks(): raised = jnp.exp(scores - row_max)  15.9 us
    all_to_all x1, waiting for transfers between devices, body(): lax.all_to_all(result_block, 'seq', split_axis=1, concat_axis=1, tiled=True)  15.3 us
    all_to_all x1, starting transfers between devices, body(): lax.all_to_all(packed, ('seq', 'head'), split_axis=1, concat_axis=1, tile...  14.6 us
    dot_general x2, matrix products, body(): jnp.dot(gathered, weight, preferred_element_type=jnp.float32)  14.2 us
  transfers between devices with their start and end apart: 6, of which 3 were waited for; matrix products, arithmetic and copies ran while one was open for 20% of the time, Pallas kernels for 0%

profile of v3, /device:TPU:1, one launch (start us, length us, event | category | flops | bytes accessed | tf_op | source)
XLA Modules:
  0.0 387.4 jit_solution(17168104822918545947)
XLA Ops:
  6.5 0.8 copy-done
  7.4 0.3 convert_convert_fusion.1
  7.7 0.0 copy-start.7
  7.7 0.7 fusion.16
  8.4 1.2 multiply_reduce_fusion
  9.6 0.1 reshape.111
  9.7 0.1 copy.72
  9.8 0.8 copy.73
  10.6 15.9 %all-to-all-start = ((bf16[256,16,2]{1,2,0:T(2,128)(2,1)}), bf16[256,16,2]{1,2,0:T(2,128)(2,1)S(1)}, u32[]{:S(2)}, u32[]{:S(2)}) async-start(bf16[256,16,2]{1,2,0:T(2,128)(2,1)} %copy.73), calls=%async_computation | async-start | bytes 262144 | tf_op jit(solution)/shard_map/all_to_all | solution.py:59
  26.6 0.7 copy.75
  27.3 1.3 copy.78
  28.6 0.7 copy.76
  29.2 1.3 copy.79
  30.6 0.7 copy.77
  31.2 1.3 copy.80
  32.5 3.3 convert_bitcast_fusion
  35.9 2.6 copy.81
  38.5 4.0 %copy.82 = bf16[3,64,4,16,2,128]{5,3,4,2,1,0:T(8,128)(2,1)S(1)} copy(bf16[3,64,4,16,2,128]{5,1,3,2,4,0:T(8,128)(2,1)S(1)} %bitcast.98) | data formatting | bytes 12582912 | tf_op jit(solution)/shard_map/transpose | solution.py:53
  42.6 3.7 copy.83
  46.2 14.6 %all-to-all-start.1 = ((bf16[3,256,16,2,128]{4,2,3,0,1:T(8,128)(2,1)}), bf16[3,256,16,2,128]{4,2,3,0,1:T(8,128)(2,1)}, u32[]{:S(2)}, u32[]{:S(2)}) async-start(bf16[3,256,16,2,128]{4,2,3,0,1:T(8,128)(2,1)} %copy.83), calls=%async_computation.1 | async-start | bytes 12582912 | tf_op jit(solution)/shard_map/all_to_all | solution.py:58
  60.8 0.3 all-gather.2.cloned.1.call-start
  61.1 0.5 all-gather.2.cloned.1.call-update
  61.6 0.2 compare_bitcast_fusion
  61.7 0.2 gt.17
  61.9 0.1 copy.74
  62.0 167.1 %all-to-all-done.1 = bf16[3,256,16,2,128]{4,2,3,0,1:T(8,128)(2,1)} async-done(((bf16[3,256,16,2,128]{4,2,3,0,1:T(8,128)(2,1)}), bf16[3,256,16,2,128]{4,2,3,0,1:T(8,128)(2,1)}, u32[]{:S(2)}, u32[]{:S(2)}) %all-to-all-start.1) | async-done | bytes 6291488 | tf_op jit(solution)/shard_map/all_to_all | solution.py:58
  229.1 3.0 fusion.53
  232.1 3.2 copy.85
  235.3 3.0 fusion.52
  238.3 1.0 copy.107
  239.3 2.0 copy.86
  241.3 8.5 %fusion.55 = (f32[16,256]{1,0:T(8,128)S(1)}, f32[16,256,512]{2,1,0:T(8,128)}) fusion(pred[16,512]{1,0:T(8,128)(4,1)S(1)} %copy.74, bf16[16,256,128]{2,1,0:T(8,128)(2,1)S(1)} %bitcast.107, bf16[16,512,128]{2,1,0:T(8,128)(2,1)} %bitcast.105), kind=kOutput, calls=%fused_computation.82 | convolution fusion | flops 545260032 | bytes 11558912 | tf_op jit(solution)/shard_map/sub | solution.py:27
  249.9 4.7 %fusion.21 = bf16[16,256,128]{2,1,0:T(8,128)(2,1)S(1)} fusion(bf16[16,512,128]{2,1,0:T(8,128)(2,1)S(1)} %bitcast.103, f32[16,256,512]{2,1,0:T(8,128)} %get-tuple-element.12, f32[16,256]{1,0:T(8,128)S(1)} %get-tuple-element.11), kind=kOutput, calls=%fused_computation.40 | convolution fusion | flops 541589504 | bytes 11550720 | tf_op jit(solution)/shard_map/cqk,ckd->cqd/dot_general | solution.py:29
  254.6 2.2 copy.87
  256.8 5.6 %all-to-all-start.2 = ((bf16[16,64,4,128]{3,0,2,1:T(8,128)(2,1)}), bf16[16,64,4,128]{3,0,2,1:T(8,128)(2,1)S(1)}, u32[]{:S(2)}, u32[]{:S(2)}) async-start(bf16[16,64,4,128]{3,0,2,1:T(8,128)(2,1)} %copy.87), calls=%async_computation.2 | async-start | bytes 2097152 | tf_op jit(solution)/shard_map/all_to_all | solution.py:76
  262.3 0.0 reduce-scatter.3.cloned.1.call-start
  262.4 0.3 convert_convert_fusion
  262.7 0.7 copy.89
  263.4 0.7 fusion.17
  264.0 0.0 copy-start.1
  264.1 2.2 broadcast_multiply_fusion
  266.3 1.9 copy.108
  268.2 7.4 %fusion.54 = (f32[16,256]{1,0:T(8,128)S(1)}, f32[16,256,512]{2,1,0:T(8,128)}) fusion(pred[16,512]{1,0:T(8,128)(4,1)S(1)} %copy.74, bf16[16,256,128]{2,1,0:T(8,128)(2,1)} %bitcast.108, bf16[16,512,128]{2,1,0:T(8,128)(2,1)S(1)} %bitcast.106), kind=kOutput, calls=%fused_computation.81 | convolution fusion | flops 545260032 | bytes 11558912 | tf_op jit(solution)/shard_map/sub | solution.py:27
  275.6 15.3 %all-to-all-done.2 = bf16[16,64,4,128]{3,0,2,1:T(8,128)(2,1)S(1)} async-done(((bf16[16,64,4,128]{3,0,2,1:T(8,128)(2,1)}), bf16[16,64,4,128]{3,0,2,1:T(8,128)(2,1)S(1)}, u32[]{:S(2)}, u32[]{:S(2)}) %all-to-all-start.2) | async-done | bytes 1048608 | tf_op jit(solution)/shard_map/all_to_all | solution.py:76
  290.9 0.7 copy.88
  291.6 0.9 copy-done.2
  292.5 0.5 fusion.25
  293.0 0.3 copy.92
  293.3 0.0 all-gather.2.cloned.1.call-done
  293.3 7.1 %convolution_convert_fusion.1 = bf16[256,4096]{1,0:T(8,128)(2,1)} fusion(bf16[1024,4096]{0,1:T(8,128)(2,1)} %all-gather.2.cloned.1.call-done, bf16[32,8,8,128]{3,2,1,0:T(8,128)(2,1)S(1)} %bitcast.114), kind=kOutput, calls=%fused_computation.12 | convolution fusion | flops 2148532224 | bytes 11010048 | tf_op jit(solution)/shard_map/dot_general | solution.py:82
  300.4 0.0 reduce-scatter.3.cloned.1.call-update
  300.4 0.0 reduce-scatter.5.cloned.1.call-start
  300.5 1.5 copy-done.5
  302.0 4.7 %fusion.20 = bf16[16,256,128]{2,1,0:T(8,128)(2,1)S(1)} fusion(bf16[16,512,128]{2,1,0:T(8,128)(2,1)S(1)} %bitcast.104, f32[16,256,512]{2,1,0:T(8,128)} %get-tuple-element.10, f32[16,256]{1,0:T(8,128)S(1)} %get-tuple-element.9), kind=kOutput, calls=%fused_computation.39 | convolution fusion | flops 541589504 | bytes 11550720 | tf_op jit(solution)/shard_map/cqk,ckd->cqd/dot_general | solution.py:29
  306.7 1.2 copy.94
  307.9 35.1 %all_to_all.20 = bf16[16,64,4,128]{3,0,2,1:T(8,128)(2,1)S(1)} all-to-all(bf16[16,64,4,128]{3,0,2,1:T(8,128)(2,1)S(1)} %copy.94), channel_id=1, replica_groups=mesh['seq'=64,'head'=4] {'seq'}, dimensions={1} | all-to-all | bytes 2097152 | tf_op jit(solution)/shard_map/all_to_all | solution.py:76
  343.0 0.7 copy.95
  343.7 0.5 fusion.24
  344.2 0.3 copy.97
  344.5 7.1 %convolution_convert_fusion = bf16[256,4096]{1,0:T(8,128)(2,1)} fusion(bf16[1024,4096]{0,1:T(8,128)(2,1)} %all-gather.2.cloned.1.call-done, bf16[32,8,8,128]{3,2,1,0:T(8,128)(2,1)S(1)} %bitcast.115), kind=kOutput, calls=%fused_computation.11 | convolution fusion | flops 2148532224 | bytes 11010048 | tf_op jit(solution)/shard_map/dot_general | solution.py:82
  351.6 0.0 reduce-scatter.5.cloned.1.call-update
  351.6 0.0 reduce-scatter.3.cloned.1.call-done
  351.7 26.8 %reduce-scatter.5.cloned.1.call-done = bf16[256,1024]{1,0:T(8,128)(2,1)} async-done(((bf16[256,4096]{1,0:T(8,128)(2,1)}), bf16[256,1024]{1,0:T(8,128)(2,1)}) %reduce-scatter.5.cloned.1.call-update) | async-done | bytes 524304 | tf_op jit(solution)/shard_map/reduce_scatter | solution.py:83
  378.4 2.2 pad_maximum_fusion
  (25 shorter events, 0.1 us)
Async XLA Ops:
  6.5 0.8 copy-start
  7.7 18.9 %copy-start.7 = (bf16[128,4096]{1,0:T(8,128)(2,1)S(1)}, bf16[128,4096]{1,0:T(8,128)(2,1)}, u32[]{:S(2)}) copy-start(bf16[128,4096]{1,0:T(8,128)(2,1)} %param.5) | copy-start | bytes 3145732
  10.6 35.6 %all-to-all-start = ((bf16[256,16,2]{1,2,0:T(2,128)(2,1)}), bf16[256,16,2]{1,2,0:T(2,128)(2,1)S(1)}, u32[]{:S(2)}, u32[]{:S(2)}) async-start(bf16[256,16,2]{1,2,0:T(2,128)(2,1)} %copy.73), calls=%async_computation | async-start | bytes 262144 | tf_op jit(solution)/shard_map/all_to_all | solution.py:59
  27.2 1.3 copy-start.8
  29.2 1.3 copy-start.9
  31.2 1.3 copy-start.10
  46.2 182.9 %all-to-all-start.1 = ((bf16[3,256,16,2,128]{4,2,3,0,1:T(8,128)(2,1)}), bf16[3,256,16,2,128]{4,2,3,0,1:T(8,128)(2,1)}, u32[]{:S(2)}, u32[]{:S(2)}) async-start(bf16[3,256,16,2,128]{4,2,3,0,1:T(8,128)(2,1)} %copy.83), calls=%async_computation.1 | async-start | bytes 12582912 | tf_op jit(solution)/shard_map/all_to_all | solution.py:58
  60.8 232.5 %all-gather.2.cloned.1.call-start = ((), (), s32[]{:S(2)}) async-start(), calls=%async_computation.6 | async-start | bytes 8519680 | tf_op jit(solution)/shard_map/all_gather | solution.py:65
  241.3 8.5 %copy-start.4 = (bf16[1,16,256,2,128]{4,3,2,1,0:T(2,128)(2,1)}, bf16[1,16,256,2,128]{4,3,2,1,0:T(2,128)(2,1)S(1)}, u32[]{:S(2)}) copy-start(bf16[1,16,256,2,128]{4,3,2,1,0:T(2,128)(2,1)S(1)} %copy.86) | copy-start | bytes 6291460
  256.8 34.2 %all-to-all-start.2 = ((bf16[16,64,4,128]{3,0,2,1:T(8,128)(2,1)}), bf16[16,64,4,128]{3,0,2,1:T(8,128)(2,1)S(1)}, u32[]{:S(2)}, u32[]{:S(2)}) async-start(bf16[16,64,4,128]{3,0,2,1:T(8,128)(2,1)} %copy.87), calls=%async_computation.2 | async-start | bytes 2097152 | tf_op jit(solution)/shard_map/all_to_all | solution.py:76
  262.3 89.3 %reduce-scatter.3.cloned.1.call-start = ((), (), s32[]{:S(2)}) async-start(), calls=%async_computation.7 | async-start | bytes 2621440 | tf_op jit(solution)/shard_map/reduce_scatter | solution.py:83
  264.0 2.3 copy-start.1
  266.3 1.9 copy-start.6
  290.9 1.6 copy-start.2
  300.4 1.6 copy-start.5
  300.4 78.0 %reduce-scatter.5.cloned.1.call-start = ((), (), s32[]{:S(2)}) async-start(), calls=%async_computation.8 | async-start | bytes 2621440 | tf_op jit(solution)/shard_map/reduce_scatter | solution.py:83
  307.9 35.8 %copy-start.3 = (bf16[8,4,128,128,2]{3,2,4,0,1:T(8,128)(2,1)S(1)}, bf16[8,4,128,128,2]{3,2,4,0,1:T(8,128)(2,1)}, u32[]{:S(2)}) copy-start(bf16[8,4,128,128,2]{3,2,4,0,1:T(8,128)(2,1)} %broadcast_multiply_fusion) | copy-start | bytes 6291460
Sparse Core Ops, SparseCore 0:
  64.4 139.8 all-gather.1
  300.6 26.7 reduce-scatter.2
  351.8 26.6 reduce-scatter.4

commit v4 on v1

--- a/solution.py
+++ b/solution.py
@@ -22,7 +22,7 @@
     scores = jnp.einsum(
         "cqd,ckd->cqk", packed[0], packed[1], preferred_element_type=jnp.float32
     ) * HD ** (-0.5)
-    scores = jnp.where(validity[:, None, :] > 0, scores, -1e30)
+    scores = jnp.where(validity[:, None, :], scores, -1e30)
     row_max = jnp.max(scores, axis=-1, keepdims=True)
     raised = jnp.exp(scores - row_max)
     weights = (raised / jnp.sum(raised, axis=-1, keepdims=True)).astype(jnp.bfloat16)
@@ -51,20 +51,25 @@
     ).astype(jnp.bfloat16)
     packed = packed.reshape(3, n_head, per_owner, n_seq, slot_depth, HD)
     packed = packed.transpose(0, 3, 1, 2, 4, 5).reshape(3, n_src, per_owner, slot_depth, HD)
-    markers = jnp.sum(own_table.astype(jnp.float32), axis=1).astype(jnp.bfloat16)
-    markers = markers.reshape(n_head, per_owner, n_seq, slot_depth)
-    markers = markers.transpose(2, 0, 1, 3).reshape(n_src, per_owner, slot_depth)
 
     arrived = lax.all_to_all(packed, ("seq", "head"), split_axis=1, concat_axis=1, tiled=True)
-    valid = lax.all_to_all(markers, ("seq", "head"), split_axis=0, concat_axis=0, tiled=True)
     arrived = arrived.transpose(0, 2, 1, 3, 4).reshape(3, per_owner, n_src * slot_depth, HD)
-    valid = valid.transpose(1, 0, 2).reshape(per_owner, n_src * slot_depth)
+
+    group_ids = lax.dynamic_slice_in_dim(all_ids, head_group * group_heads, group_heads, 0)
+    seen_ids = lax.all_gather(group_ids, "seq", axis=1, tiled=True)
+    seen_ids = seen_ids.reshape(group_heads, n_src, sub_rows)
+    owned = jnp.arange(CLUSTERS // n_seq, dtype=jnp.int32) * n_seq + lax.axis_index("seq")
+    counts = jnp.sum(
+        (seen_ids[:, None, :, :] == owned[None, :, None, None]).astype(jnp.int32), axis=-1
+    )
+    counts = counts.reshape(per_owner, n_src)
+    valid = counts[:, :, None] > jnp.arange(slot_depth, dtype=jnp.int32)
+    valid = valid.reshape(per_owner, n_src * slot_depth)
     result_block = attend_blocks(arrived, valid)
     result_block = result_block.reshape(per_owner, n_seq, n_head * slot_depth, HD)
     returned = lax.all_to_all(result_block, "seq", split_axis=1, concat_axis=1, tiled=True)
     returned = returned.reshape(group_heads, CLUSTERS, n_head, slot_depth, HD)
 
-    group_ids = lax.dynamic_slice_in_dim(all_ids, head_group * group_heads, group_heads, 0)
     group_ids = group_ids.reshape(group_heads, n_head, sub_rows)
     home_table = slot_table(group_ids, slot_depth)
     gathered = jnp.einsum(

time: 386 us -> 355 us (0.920)
  waiting for transfers between devices: 260 us -> 241 us
  starting transfers between devices: 35.8 us -> 22.1 us
    all_to_all x1, waiting for transfers between devices: 167 us -> 56.2 us  [body(): lax.all_to_all(packed, ('seq', 'head'), split_axis=1, concat_axis=1, tile...]
    all_gather x0 -> x1, waiting for transfers between devices: none -> 91.2 us  [body(): seen_ids = lax.all_gather(group_ids, 'seq', axis=1, tiled=True)]
    all_to_all x1 -> x0, starting transfers between devices: 15.7 us -> none  [body(): lax.all_to_all(markers, ('seq', 'head'), split_axis=0, concat_axis=0, til...]
  transfers between devices with their start and end apart: 5 -> 5, of which waited for: 3 -> 4; matrix products, arithmetic and copies ran while one was open for 16% -> 13% of each run, Pallas kernels for 0% -> 0%
where the time goes in v4:
time: 355 us; the launch traced here: 354 us
  waiting for transfers between devices  241 us (68%)
  local copies, waits for them, and re-layouts  40.2 us (11%)
  matrix products  35.8 us (10%)
  starting transfers between devices  22.1 us (6%)
  between operations  13.4 us (4%)
    all_gather x1, waiting for transfers between devices, body(): seen_ids = lax.all_gather(group_ids, 'seq', axis=1, tiled=True)  91.2 us
    all_to_all x1, waiting for transfers between devices, body(): lax.all_to_all(packed, ('seq', 'head'), split_axis=1, concat_axis=1, tile...  56.2 us
    all_to_all x1, waiting for transfers between devices, body(): lax.all_to_all(result_block, 'seq', split_axis=1, concat_axis=1, tiled=True)  48.7 us
    reduce_scatter x1, waiting for transfers between devices, body(): lax.psum_scatter(partial_value.astype(jnp.bfloat16), 'head', scatter_dime...  43.5 us
    all_to_all x1, starting transfers between devices, body(): lax.all_to_all(packed, ('seq', 'head'), split_axis=1, concat_axis=1, tile...  16.5 us
    sub x1, matrix products, attend_blocks(): raised = jnp.exp(scores - row_max)  9.82 us
    dot_general x1, matrix products, body(): jnp.dot(gathered, lax.all_gather(out_weight, 'seq', axis=1, tiled=True),...  9.5 us
    dot_general x1, matrix products, attend_blocks(): jnp.einsum('cqk,ckd->cqd', weights, packed[2], preferred_element_type=jnp...  9.25 us
  transfers between devices with their start and end apart: 5, of which 4 were waited for; matrix products, arithmetic and copies ran while one was open for 13% of the time, Pallas kernels for 0%

profile of v4, /device:TPU:1, one launch (start us, length us, event | category | flops | bytes accessed | tf_op | source)
XLA Modules:
  0.0 354.4 jit_solution(14528924154040969133)
XLA Ops:
  6.5 0.0 copy-start
  6.5 0.0 copy-start.2
  6.5 0.8 copy-done
  7.4 1.3 convert_convert_fusion.1
  8.7 0.7 fusion.11
  9.4 0.0 copy-done.2
  9.4 0.0 copy-start.3
  9.4 0.7 copy.67
  10.1 1.3 copy.70
  11.4 0.0 copy-done.3
  11.4 0.0 copy-start.4
  11.4 0.7 copy.68
  12.1 1.3 copy.71
  13.4 0.0 copy-done.4
  13.4 0.0 copy-start.5
  13.4 0.7 copy.69
  14.0 0.0 copy-start.7
  14.0 1.3 copy.72
  15.4 0.0 copy-done.5
  15.4 0.0 copy-done.7
  15.4 3.3 convert_bitcast_fusion
  18.7 2.6 copy.73
  21.3 4.0 %copy.74 = bf16[3,64,4,16,2,128]{5,3,4,2,1,0:T(8,128)(2,1)S(1)} copy(bf16[3,64,4,16,2,128]{5,1,3,2,4,0:T(8,128)(2,1)S(1)} %bitcast.66) | data formatting | bytes 12582912 | tf_op jit(solution)/shard_map/transpose | solution.py:53
  25.4 3.7 %copy.75 = bf16[3,256,16,2,128]{4,2,3,0,1:T(8,128)(2,1)} copy(bf16[3,256,16,2,128]{4,2,3,1,0:T(8,128)(2,1)S(1)} %bitcast.67) | data formatting | bytes 12582912 | tf_op jit(solution)/shard_map/reshape | solution.py:53
  29.1 16.5 %all-to-all-start = ((bf16[3,256,16,2,128]{4,2,3,0,1:T(8,128)(2,1)}), bf16[3,256,16,2,128]{4,2,3,0,1:T(8,128)(2,1)}, u32[]{:S(2)}, u32[]{:S(2)}) async-start(bf16[3,256,16,2,128]{4,2,3,0,1:T(8,128)(2,1)} %copy.75), calls=%async_computation | async-start | bytes 12582912 | tf_op jit(solution)/shard_map/all_to_all | solution.py:55
  45.6 0.0 all-gather.6.cloned.1.call-start
  45.7 0.6 copy.105
  46.3 0.1 all-gather.6.cloned.1.call-update
  46.4 0.0 all-gather.4.cloned.1.call-start
  46.4 0.7 all-gather.4.cloned.1.call-update
  47.2 0.1 gt.29
  47.3 91.2 %all-gather.6.cloned.1.call-done = s32[8,32768,1]{1,0,2:T(8,128)} async-done(((s32[8,512,1]{1,0,2:T(8,128)}), s32[8,32768,1]{1,0,2:T(8,128)}) %all-gather.6.cloned.1.call-update) | async-done | bytes 1048592 | tf_op jit(solution)/shard_map/all_gather | solution.py:59
  138.5 1.4 copy.64
  140.0 0.7 convert_reduce_fusion
  140.7 0.1 copy.65
  140.8 0.1 gt.26
  140.9 0.1 broadcast_compare_fusion
  141.0 0.1 copy.66
  141.2 56.2 %all-to-all-done = bf16[3,256,16,2,128]{4,2,3,0,1:T(8,128)(2,1)} async-done(((bf16[3,256,16,2,128]{4,2,3,0,1:T(8,128)(2,1)}), bf16[3,256,16,2,128]{4,2,3,0,1:T(8,128)(2,1)}, u32[]{:S(2)}, u32[]{:S(2)}) %all-to-all-start) | async-done | bytes 6291488 | tf_op jit(solution)/shard_map/all_to_all | solution.py:55
  197.4 4.5 %fusion.45 = (bf16[1,16,256,2,128]{4,1,3,0,2:T(8,128)(2,1)S(1)}, bf16[1,16,256,2,128]{4,1,3,0,2:T(8,128)(2,1)S(1)}, bf16[1,16,256,2,128]{4,1,3,0,2:T(8,128)(2,1)S(1)}) fusion(bf16[3,16,256,2,128]{4,1,3,0,2:T(8,128)(2,1)} %bitcast.17), kind=kLoop, calls=%fused_computation.60 | loop fusion | bytes 12582912 | tf_op jit(solution)/shard_map/slice | solution.py:23
  201.9 2.0 copy.76
  203.9 3.2 copy.77
  207.2 3.2 copy.78
  210.4 9.8 %fusion.46 = (f32[16,512]{1,0:T(8,128)S(1)}, f32[16,512,512]{1,2,0:T(8,128)}) fusion(pred[16,512]{1,0:T(8,128)(4,1)S(1)} %copy.66, bf16[16,512,128]{2,1,0:T(8,128)(2,1)S(1)} %bitcast.71, bf16[16,512,128]{2,1,0:T(8,128)(2,1)} %bitcast.72), kind=kOutput, calls=%fused_computation.61 | convolution fusion | flops 1090519552 | bytes 21012480 | tf_op jit(solution)/shard_map/sub | solution.py:27
  220.2 9.3 %convert_bitcast_fusion.1 = bf16[16,64,8,128]{3,2,1,0:T(8,128)(2,1)S(1)} fusion(bf16[16,512,128]{2,1,0:T(8,128)(2,1)} %bitcast.73, f32[16,512,512]{1,2,0:T(8,128)} %get-tuple-element.11, f32[16,512]{1,0:T(8,128)S(1)} %get-tuple-element.10), kind=kOutput, calls=%fused_computation.28 | convolution fusion | flops 1083179008 | bytes 21004288 | tf_op jit(solution)/shard_map/cqk,ckd->cqd/dot_general | solution.py:29
  229.5 3.8 %copy.80 = bf16[16,64,8,128]{3,0,2,1:T(8,128)(2,1)} copy(bf16[16,64,8,128]{3,2,1,0:T(8,128)(2,1)S(1)} %convert_bitcast_fusion.1) | data formatting | bytes 4194304 | tf_op jit(solution)/shard_map/reshape | solution.py:69
  233.3 0.0 copy-start.8
  233.3 5.4 %all-to-all-start.1 = ((bf16[16,64,8,128]{3,0,2,1:T(8,128)(2,1)}), bf16[16,64,8,128]{3,0,2,1:T(8,128)(2,1)S(1)}, u32[]{:S(2)}, u32[]{:S(2)}) async-start(bf16[16,64,8,128]{3,0,2,1:T(8,128)(2,1)} %copy.80), calls=%async_computation.1 | async-start | bytes 4194304 | tf_op jit(solution)/shard_map/all_to_all | solution.py:70
  238.7 0.0 reduce-scatter.2.cloned.1.call-start
  238.8 0.0 copy-done.8
  238.8 0.3 convert_convert_fusion
  239.0 1.6 copy.82
  240.6 0.7 fusion.12
  241.3 0.0 copy-start.6
  241.3 48.7 %all-to-all-done.1 = bf16[16,64,8,128]{3,0,2,1:T(8,128)(2,1)S(1)} async-done(((bf16[16,64,8,128]{3,0,2,1:T(8,128)(2,1)}), bf16[16,64,8,128]{3,0,2,1:T(8,128)(2,1)S(1)}, u32[]{:S(2)}, u32[]{:S(2)}) %all-to-all-start.1) | async-done | bytes 2097184 | tf_op jit(solution)/shard_map/all_to_all | solution.py:70
  290.1 1.4 copy.81
  291.4 0.0 copy-done.6
  291.4 2.6 fusion.25
  294.0 0.7 copy.84
  294.7 0.0 all-gather.4.cloned.1.call-done
  294.8 9.5 %convolution_convert_fusion = bf16[512,4096]{1,0:T(8,128)(2,1)} fusion(bf16[1024,4096]{0,1:T(8,128)(2,1)} %all-gather.4.cloned.1.call-done, bf16[64,8,8,128]{3,2,1,0:T(8,128)(2,1)S(1)} %bitcast.77), kind=kOutput, calls=%fused_computation.10 | convolution fusion | flops 4297064448 | bytes 13631488 | tf_op jit(solution)/shard_map/dot_general | solution.py:79
  304.3 0.0 reduce-scatter.2.cloned.1.call-update
  304.3 43.5 %reduce-scatter.2.cloned.1.call-done = bf16[512,1024]{1,0:T(8,128)(2,1)} async-done(((bf16[512,4096]{1,0:T(8,128)(2,1)}), bf16[512,1024]{1,0:T(8,128)(2,1)}) %reduce-scatter.2.cloned.1.call-update) | async-done | bytes 1048592 | tf_op jit(solution)/shard_map/reduce_scatter | solution.py:84
  347.8 0.0 copy-done.1
  (10 shorter events, 0.1 us)
Async XLA Ops:
  6.5 0.8 copy-start
  6.5 2.8 copy-start.2
  9.4 2.0 copy-start.3
  11.4 2.0 copy-start.4
  13.4 2.0 copy-start.5
  14.0 1.3 copy-start.7
  29.1 168.3 %all-to-all-start = ((bf16[3,256,16,2,128]{4,2,3,0,1:T(8,128)(2,1)}), bf16[3,256,16,2,128]{4,2,3,0,1:T(8,128)(2,1)}, u32[]{:S(2)}, u32[]{:S(2)}) async-start(bf16[3,256,16,2,128]{4,2,3,0,1:T(8,128)(2,1)} %copy.75), calls=%async_computation | async-start | bytes 12582912 | tf_op jit(solution)/shard_map/all_to_all | solution.py:55
  45.6 92.9 %all-gather.6.cloned.1.call-start = ((), (), s32[]{:S(2)}) async-start(), calls=%async_computation.5 | async-start | bytes 1064960 | tf_op jit(solution)/shard_map/all_gather | solution.py:59
  46.4 248.4 %all-gather.4.cloned.1.call-start = ((), (), s32[]{:S(2)}) async-start(), calls=%async_computation.3 | async-start | bytes 8519680 | tf_op jit(solution)/shard_map/all_gather | solution.py:81
  233.3 5.5 %copy-start.8 = (s32[8,512,1]{1,0,2:T(8,128)S(1)}, s32[8,512,1]{1,0,2:T(8,128)}, u32[]{:S(2)}) copy-start(s32[8,512,1]{1,0,2:T(8,128)} %copy.105) | copy-start | bytes 49156
  233.3 56.8 %all-to-all-start.1 = ((bf16[16,64,8,128]{3,0,2,1:T(8,128)(2,1)}), bf16[16,64,8,128]{3,0,2,1:T(8,128)(2,1)S(1)}, u32[]{:S(2)}, u32[]{:S(2)}) async-start(bf16[16,64,8,128]{3,0,2,1:T(8,128)(2,1)} %copy.80), calls=%async_computation.1 | async-start | bytes 4194304 | tf_op jit(solution)/shard_map/all_to_all | solution.py:70
  238.7 109.1 %reduce-scatter.2.cloned.1.call-start = ((), (), s32[]{:S(2)}) async-start(), calls=%async_computation.4 | async-start | bytes 5242880 | tf_op jit(solution)/shard_map/reduce_scatter | solution.py:84
  241.3 50.1 %copy-start.6 = (bf16[8,4,128,128]{3,2,0,1:T(8,128)(2,1)S(1)}, bf16[8,4,128,128]{3,2,0,1:T(8,128)(2,1)}, u32[]{:S(2)}) copy-start(bf16[8,4,128,128]{3,2,0,1:T(8,128)(2,1)} %copy.82) | copy-start | bytes 3145732
  304.3 43.6 %copy-start.1 = (s32[32,512,1]{1,2,0:T(1,128)S(1)}, s32[32,512,1]{1,2,0:T(1,128)}, u32[]{:S(2)}) copy-start(s32[32,512,1]{1,2,0:T(1,128)} %param.8) | copy-start | bytes 196612
Sparse Core Ops, SparseCore 0:
  49.3 89.2 all-gather.5
  141.3 91.9 all-gather.3
  304.4 43.3 reduce-scatter.1

commit v5 on v4

--- a/solution.py
+++ b/solution.py
@@ -45,15 +45,17 @@
 
     own_ids = lax.dynamic_slice_in_dim(all_ids, head_group * sub_rows, sub_rows, 1)
     own_table = slot_table(own_ids[:, None, :], slot_depth)[:, 0]
-    stacked = jnp.stack([t.reshape(sub_rows, HEADS, HD) for t in (queries, keys, values)])
+    stacked = jnp.stack([t.reshape(sub_rows, n_head, group_heads, HD) for t in (queries, keys, values)])
+    own_table = own_table.reshape(
+        n_head, group_heads, sub_rows, CLUSTERS // n_seq, n_seq, slot_depth
+    )
     packed = jnp.einsum(
-        "htcr,xthd->xhcrd", own_table, stacked, preferred_element_type=jnp.float32
+        "gjtacr,xtgjd->cgxjard", own_table, stacked, preferred_element_type=jnp.float32
     ).astype(jnp.bfloat16)
-    packed = packed.reshape(3, n_head, per_owner, n_seq, slot_depth, HD)
-    packed = packed.transpose(0, 3, 1, 2, 4, 5).reshape(3, n_src, per_owner, slot_depth, HD)
+    packed = packed.reshape(n_src, 3, per_owner, slot_depth, HD)
 
-    arrived = lax.all_to_all(packed, ("seq", "head"), split_axis=1, concat_axis=1, tiled=True)
-    arrived = arrived.transpose(0, 2, 1, 3, 4).reshape(3, per_owner, n_src * slot_depth, HD)
+    arrived = lax.all_to_all(packed, ("seq", "head"), split_axis=0, concat_axis=0, tiled=True)
+    arrived = arrived.transpose(1, 2, 0, 3, 4).reshape(3, per_owner, n_src * slot_depth, HD)
 
     group_ids = lax.dynamic_slice_in_dim(all_ids, head_group * group_heads, group_heads, 0)
     seen_ids = lax.all_gather(group_ids, "seq", axis=1, tiled=True)

time: 355 us -> 358 us (level)
  local copies, waits for them, and re-layouts: 40.2 us -> 44.6 us
    convert_element_type x1, local copies, waits for them, and re-layouts: 2.63 us -> 15.6 us  [body(): packed = jnp.einsum('gjtacr,xtgjd->cgxjard', own_table, stacked, preferre...]
    transpose x1 -> x0, local copies, waits for them, and re-layouts: 4.05 us -> none  [body(): packed.transpose(0, 3, 1, 2, 4, 5)]
    reshape x1 -> x0, local copies, waits for them, and re-layouts: 3.72 us -> none  [body(): packed.transpose(0, 3, 1, 2, 4, 5)]
where the time goes in v5:
time: 358 us
  waiting for transfers between devices  240 us (67%)
  local copies, waits for them, and re-layouts  44.6 us (12%)
  matrix products  35.4 us (10%)
  starting transfers between devices  22.2 us (6%)
  between operations  13.4 us (4%)
    all_gather x1, waiting for transfers between devices, body(): seen_ids = lax.all_gather(group_ids, 'seq', axis=1, tiled=True)  91.2 us
    all_to_all x1, waiting for transfers between devices, body(): lax.all_to_all(packed, ('seq', 'head'), split_axis=0, concat_axis=0, tile...  56.2 us
    all_to_all x1, waiting for transfers between devices, body(): lax.all_to_all(result_block, 'seq', split_axis=1, concat_axis=1, tiled=True)  48.7 us
    reduce_scatter x1, waiting for transfers between devices, body(): lax.psum_scatter(partial_value.astype(jnp.bfloat16), 'head', scatter_dime...  43.5 us
    all_to_all x1, starting transfers between devices, body(): lax.all_to_all(packed, ('seq', 'head'), split_axis=0, concat_axis=0, tile...  16.5 us
    convert_element_type x1, local copies, waits for them, and re-layouts, body(): packed = jnp.einsum('gjtacr,xtgjd->cgxjard', own_table, stacked, preferre...  15.6 us
    sub x1, matrix products, attend_blocks(): raised = jnp.exp(scores - row_max)  9.83 us
    dot_general x1, matrix products, body(): jnp.dot(gathered, lax.all_gather(out_weight, 'seq', axis=1, tiled=True),...  9.47 us
  transfers between devices with their start and end apart: 5, of which 4 were waited for; matrix products, arithmetic and copies ran while one was open for 13% of the time, Pallas kernels for 0%

profile of v5, /device:TPU:1, one launch (start us, length us, event | category | flops | bytes accessed | tf_op | source)
XLA Modules:
  0.0 357.6 jit_solution(1099226125662560766)
XLA Ops:
  6.5 0.0 copy-start
  6.5 0.0 copy-start.2
  6.5 0.8 copy-done
  7.4 0.7 fusion.11
  8.1 0.0 copy-done.2
  8.1 0.0 copy-start.3
  8.1 0.7 copy.67
  8.8 1.3 copy.70
  10.1 0.0 copy-done.3
  10.1 0.0 copy-start.4
  10.1 0.7 copy.68
  10.8 0.7 copy.71
  11.4 0.0 copy-done.4
  11.4 0.7 copy.69
  12.1 0.0 copy-start.6
  12.1 1.3 copy.72
  13.4 0.3 convert_convert_fusion.1
  13.8 0.0 copy-done.6
  13.8 3.0 convert_bitcast_fusion
  16.8 15.6 %copy.73 = bf16[64,4,3,8,2,2,128]{6,4,3,5,2,1,0:T(2,128)(2,1)} copy(bf16[64,4,3,8,2,2,128]{6,0,5,4,2,3,1:T(8,128)(2,1)S(1)} %convert_bitcast_fusion) | data formatting | bytes 12582912 | tf_op jit(solution)/shard_map/convert_element_type | solution.py:54
  32.4 16.5 %all-to-all-start = ((bf16[256,3,16,2,128]{4,2,3,1,0:T(8,128)(2,1)}), bf16[256,3,16,2,128]{4,2,3,1,0:T(8,128)(2,1)}, u32[]{:S(2)}, u32[]{:S(2)}) async-start(bf16[256,3,16,2,128]{4,2,3,1,0:T(8,128)(2,1)} %bitcast.66), calls=%async_computation | async-start | bytes 12582912 | tf_op jit(solution)/shard_map/all_to_all | solution.py:57
  48.9 0.0 all-gather.6.cloned.1.call-start
  49.0 0.6 copy.103
  49.6 0.1 all-gather.6.cloned.1.call-update
  49.6 0.2 all-gather.4.cloned.1.call-start
  49.9 0.5 all-gather.4.cloned.1.call-update
  50.4 0.1 gt.29
  50.6 91.2 %all-gather.6.cloned.1.call-done = s32[8,32768,1]{1,0,2:T(8,128)} async-done(((s32[8,512,1]{1,0,2:T(8,128)}), s32[8,32768,1]{1,0,2:T(8,128)}) %all-gather.6.cloned.1.call-update) | async-done | bytes 1048592 | tf_op jit(solution)/shard_map/all_gather | solution.py:61
  141.8 1.4 copy.64
  143.2 0.7 convert_reduce_fusion
  144.0 0.1 copy.65
  144.1 0.1 gt.26
  144.2 0.1 broadcast_compare_fusion
  144.3 0.1 copy.66
  144.4 56.2 %all-to-all-done = bf16[256,3,16,2,128]{4,2,3,1,0:T(8,128)(2,1)} async-done(((bf16[256,3,16,2,128]{4,2,3,1,0:T(8,128)(2,1)}), bf16[256,3,16,2,128]{4,2,3,1,0:T(8,128)(2,1)}, u32[]{:S(2)}, u32[]{:S(2)}) %all-to-all-start) | async-done | bytes 6291488 | tf_op jit(solution)/shard_map/all_to_all | solution.py:57
  200.6 4.5 %fusion.45 = (bf16[1,16,256,2,128]{4,1,3,0,2:T(8,128)(2,1)S(1)}, bf16[1,16,256,2,128]{4,1,3,0,2:T(8,128)(2,1)S(1)}, bf16[1,16,256,2,128]{4,1,3,0,2:T(8,128)(2,1)S(1)}) fusion(bf16[3,16,256,2,128]{4,1,3,0,2:T(8,128)(2,1)} %bitcast.17), kind=kLoop, calls=%fused_computation.61 | loop fusion | bytes 12582912 | tf_op jit(solution)/shard_map/slice | solution.py:23
  205.2 2.0 copy.74
  207.2 3.2 copy.75
  210.4 3.3 copy.76
  213.7 9.8 %fusion.46 = (f32[16,512]{1,0:T(8,128)S(1)}, f32[16,512,512]{1,2,0:T(8,128)}) fusion(pred[16,512]{1,0:T(8,128)(4,1)S(1)} %copy.66, bf16[16,512,128]{2,1,0:T(8,128)(2,1)S(1)} %bitcast.70, bf16[16,512,128]{2,1,0:T(8,128)(2,1)} %bitcast.71), kind=kOutput, calls=%fused_computation.62 | convolution fusion | flops 1090519552 | bytes 21012480 | tf_op jit(solution)/shard_map/sub | solution.py:27
  223.5 9.3 %convert_bitcast_fusion.1 = bf16[16,64,8,128]{3,2,1,0:T(8,128)(2,1)S(1)} fusion(bf16[16,512,128]{2,1,0:T(8,128)(2,1)} %bitcast.72, f32[16,512,512]{1,2,0:T(8,128)} %get-tuple-element.11, f32[16,512]{1,0:T(8,128)S(1)} %get-tuple-element.10), kind=kOutput, calls=%fused_computation.28 | convolution fusion | flops 1083179008 | bytes 21004288 | tf_op jit(solution)/shard_map/cqk,ckd->cqd/dot_general | solution.py:29
  232.8 3.8 %copy.78 = bf16[16,64,8,128]{3,0,2,1:T(8,128)(2,1)} copy(bf16[16,64,8,128]{3,2,1,0:T(8,128)(2,1)S(1)} %convert_bitcast_fusion.1) | data formatting | bytes 4194304 | tf_op jit(solution)/shard_map/reshape | solution.py:71
  236.5 0.0 copy-start.7
  236.5 5.4 %all-to-all-start.1 = ((bf16[16,64,8,128]{3,0,2,1:T(8,128)(2,1)}), bf16[16,64,8,128]{3,0,2,1:T(8,128)(2,1)S(1)}, u32[]{:S(2)}, u32[]{:S(2)}) async-start(bf16[16,64,8,128]{3,0,2,1:T(8,128)(2,1)} %copy.78), calls=%async_computation.1 | async-start | bytes 4194304 | tf_op jit(solution)/shard_map/all_to_all | solution.py:72
  241.9 0.0 reduce-scatter.2.cloned.1.call-start
  242.0 0.0 copy-done.7
  242.0 0.3 convert_convert_fusion
  242.3 1.6 copy.80
  243.8 0.7 fusion.12
  244.6 0.0 copy-start.5
  244.6 48.7 %all-to-all-done.1 = bf16[16,64,8,128]{3,0,2,1:T(8,128)(2,1)S(1)} async-done(((bf16[16,64,8,128]{3,0,2,1:T(8,128)(2,1)}), bf16[16,64,8,128]{3,0,2,1:T(8,128)(2,1)S(1)}, u32[]{:S(2)}, u32[]{:S(2)}) %all-to-all-start.1) | async-done | bytes 2097184 | tf_op jit(solution)/shard_map/all_to_all | solution.py:72
  293.3 1.4 copy.79
  294.7 0.0 copy-done.5
  294.7 2.6 fusion.25
  297.2 0.7 copy.82
  298.0 0.0 all-gather.4.cloned.1.call-done
  298.0 9.5 %convolution_convert_fusion = bf16[512,4096]{1,0:T(8,128)(2,1)} fusion(bf16[1024,4096]{0,1:T(8,128)(2,1)} %all-gather.4.cloned.1.call-done, bf16[64,8,8,128]{3,2,1,0:T(8,128)(2,1)S(1)} %bitcast.76), kind=kOutput, calls=%fused_computation.10 | convolution fusion | flops 4297064448 | bytes 13631488 | tf_op jit(solution)/shard_map/dot_general | solution.py:81
  307.5 0.0 copy-start.1
  307.5 0.0 reduce-scatter.2.cloned.1.call-update
  307.5 43.5 %reduce-scatter.2.cloned.1.call-done = bf16[512,1024]{1,0:T(8,128)(2,1)} async-done(((bf16[512,4096]{1,0:T(8,128)(2,1)}), bf16[512,1024]{1,0:T(8,128)(2,1)}) %reduce-scatter.2.cloned.1.call-update) | async-done | bytes 1048592 | tf_op jit(solution)/shard_map/reduce_scatter | solution.py:86
  351.1 0.0 copy-done.1
  (10 shorter events, 0.1 us)
Async XLA Ops:
  6.5 0.8 copy-start
  6.5 1.6 copy-start.2
  8.1 2.0 copy-start.3
  10.1 1.3 copy-start.4
  12.1 1.7 copy-start.6
  32.4 168.3 %all-to-all-start = ((bf16[256,3,16,2,128]{4,2,3,1,0:T(8,128)(2,1)}), bf16[256,3,16,2,128]{4,2,3,1,0:T(8,128)(2,1)}, u32[]{:S(2)}, u32[]{:S(2)}) async-start(bf16[256,3,16,2,128]{4,2,3,1,0:T(8,128)(2,1)} %bitcast.66), calls=%async_computation | async-start | bytes 12582912 | tf_op jit(solution)/shard_map/all_to_all | solution.py:57
  48.9 92.9 %all-gather.6.cloned.1.call-start = ((), (), s32[]{:S(2)}) async-start(), calls=%async_computation.5 | async-start | bytes 1064960 | tf_op jit(solution)/shard_map/all_gather | solution.py:61
  49.6 248.3 %all-gather.4.cloned.1.call-start = ((), (), s32[]{:S(2)}) async-start(), calls=%async_computation.3 | async-start | bytes 8519680 | tf_op jit(solution)/shard_map/all_gather | solution.py:83
  236.5 5.5 %copy-start.7 = (s32[8,512,1]{1,0,2:T(8,128)S(1)}, s32[8,512,1]{1,0,2:T(8,128)}, u32[]{:S(2)}) copy-start(s32[8,512,1]{1,0,2:T(8,128)} %copy.103) | copy-start | bytes 49156
  236.5 56.8 %all-to-all-start.1 = ((bf16[16,64,8,128]{3,0,2,1:T(8,128)(2,1)}), bf16[16,64,8,128]{3,0,2,1:T(8,128)(2,1)S(1)}, u32[]{:S(2)}, u32[]{:S(2)}) async-start(bf16[16,64,8,128]{3,0,2,1:T(8,128)(2,1)} %copy.78), calls=%async_computation.1 | async-start | bytes 4194304 | tf_op jit(solution)/shard_map/all_to_all | solution.py:72
  241.9 109.1 %reduce-scatter.2.cloned.1.call-start = ((), (), s32[]{:S(2)}) async-start(), calls=%async_computation.4 | async-start | bytes 5242880 | tf_op jit(solution)/shard_map/reduce_scatter | solution.py:86
  244.6 50.1 %copy-start.5 = (bf16[8,4,128,128]{3,2,0,1:T(8,128)(2,1)S(1)}, bf16[8,4,128,128]{3,2,0,1:T(8,128)(2,1)}, u32[]{:S(2)}) copy-start(bf16[8,4,128,128]{3,2,0,1:T(8,128)(2,1)} %copy.80) | copy-start | bytes 3145732
  307.5 43.6 %copy-start.1 = (s32[32,512,1]{1,2,0:T(1,128)S(1)}, s32[32,512,1]{1,2,0:T(1,128)}, u32[]{:S(2)}) copy-start(s32[32,512,1]{1,2,0:T(1,128)} %param.8) | copy-start | bytes 196612
Sparse Core Ops, SparseCore 0:
  52.5 89.2 all-gather.5
  144.6 91.9 all-gather.3
  307.6 43.3 reduce-scatter.1

commit v6 on v4

--- a/solution.py
+++ b/solution.py
@@ -1,6 +1,7 @@
 import jax
 import jax.numpy as jnp
 from jax import lax
+from jax.experimental import pallas as pl
 from jax.sharding import PartitionSpec as P
 
 HEADS = 32
@@ -18,17 +19,33 @@
     return onehot.astype(jnp.bfloat16)[..., :, None] * depth_hit[..., None, :]
 
 
-def attend_blocks(packed, validity):
-    scores = jnp.einsum(
-        "cqd,ckd->cqk", packed[0], packed[1], preferred_element_type=jnp.float32
+def attend_kernel(q_ref, k_ref, v_ref, mask_ref, out_ref):
+    scores = lax.dot_general(
+        q_ref[0], k_ref[0], (((1,), (1,)), ((), ())), preferred_element_type=jnp.float32
     ) * HD ** (-0.5)
-    scores = jnp.where(validity[:, None, :], scores, -1e30)
+    scores = jnp.where(mask_ref[0] > 0, scores, -1e30)
     row_max = jnp.max(scores, axis=-1, keepdims=True)
     raised = jnp.exp(scores - row_max)
     weights = (raised / jnp.sum(raised, axis=-1, keepdims=True)).astype(jnp.bfloat16)
-    return jnp.einsum(
-        "cqk,ckd->cqd", weights, packed[2], preferred_element_type=jnp.float32
-    ).astype(jnp.bfloat16)
+    out_ref[0] = jnp.dot(weights, v_ref[0], preferred_element_type=jnp.float32).astype(out_ref.dtype)
+
+
+def attend_blocks(packed, validity):
+    items, slots, _ = packed.shape[1:]
+    mask = validity.astype(jnp.float32).reshape(items, 1, slots)
+    row_spec = pl.BlockSpec((1, slots, HD), lambda i: (i, 0, 0))
+    return pl.pallas_call(
+        attend_kernel,
+        grid=(items,),
+        in_specs=[row_spec, row_spec, row_spec, pl.BlockSpec((1, 1, slots), lambda i: (i, 0, 0))],
+        out_specs=row_spec,
+        out_shape=jax.ShapeDtypeStruct((items, slots, HD), jnp.bfloat16),
+        cost_estimate=pl.CostEstimate(
+            flops=4 * items * slots * slots * HD,
+            transcendentals=items * slots * slots,
+            bytes_accessed=4 * items * slots * HD * 2,
+        ),
+    )(packed[0], packed[1], packed[2], mask)
 
 
 def body(queries, keys, values, cluster_ids, out_weight):

time: 355 us -> 363 us (1.023)
  matrix products: 35.8 us -> 16.4 us
  Pallas kernels: 0 us -> 18 us
  waiting for transfers between devices: 241 us -> 247 us
    all_to_all x1, waiting for transfers between devices: 56.2 us -> 96.4 us  [body(): lax.all_to_all(packed, ('seq', 'head'), split_axis=1, concat_axis=1, tile...]
    all_gather x1, waiting for transfers between devices: 91.2 us -> 57.9 us  [body(): seen_ids = lax.all_gather(group_ids, 'seq', axis=1, tiled=True)]
    pallas_call x0 -> x1, Pallas kernels: none -> 18 us  [attend_blocks(): pl.pallas_call(attend_kernel, grid=(items,), in_specs=[row_spec, row_spec...]
    sub x1 -> x0, matrix products: 9.82 us -> none  [attend_blocks(): raised = jnp.exp(scores - row_max)]
    dot_general x1 -> x0, matrix products: 9.25 us -> none  [attend_blocks(): jnp.einsum('cqk,ckd->cqd', weights, packed[2], preferred_element_type=jnp...]
    slice x2 -> x1, local copies, waits for them, and re-layouts: 7.75 us -> 3.22 us  [attend_blocks(): packed[1]]
    slice x1 -> x2, local copies, waits for them, and re-layouts: 3.25 us -> 7.44 us  [attend_blocks(): packed[2]]
  transfers between devices with their start and end apart: 5 -> 5, of which waited for: 4 -> 4; matrix products, arithmetic and copies ran while one was open for 13% -> 14% of each run, Pallas kernels for 0% -> 5%
where the time goes in v6:
time: 363 us; the launch traced here: 362 us
  waiting for transfers between devices  247 us (68%)
  local copies, waits for them, and re-layouts  41.6 us (11%)
  starting transfers between devices  23.6 us (7%)
  Pallas kernels  18 us (5%)
  matrix products  16.4 us (5%)
  between operations  13.4 us (4%)
    all_to_all x1, waiting for transfers between devices, body(): lax.all_to_all(packed, ('seq', 'head'), split_axis=1, concat_axis=1, tile...  96.4 us
    all_gather x1, waiting for transfers between devices, body(): seen_ids = lax.all_gather(group_ids, 'seq', axis=1, tiled=True)  57.9 us
    all_to_all x1, waiting for transfers between devices, body(): lax.all_to_all(result_block, 'seq', split_axis=1, concat_axis=1, tiled=True)  48.8 us
    reduce_scatter x1, waiting for transfers between devices, body(): lax.psum_scatter(partial_value.astype(jnp.bfloat16), 'head', scatter_dime...  43.7 us
    pallas_call x1, Pallas kernels, attend_blocks(): pl.pallas_call(attend_kernel, grid=(items,), in_specs=[row_spec, row_spec...  18 us
    all_to_all x1, starting transfers between devices, body(): lax.all_to_all(packed, ('seq', 'head'), split_axis=1, concat_axis=1, tile...  16.5 us
    dot_general x1, matrix products, body(): jnp.dot(gathered, lax.all_gather(out_weight, 'seq', axis=1, tiled=True),...  9.51 us
    slice x2, local copies, waits for them, and re-layouts, attend_blocks(): packed[2]  7.44 us
  transfers between devices with their start and end apart: 5, of which 4 were waited for; matrix products, arithmetic and copies ran while one was open for 14% of the time, Pallas kernels for 5%

profile of v6, /device:TPU:1, one launch (start us, length us, event | category | flops | bytes accessed | tf_op | source)
XLA Modules:
  0.0 362.3 jit_solution(141769643230938275)
XLA Ops:
  6.5 0.0 copy-start
  6.5 0.0 copy-start.2
  6.5 0.0 all-gather.6.cloned.1.call-start
  6.5 0.8 copy-done
  7.4 0.6 copy.121
  8.0 0.0 all-gather.6.cloned.1.call-update
  8.0 0.7 fusion.5
  8.7 0.0 copy-done.2
  8.7 0.0 copy-start.3
  8.7 0.7 copy.80
  9.4 1.3 copy.83
  10.7 0.0 copy-done.3
  10.7 0.0 copy-start.4
  10.7 0.7 copy.81
  11.4 0.7 copy.84
  12.0 0.0 copy-done.4
  12.1 0.7 copy.82
  12.7 0.0 copy-start.6
  12.7 1.3 copy.85
  14.1 0.3 convert_convert_fusion.1
  14.3 0.0 copy-done.6
  14.3 3.0 convert_bitcast_fusion
  17.4 2.6 copy.86
  20.0 4.0 %copy.87 = bf16[3,64,4,16,2,128]{5,3,4,2,1,0:T(8,128)(2,1)S(1)} copy(bf16[3,64,4,16,2,128]{5,1,3,2,4,0:T(8,128)(2,1)S(1)} %bitcast.60) | data formatting | bytes 12582912 | tf_op jit(solution)/shard_map/transpose | solution.py:70
  24.1 3.7 %copy.88 = bf16[3,256,16,2,128]{4,2,3,0,1:T(8,128)(2,1)} copy(bf16[3,256,16,2,128]{4,2,3,1,0:T(8,128)(2,1)S(1)} %bitcast.61) | data formatting | bytes 12582912 | tf_op jit(solution)/shard_map/reshape | solution.py:70
  27.7 16.5 %all-to-all-start = ((bf16[3,256,16,2,128]{4,2,3,0,1:T(8,128)(2,1)}), bf16[3,256,16,2,128]{4,2,3,0,1:T(8,128)(2,1)}, u32[]{:S(2)}, u32[]{:S(2)}) async-start(bf16[3,256,16,2,128]{4,2,3,0,1:T(8,128)(2,1)} %copy.88), calls=%async_computation | async-start | bytes 12582912 | tf_op jit(solution)/shard_map/all_to_all | solution.py:72
  44.2 0.2 all-gather.4.cloned.1.call-start
  44.5 0.5 all-gather.4.cloned.1.call-update
  45.0 0.1 gt.33
  45.2 57.9 %all-gather.6.cloned.1.call-done = s32[8,32768,1]{1,0,2:T(8,128)} async-done(((s32[8,512,1]{1,0,2:T(8,128)}), s32[8,32768,1]{1,0,2:T(8,128)}) %all-gather.6.cloned.1.call-update) | async-done | bytes 1048592 | tf_op jit(solution)/shard_map/all_gather | solution.py:76
  103.1 1.4 copy.93
  104.5 0.7 convert_reduce_fusion
  105.2 0.1 copy.94
  105.3 0.1 gt.30
  105.4 0.1 copy.95
  105.5 0.7 compare_convert_fusion.mask_ref
  106.2 96.4 %all-to-all-done = bf16[3,256,16,2,128]{4,2,3,0,1:T(8,128)(2,1)} async-done(((bf16[3,256,16,2,128]{4,2,3,0,1:T(8,128)(2,1)}), bf16[3,256,16,2,128]{4,2,3,0,1:T(8,128)(2,1)}, u32[]{:S(2)}, u32[]{:S(2)}) %all-to-all-start) | async-done | bytes 6291488 | tf_op jit(solution)/shard_map/all_to_all | solution.py:72
  202.6 4.2 %fusion.35 = (bf16[1,16,256,2,128]{4,1,3,0,2:T(8,128)(2,1)S(1)}, bf16[1,16,256,2,128]{4,1,3,0,2:T(8,128)(2,1)S(1)}, bf16[1,16,256,2,128]{4,1,3,0,2:T(8,128)(2,1)S(1)}) fusion(bf16[3,16,256,2,128]{4,1,3,0,2:T(8,128)(2,1)} %bitcast.15), kind=kLoop, calls=%fused_computation.47 | loop fusion | bytes 12582912 | tf_op jit(solution)/shard_map/slice | solution.py:48
  206.8 3.2 copy.89
  210.0 3.2 copy.90
  213.3 3.2 copy.91
  216.4 18.0 %shard_map.55 = bf16[16,512,128]{2,1,0:T(8,128)(2,1)} custom-call(bf16[16,512,128]{2,1,0:T(8,128)(2,1)} %bitcast.62, bf16[16,512,128]{2,1,0:T(8,128)(2,1)} %bitcast.63, bf16[16,512,128]{2,1,0:T(8,128)(2,1)} %bitcast.64, f32[16,1,512]{2,1,0:T(1,128)} %compare_convert_fusion.mask_ref), custom_call_target="tpu_custom_call" | custom-call | flops 2147483648 | bytes 8388608 | tf_op jit(solution)/shard_map/pallas_call | solution.py:37
  234.5 5.4 %copy.97 = bf16[16,64,8,128]{3,0,2,1:T(8,128)(2,1)} copy(bf16[16,64,8,128]{3,2,1,0:T(8,128)(2,1)} %bitcast.65) | data formatting | bytes 4194304 | tf_op jit(solution)/shard_map/reshape | solution.py:86
  239.8 0.0 copy-start.7
  239.8 6.6 %all-to-all-start.1 = ((bf16[16,64,8,128]{3,0,2,1:T(8,128)(2,1)}), bf16[16,64,8,128]{3,0,2,1:T(8,128)(2,1)S(1)}, u32[]{:S(2)}, u32[]{:S(2)}) async-start(bf16[16,64,8,128]{3,0,2,1:T(8,128)(2,1)} %copy.97), calls=%async_computation.1 | async-start | bytes 4194304 | tf_op jit(solution)/shard_map/all_to_all | solution.py:87
  246.4 0.3 reduce-scatter.2.cloned.1.call-start
  246.7 0.0 copy-done.7
  246.7 0.3 convert_convert_fusion
  247.0 1.3 copy.99
  248.3 0.7 fusion.6
  249.0 0.0 copy-start.5
  249.0 48.8 %all-to-all-done.1 = bf16[16,64,8,128]{3,0,2,1:T(8,128)(2,1)S(1)} async-done(((bf16[16,64,8,128]{3,0,2,1:T(8,128)(2,1)}), bf16[16,64,8,128]{3,0,2,1:T(8,128)(2,1)S(1)}, u32[]{:S(2)}, u32[]{:S(2)}) %all-to-all-start.1) | async-done | bytes 2097184 | tf_op jit(solution)/shard_map/all_to_all | solution.py:87
  297.8 1.4 copy.98
  299.2 0.0 copy-done.5
  299.2 2.6 fusion.17
  301.7 0.7 copy.101
  302.5 0.0 all-gather.4.cloned.1.call-done
  302.5 9.5 %convolution_convert_fusion = bf16[512,4096]{1,0:T(8,128)(2,1)} fusion(bf16[1024,4096]{0,1:T(8,128)(2,1)} %all-gather.4.cloned.1.call-done, bf16[64,8,8,128]{3,2,1,0:T(8,128)(2,1)S(1)} %bitcast.72), kind=kOutput, calls=%fused_computation.1 | convolution fusion | flops 4297064448 | bytes 13631488 | tf_op jit(solution)/shard_map/dot_general | solution.py:96
  312.0 0.0 copy-start.1
  312.0 0.0 reduce-scatter.2.cloned.1.call-update
  312.0 43.7 %reduce-scatter.2.cloned.1.call-done = bf16[512,1024]{1,0:T(8,128)(2,1)} async-done(((bf16[512,4096]{1,0:T(8,128)(2,1)}), bf16[512,1024]{1,0:T(8,128)(2,1)}) %reduce-scatter.2.cloned.1.call-update) | async-done | bytes 1048592 | tf_op jit(solution)/shard_map/reduce_scatter | solution.py:101
  355.7 0.0 copy-done.1
  (9 shorter events, 0.1 us)
Async XLA Ops:
  6.5 0.8 copy-start
  6.5 2.2 copy-start.2
  6.5 96.5 %all-gather.6.cloned.1.call-start = ((), (), s32[]{:S(2)}) async-start(), calls=%async_computation.5 | async-start | bytes 1064960 | tf_op jit(solution)/shard_map/all_gather | solution.py:76
  8.7 2.0 copy-start.3
  10.7 1.3 copy-start.4
  12.7 1.6 copy-start.6
  27.7 174.8 %all-to-all-start = ((bf16[3,256,16,2,128]{4,2,3,0,1:T(8,128)(2,1)}), bf16[3,256,16,2,128]{4,2,3,0,1:T(8,128)(2,1)}, u32[]{:S(2)}, u32[]{:S(2)}) async-start(bf16[3,256,16,2,128]{4,2,3,0,1:T(8,128)(2,1)} %copy.88), calls=%async_computation | async-start | bytes 12582912 | tf_op jit(solution)/shard_map/all_to_all | solution.py:72
  44.2 258.2 %all-gather.4.cloned.1.call-start = ((), (), s32[]{:S(2)}) async-start(), calls=%async_computation.3 | async-start | bytes 8519680 | tf_op jit(solution)/shard_map/all_gather | solution.py:98
  239.8 6.9 %copy-start.7 = (s32[8,512,1]{1,0,2:T(8,128)S(1)}, s32[8,512,1]{1,0,2:T(8,128)}, u32[]{:S(2)}) copy-start(s32[8,512,1]{1,0,2:T(8,128)} %copy.121) | copy-start | bytes 49156
  239.8 58.0 %all-to-all-start.1 = ((bf16[16,64,8,128]{3,0,2,1:T(8,128)(2,1)}), bf16[16,64,8,128]{3,0,2,1:T(8,128)(2,1)S(1)}, u32[]{:S(2)}, u32[]{:S(2)}) async-start(bf16[16,64,8,128]{3,0,2,1:T(8,128)(2,1)} %copy.97), calls=%async_computation.1 | async-start | bytes 4194304 | tf_op jit(solution)/shard_map/all_to_all | solution.py:87
  246.4 109.3 %reduce-scatter.2.cloned.1.call-start = ((), (), s32[]{:S(2)}) async-start(), calls=%async_computation.4 | async-start | bytes 5242880 | tf_op jit(solution)/shard_map/reduce_scatter | solution.py:101
  249.0 50.2 %copy-start.5 = (bf16[8,4,128,128]{3,2,0,1:T(8,128)(2,1)S(1)}, bf16[8,4,128,128]{3,2,0,1:T(8,128)(2,1)}, u32[]{:S(2)}) copy-start(bf16[8,4,128,128]{3,2,0,1:T(8,128)(2,1)} %copy.99) | copy-start | bytes 3145732
  312.0 43.7 %copy-start.1 = (s32[32,512,1]{1,2,0:T(1,128)S(1)}, s32[32,512,1]{1,2,0:T(1,128)}, u32[]{:S(2)}) copy-start(s32[32,512,1]{1,2,0:T(1,128)} %param.8) | copy-start | bytes 196612
Sparse Core Ops, SparseCore 0:
  10.1 92.8 all-gather.5
  105.9 108.4 all-gather.3
  312.2 43.5 reduce-scatter.1

commit v7 on v6

--- a/solution.py
+++ b/solution.py
@@ -27,19 +27,21 @@
     row_max = jnp.max(scores, axis=-1, keepdims=True)
     raised = jnp.exp(scores - row_max)
     weights = (raised / jnp.sum(raised, axis=-1, keepdims=True)).astype(jnp.bfloat16)
-    out_ref[0] = jnp.dot(weights, v_ref[0], preferred_element_type=jnp.float32).astype(out_ref.dtype)
+    result = jnp.dot(weights, v_ref[0], preferred_element_type=jnp.float32)
+    out_ref[:, 0] = result.reshape(out_ref.shape[0], out_ref.shape[2], HD).astype(out_ref.dtype)
 
 
-def attend_blocks(packed, validity):
+def attend_blocks(packed, validity, n_dest):
     items, slots, _ = packed.shape[1:]
+    lanes = slots // n_dest
     mask = validity.astype(jnp.float32).reshape(items, 1, slots)
     row_spec = pl.BlockSpec((1, slots, HD), lambda i: (i, 0, 0))
     return pl.pallas_call(
         attend_kernel,
         grid=(items,),
         in_specs=[row_spec, row_spec, row_spec, pl.BlockSpec((1, 1, slots), lambda i: (i, 0, 0))],
-        out_specs=row_spec,
-        out_shape=jax.ShapeDtypeStruct((items, slots, HD), jnp.bfloat16),
+        out_specs=pl.BlockSpec((n_dest, 1, lanes, HD), lambda i: (0, i, 0, 0)),
+        out_shape=jax.ShapeDtypeStruct((n_dest, items, lanes, HD), jnp.bfloat16),
         cost_estimate=pl.CostEstimate(
             flops=4 * items * slots * slots * HD,
             transcendentals=items * slots * slots,
@@ -69,12 +71,14 @@
     packed = packed.reshape(3, n_head, per_owner, n_seq, slot_depth, HD)
     packed = packed.transpose(0, 3, 1, 2, 4, 5).reshape(3, n_src, per_owner, slot_depth, HD)
 
+    group_ids = lax.dynamic_slice_in_dim(cluster_ids, head_group * group_heads, group_heads, 0)
+    group_ids, packed = lax.optimization_barrier((group_ids, packed))
     arrived = lax.all_to_all(packed, ("seq", "head"), split_axis=1, concat_axis=1, tiled=True)
     arrived = arrived.transpose(0, 2, 1, 3, 4).reshape(3, per_owner, n_src * slot_depth, HD)
 
-    group_ids = lax.dynamic_slice_in_dim(all_ids, head_group * group_heads, group_heads, 0)
     seen_ids = lax.all_gather(group_ids, "seq", axis=1, tiled=True)
     seen_ids = seen_ids.reshape(group_heads, n_src, sub_rows)
+    group_ids = group_ids[:, :, 0]
     owned = jnp.arange(CLUSTERS // n_seq, dtype=jnp.int32) * n_seq + lax.axis_index("seq")
     counts = jnp.sum(
         (seen_ids[:, None, :, :] == owned[None, :, None, None]).astype(jnp.int32), axis=-1
@@ -82,10 +86,9 @@
     counts = counts.reshape(per_owner, n_src)
     valid = counts[:, :, None] > jnp.arange(slot_depth, dtype=jnp.int32)
     valid = valid.reshape(per_owner, n_src * slot_depth)
-    result_block = attend_blocks(arrived, valid)
-    result_block = result_block.reshape(per_owner, n_seq, n_head * slot_depth, HD)
-    returned = lax.all_to_all(result_block, "seq", split_axis=1, concat_axis=1, tiled=True)
-    returned = returned.reshape(group_heads, CLUSTERS, n_head, slot_depth, HD)
+    result_block = attend_blocks(arrived, valid, n_seq)
+    returned = lax.all_to_all(result_block, "seq", split_axis=0, concat_axis=0, tiled=True)
+    returned = returned.transpose(1, 0, 2, 3).reshape(group_heads, CLUSTERS, n_head, slot_depth, HD)
 
     group_ids = group_ids.reshape(group_heads, n_head, sub_rows)
     home_table = slot_table(group_ids, slot_depth)

time: 363 us -> 362 us (level)
    all_to_all x1, waiting for transfers between devices: 96.4 us -> 80.9 us  [body(): lax.all_to_all(packed, ('seq', 'head'), split_axis=1, concat_axis=1, tile...]
    all_gather x1, waiting for transfers between devices: 57.9 us -> 69 us  [body(): seen_ids = lax.all_gather(group_ids, 'seq', axis=1, tiled=True)]
    reshape x2 -> x0, local copies, waits for them, and re-layouts: 9.01 us -> none  [the longest x1 5.36 us: body(): result_block.reshape(per_owner, n_seq, n_head * slot_depth, HD)]
    optimization_barrier x0 -> x1, local copies, waits for them, and re-layouts: none -> 6.55 us  [body(): group_ids, packed = lax.optimization_barrier((group_ids, packed))]
  transfers between devices with their start and end apart: 5 -> 5, of which waited for: 4 -> 4; matrix products, arithmetic and copies ran while one was open for 14% -> 8% of each run, Pallas kernels for 5% -> 5%
where the time goes in v7:
time: 362 us; the launch traced here: 361 us
  waiting for transfers between devices  244 us (67%)
  local copies, waits for them, and re-layouts  41.2 us (11%)
  starting transfers between devices  23.2 us (6%)
  Pallas kernels  18 us (5%)
  matrix products  16.7 us (5%)
  between operations  13.4 us (4%)
  other arithmetic  4.12 us (1%)
    all_to_all x1, waiting for transfers between devices, body(): lax.all_to_all(packed, ('seq', 'head'), split_axis=1, concat_axis=1, tile...  80.9 us
    all_gather x1, waiting for transfers between devices, body(): seen_ids = lax.all_gather(group_ids, 'seq', axis=1, tiled=True)  69 us
    all_to_all x1, waiting for transfers between devices, body(): lax.all_to_all(result_block, 'seq', split_axis=0, concat_axis=0, tiled=True)  48.8 us
    reduce_scatter x1, waiting for transfers between devices, body(): lax.psum_scatter(partial_value.astype(jnp.bfloat16), 'head', scatter_dime...  44.6 us
    pallas_call x1, Pallas kernels, attend_blocks(): pl.pallas_call(attend_kernel, grid=(items,), in_specs=[row_spec, row_spec...  18 us
    all_to_all x1, starting transfers between devices, body(): lax.all_to_all(packed, ('seq', 'head'), split_axis=1, concat_axis=1, tile...  16.5 us
    dot_general x1, matrix products, body(): jnp.dot(gathered, lax.all_gather(out_weight, 'seq', axis=1, tiled=True),...  9.51 us
    slice x2, local copies, waits for them, and re-layouts, attend_blocks(): packed[2]  7.67 us
  transfers between devices with their start and end apart: 5, of which 4 were waited for; matrix products, arithmetic and copies ran while one was open for 8% of the time, Pallas kernels for 5%

profile of v7, /device:TPU:1, one launch (start us, length us, event | category | flops | bytes accessed | tf_op | source)
XLA Modules:
  0.0 360.6 jit_solution(10946349265261514023)
XLA Ops:
  6.5 0.0 copy-start
  6.5 0.0 copy-start.2
  6.5 0.0 all-gather.3.cloned.1.call-start
  6.5 0.8 copy-done
  7.4 1.2 convert_convert_fusion.1
  8.6 0.7 fusion.5
  9.3 0.0 copy-done.2
  9.4 0.0 copy-start.3
  9.4 0.7 copy.75
  10.0 1.3 copy.78
  11.4 0.0 copy-done.3
  11.4 0.0 copy-start.4
  11.4 0.7 copy.76
  12.0 1.3 copy.79
  13.3 0.0 copy-done.4
  13.3 0.0 copy-start.5
  13.3 0.7 copy.77
  14.0 0.0 copy-start.7
  14.0 1.3 copy.80
  15.3 0.0 copy-done.5
  15.3 0.0 copy-done.7
  15.3 3.3 convert_bitcast_fusion
  18.6 2.6 copy.81
  21.3 6.7 %copy.82 = bf16[3,64,4,16,2,128]{5,3,4,2,1,0:T(8,128)(2,1)} copy(bf16[3,64,4,16,2,128]{5,1,3,2,4,0:T(8,128)(2,1)S(1)} %bitcast.59) | data formatting | bytes 12582912 | tf_op jit(solution)/shard_map/transpose | solution.py:72
  28.0 0.6 constant_dynamic-slice_fusion.1
  28.6 0.0 all-gather.3.cloned.1.call-update
  28.6 6.6 %copy.83 = bf16[3,256,16,2,128]{4,2,3,0,1:T(8,128)(2,1)} copy(bf16[3,256,16,2,128]{4,2,3,1,0:T(8,128)(2,1)} %bitcast.58) | data formatting | bytes 12582912 | tf_op jit(solution)/shard_map/optimization_barrier | solution.py:75
  35.2 16.5 %all-to-all-start = ((bf16[3,256,16,2,128]{4,2,3,0,1:T(8,128)(2,1)}), bf16[3,256,16,2,128]{4,2,3,0,1:T(8,128)(2,1)}, u32[]{:S(2)}, u32[]{:S(2)}) async-start(bf16[3,256,16,2,128]{4,2,3,0,1:T(8,128)(2,1)} %copy.83), calls=%async_computation | async-start | bytes 12582912 | tf_op jit(solution)/shard_map/all_to_all | solution.py:76
  51.7 0.0 all-gather.5.cloned.1.call-start
  51.8 0.7 all-gather.5.cloned.1.call-update
  52.5 0.1 gt.33
  52.6 69.0 %all-gather.3.cloned.1.call-done = s32[8,32768,1]{1,2,0:T(1,128)} async-done(((s32[8,512,1]{1,2,0:T(1,128)}), s32[8,32768,1]{1,2,0:T(1,128)}) %all-gather.3.cloned.1.call-update) | async-done | bytes 1048592 | tf_op jit(solution)/shard_map/all_gather | solution.py:79
  121.6 1.9 convert_reduce_fusion
  123.6 0.1 copy.87
  123.7 0.1 gt.30
  123.8 0.1 copy.88
  123.9 0.7 compare_convert_fusion.mask_ref
  124.5 80.9 %all-to-all-done = bf16[3,256,16,2,128]{4,2,3,0,1:T(8,128)(2,1)} async-done(((bf16[3,256,16,2,128]{4,2,3,0,1:T(8,128)(2,1)}), bf16[3,256,16,2,128]{4,2,3,0,1:T(8,128)(2,1)}, u32[]{:S(2)}, u32[]{:S(2)}) %all-to-all-start) | async-done | bytes 6291488 | tf_op jit(solution)/shard_map/all_to_all | solution.py:76
  205.5 4.5 %fusion.35 = (bf16[1,16,256,2,128]{4,1,3,0,2:T(8,128)(2,1)S(1)}, bf16[1,16,256,2,128]{4,1,3,0,2:T(8,128)(2,1)S(1)}, bf16[1,16,256,2,128]{4,1,3,0,2:T(8,128)(2,1)S(1)}) fusion(bf16[3,16,256,2,128]{4,1,3,0,2:T(8,128)(2,1)} %bitcast.15), kind=kLoop, calls=%fused_computation.46 | loop fusion | bytes 12582912 | tf_op jit(solution)/shard_map/slice | solution.py:50
  210.0 3.2 copy.84
  213.2 3.2 copy.85
  216.4 3.2 copy.86
  219.6 18.0 %shard_map.55 = bf16[64,16,8,128]{3,2,1,0:T(8,128)(2,1)} custom-call(bf16[16,512,128]{2,1,0:T(8,128)(2,1)} %bitcast.61, bf16[16,512,128]{2,1,0:T(8,128)(2,1)} %bitcast.62, bf16[16,512,128]{2,1,0:T(8,128)(2,1)} %bitcast.63, f32[16,1,512]{2,1,0:T(1,128)} %compare_convert_fusion.mask_ref), custom_call_target="tpu_custom_call" | custom-call | flops 2147483648 | bytes 8388608 | tf_op jit(solution)/shard_map/pallas_call | solution.py:39
  237.6 0.0 copy-start.8
  237.6 6.3 %all-to-all-start.1 = ((bf16[64,16,8,128]{3,2,1,0:T(8,128)(2,1)}), bf16[64,16,8,128]{3,2,1,0:T(8,128)(2,1)S(1)}, u32[]{:S(2)}, u32[]{:S(2)}) async-start(bf16[64,16,8,128]{3,2,1,0:T(8,128)(2,1)} %shard_map.55), calls=%async_computation.1 | async-start | bytes 4194304 | tf_op jit(solution)/shard_map/all_to_all | solution.py:90
  244.0 0.3 reduce-scatter.2.cloned.1.call-start
  244.2 0.0 copy-done.8
  244.2 0.3 convert_convert_fusion
  244.5 1.3 copy.92
  245.8 0.7 fusion.6
  246.5 48.8 %all-to-all-done.1 = bf16[64,16,8,128]{3,2,1,0:T(8,128)(2,1)S(1)} async-done(((bf16[64,16,8,128]{3,2,1,0:T(8,128)(2,1)}), bf16[64,16,8,128]{3,2,1,0:T(8,128)(2,1)S(1)}, u32[]{:S(2)}, u32[]{:S(2)}) %all-to-all-start.1) | async-done | bytes 2097184 | tf_op jit(solution)/shard_map/all_to_all | solution.py:90
  295.3 0.0 copy-start.6
  295.3 1.4 copy.90
  296.7 0.0 copy-done.6
  296.7 2.6 fusion.17
  299.2 0.7 copy.94
  300.0 0.0 all-gather.5.cloned.1.call-done
  300.0 9.5 %convolution_convert_fusion = bf16[512,4096]{1,0:T(8,128)(2,1)} fusion(bf16[1024,4096]{0,1:T(8,128)(2,1)} %all-gather.5.cloned.1.call-done, bf16[64,8,8,128]{3,2,1,0:T(8,128)(2,1)S(1)} %bitcast.70), kind=kOutput, calls=%fused_computation.1 | convolution fusion | flops 4297064448 | bytes 13631488 | tf_op jit(solution)/shard_map/dot_general | solution.py:99
  309.5 0.0 copy-start.1
  309.5 0.0 reduce-scatter.2.cloned.1.call-update
  309.5 44.6 %reduce-scatter.2.cloned.1.call-done = bf16[512,1024]{1,0:T(8,128)(2,1)} async-done(((bf16[512,4096]{1,0:T(8,128)(2,1)}), bf16[512,1024]{1,0:T(8,128)(2,1)}) %reduce-scatter.2.cloned.1.call-update) | async-done | bytes 1048592 | tf_op jit(solution)/shard_map/reduce_scatter | solution.py:104
  354.1 0.0 copy-done.1
  (9 shorter events, 0.1 us)
Async XLA Ops:
  6.5 0.8 copy-start
  6.5 2.8 copy-start.2
  6.5 115.1 %all-gather.3.cloned.1.call-start = ((), (), s32[]{:S(2)}) async-start(), calls=%async_computation.3 | async-start | bytes 1064960 | tf_op jit(solution)/shard_map/all_gather | solution.py:79
  9.4 2.0 copy-start.3
  11.4 2.0 copy-start.4
  13.3 2.0 copy-start.5
  14.0 1.3 copy-start.7
  35.2 170.3 %all-to-all-start = ((bf16[3,256,16,2,128]{4,2,3,0,1:T(8,128)(2,1)}), bf16[3,256,16,2,128]{4,2,3,0,1:T(8,128)(2,1)}, u32[]{:S(2)}, u32[]{:S(2)}) async-start(bf16[3,256,16,2,128]{4,2,3,0,1:T(8,128)(2,1)} %copy.83), calls=%async_computation | async-start | bytes 12582912 | tf_op jit(solution)/shard_map/all_to_all | solution.py:76
  51.7 248.3 %all-gather.5.cloned.1.call-start = ((), (), s32[]{:S(2)}) async-start(), calls=%async_computation.4 | async-start | bytes 8519680 | tf_op jit(solution)/shard_map/all_gather | solution.py:101
  237.6 6.6 %copy-start.8 = (s32[8,512,1]{1,2,0:T(1,128)S(1)}, s32[8,512,1]{1,2,0:T(1,128)}, u32[]{:S(2)}) copy-start(s32[8,512,1]{1,2,0:T(1,128)} %constant_dynamic-slice_fusion.1) | copy-start | bytes 49156
  237.6 57.7 %all-to-all-start.1 = ((bf16[64,16,8,128]{3,2,1,0:T(8,128)(2,1)}), bf16[64,16,8,128]{3,2,1,0:T(8,128)(2,1)S(1)}, u32[]{:S(2)}, u32[]{:S(2)}) async-start(bf16[64,16,8,128]{3,2,1,0:T(8,128)(2,1)} %shard_map.55), calls=%async_computation.1 | async-start | bytes 4194304 | tf_op jit(solution)/shard_map/all_to_all | solution.py:90
  244.0 110.1 %reduce-scatter.2.cloned.1.call-start = ((), (), s32[]{:S(2)}) async-start(), calls=%async_computation.5 | async-start | bytes 5242880 | tf_op jit(solution)/shard_map/reduce_scatter | solution.py:104
  295.3 1.4 copy-start.6
  309.5 44.6 %copy-start.1 = (s32[32,512,1]{1,2,0:T(1,128)S(1)}, s32[32,512,1]{1,2,0:T(1,128)}, u32[]{:S(2)}) copy-start(s32[32,512,1]{1,2,0:T(1,128)} %param.8) | copy-start | bytes 196612
Sparse Core Ops, SparseCore 0:
  28.7 92.8 all-gather.2
  124.4 98.9 all-gather.4
  309.7 44.3 reduce-scatter.1

commit v8 on v7

--- a/solution.py
+++ b/solution.py
@@ -43,8 +43,8 @@
         out_specs=pl.BlockSpec((n_dest, 1, lanes, HD), lambda i: (0, i, 0, 0)),
         out_shape=jax.ShapeDtypeStruct((n_dest, items, lanes, HD), jnp.bfloat16),
         cost_estimate=pl.CostEstimate(
-            flops=4 * items * slots * slots * HD,
-            transcendentals=items * slots * slots,
+            flops=40 * items * slots * slots * HD,
+            transcendentals=10 * items * slots * slots,
             bytes_accessed=4 * items * slots * HD * 2,
         ),
     )(packed[0], packed[1], packed[2], mask)
@@ -72,7 +72,6 @@
     packed = packed.transpose(0, 3, 1, 2, 4, 5).reshape(3, n_src, per_owner, slot_depth, HD)
 
     group_ids = lax.dynamic_slice_in_dim(cluster_ids, head_group * group_heads, group_heads, 0)
-    group_ids, packed = lax.optimization_barrier((group_ids, packed))
     arrived = lax.all_to_all(packed, ("seq", "head"), split_axis=1, concat_axis=1, tiled=True)
     arrived = arrived.transpose(0, 2, 1, 3, 4).reshape(3, per_owner, n_src * slot_depth, HD)
 

time: 362 us -> 352 us (0.972)
  local copies, waits for them, and re-layouts: 41.2 us -> 37.1 us
  waiting for transfers between devices: 244 us -> 240 us
    all_to_all x1, waiting for transfers between devices: 80.9 us -> 55.7 us  [body(): lax.all_to_all(packed, ('seq', 'head'), split_axis=1, concat_axis=1, tile...]
    all_gather x1, waiting for transfers between devices: 69 us -> 91.2 us  [body(): seen_ids = lax.all_gather(group_ids, 'seq', axis=1, tiled=True)]
    optimization_barrier x1 -> x0, local copies, waits for them, and re-layouts: 6.55 us -> none  [body(): group_ids, packed = lax.optimization_barrier((group_ids, packed))]
    reshape x0 -> x1, local copies, waits for them, and re-layouts: none -> 3.65 us  [body(): packed.transpose(0, 3, 1, 2, 4, 5)]
  transfers between devices with their start and end apart: 5 -> 5, of which waited for: 4 -> 4; matrix products, arithmetic and copies ran while one was open for 8% -> 7% of each run, Pallas kernels for 5% -> 5%
where the time goes in v8:
time: 352 us; the launch traced here: 351 us
  waiting for transfers between devices  240 us (68%)
  local copies, waits for them, and re-layouts  37.1 us (11%)
  starting transfers between devices  22.3 us (6%)
  Pallas kernels  18.2 us (5%)
  matrix products  16.7 us (5%)
  between operations  13.4 us (4%)
    all_gather x1, waiting for transfers between devices, body(): seen_ids = lax.all_gather(group_ids, 'seq', axis=1, tiled=True)  91.2 us
    all_to_all x1, waiting for transfers between devices, body(): lax.all_to_all(packed, ('seq', 'head'), split_axis=1, concat_axis=1, tile...  55.7 us
    all_to_all x1, waiting for transfers between devices, body(): lax.all_to_all(result_block, 'seq', split_axis=0, concat_axis=0, tiled=True)  48.8 us
    reduce_scatter x1, waiting for transfers between devices, body(): lax.psum_scatter(partial_value.astype(jnp.bfloat16), 'head', scatter_dime...  43.5 us
    pallas_call x1, Pallas kernels, attend_blocks(): pl.pallas_call(attend_kernel, grid=(items,), in_specs=[row_spec, row_spec...  18.2 us
    all_to_all x1, starting transfers between devices, body(): lax.all_to_all(packed, ('seq', 'head'), split_axis=1, concat_axis=1, tile...  16.5 us
    dot_general x1, matrix products, body(): jnp.dot(gathered, lax.all_gather(out_weight, 'seq', axis=1, tiled=True),...  9.5 us
    slice x2, local copies, waits for them, and re-layouts, attend_blocks(): packed[2]  7.72 us
  transfers between devices with their start and end apart: 5, of which 4 were waited for; matrix products, arithmetic and copies ran while one was open for 7% of the time, Pallas kernels for 5%

profile of v8, /device:TPU:1, one launch (start us, length us, event | category | flops | bytes accessed | tf_op | source)
XLA Modules:
  0.0 350.8 jit_solution(17025183279002031212)
XLA Ops:
  6.5 0.0 copy-start
  6.5 0.0 copy-start.2
  6.5 0.8 copy-done
  7.4 1.2 convert_convert_fusion.1
  8.6 0.7 fusion.5
  9.3 0.0 copy-done.2
  9.4 0.0 copy-start.3
  9.4 0.7 copy.78
  10.0 1.3 copy.81
  11.4 0.0 copy-done.3
  11.4 0.0 copy-start.4
  11.4 0.7 copy.79
  12.0 1.3 copy.82
  13.3 0.0 copy-done.4
  13.3 0.0 copy-start.5
  13.3 0.7 copy.80
  14.0 0.0 copy-start.7
  14.0 1.3 copy.83
  15.3 0.0 copy-done.5
  15.3 0.0 copy-done.7
  15.3 3.3 convert_bitcast_fusion
  18.6 2.6 copy.84
  21.3 4.0 %copy.85 = bf16[3,64,4,16,2,128]{5,3,4,2,1,0:T(8,128)(2,1)S(1)} copy(bf16[3,64,4,16,2,128]{5,1,3,2,4,0:T(8,128)(2,1)S(1)} %bitcast.60) | data formatting | bytes 12582912 | tf_op jit(solution)/shard_map/transpose | solution.py:72
  25.3 3.7 %copy.86 = bf16[3,256,16,2,128]{4,2,3,0,1:T(8,128)(2,1)} copy(bf16[3,256,16,2,128]{4,2,3,1,0:T(8,128)(2,1)S(1)} %bitcast.61) | data formatting | bytes 12582912 | tf_op jit(solution)/shard_map/reshape | solution.py:72
  29.0 16.5 %all-to-all-start = ((bf16[3,256,16,2,128]{4,2,3,0,1:T(8,128)(2,1)}), bf16[3,256,16,2,128]{4,2,3,0,1:T(8,128)(2,1)}, u32[]{:S(2)}, u32[]{:S(2)}) async-start(bf16[3,256,16,2,128]{4,2,3,0,1:T(8,128)(2,1)} %copy.86), calls=%async_computation | async-start | bytes 12582912 | tf_op jit(solution)/shard_map/all_to_all | solution.py:75
  45.5 0.0 all-gather.3.cloned.1.call-start
  45.6 0.6 copy.118
  46.2 0.1 all-gather.3.cloned.1.call-update
  46.3 0.0 all-gather.5.cloned.1.call-start
  46.3 0.7 all-gather.5.cloned.1.call-update
  47.0 0.1 gt.33
  47.2 91.2 %all-gather.3.cloned.1.call-done = s32[8,32768,1]{1,0,2:T(8,128)} async-done(((s32[8,512,1]{1,0,2:T(8,128)}), s32[8,32768,1]{1,0,2:T(8,128)}) %all-gather.3.cloned.1.call-update) | async-done | bytes 1048592 | tf_op jit(solution)/shard_map/all_gather | solution.py:78
  138.4 1.4 copy.91
  139.9 0.7 convert_reduce_fusion
  140.6 0.1 copy.92
  140.7 0.1 gt.30
  140.8 0.1 copy.93
  140.9 0.7 compare_convert_fusion.mask_ref
  141.5 55.7 %all-to-all-done = bf16[3,256,16,2,128]{4,2,3,0,1:T(8,128)(2,1)} async-done(((bf16[3,256,16,2,128]{4,2,3,0,1:T(8,128)(2,1)}), bf16[3,256,16,2,128]{4,2,3,0,1:T(8,128)(2,1)}, u32[]{:S(2)}, u32[]{:S(2)}) %all-to-all-start) | async-done | bytes 6291488 | tf_op jit(solution)/shard_map/all_to_all | solution.py:75
  197.3 4.5 %fusion.35 = (bf16[1,16,256,2,128]{4,1,3,0,2:T(8,128)(2,1)S(1)}, bf16[1,16,256,2,128]{4,1,3,0,2:T(8,128)(2,1)S(1)}, bf16[1,16,256,2,128]{4,1,3,0,2:T(8,128)(2,1)S(1)}) fusion(bf16[3,16,256,2,128]{4,1,3,0,2:T(8,128)(2,1)} %bitcast.15), kind=kLoop, calls=%fused_computation.47 | loop fusion | bytes 12582912 | tf_op jit(solution)/shard_map/slice | solution.py:50
  201.8 3.2 copy.87
  205.0 3.2 copy.88
  208.2 3.2 copy.89
  211.4 18.2 %shard_map.55 = bf16[64,16,8,128]{3,2,1,0:T(8,128)(2,1)} custom-call(bf16[16,512,128]{2,1,0:T(8,128)(2,1)} %bitcast.66, bf16[16,512,128]{2,1,0:T(8,128)(2,1)} %bitcast.67, bf16[16,512,128]{2,1,0:T(8,128)(2,1)} %bitcast.68, f32[16,1,512]{2,1,0:T(1,128)} %compare_convert_fusion.mask_ref), custom_call_target="tpu_custom_call" | custom-call | flops 21474836480 | bytes 8388608 | tf_op jit(solution)/shard_map/pallas_call | solution.py:39
  229.6 0.0 copy-start.8
  229.6 5.5 %all-to-all-start.1 = ((bf16[64,16,8,128]{3,2,1,0:T(8,128)(2,1)}), bf16[64,16,8,128]{3,2,1,0:T(8,128)(2,1)S(1)}, u32[]{:S(2)}, u32[]{:S(2)}) async-start(bf16[64,16,8,128]{3,2,1,0:T(8,128)(2,1)} %shard_map.55), calls=%async_computation.1 | async-start | bytes 4194304 | tf_op jit(solution)/shard_map/all_to_all | solution.py:89
  235.1 0.3 reduce-scatter.2.cloned.1.call-start
  235.4 0.0 copy-done.8
  235.4 0.3 convert_convert_fusion
  235.6 1.3 copy.96
  237.0 0.7 fusion.6
  237.7 48.8 %all-to-all-done.1 = bf16[64,16,8,128]{3,2,1,0:T(8,128)(2,1)S(1)} async-done(((bf16[64,16,8,128]{3,2,1,0:T(8,128)(2,1)}), bf16[64,16,8,128]{3,2,1,0:T(8,128)(2,1)S(1)}, u32[]{:S(2)}, u32[]{:S(2)}) %all-to-all-start.1) | async-done | bytes 2097184 | tf_op jit(solution)/shard_map/all_to_all | solution.py:89
  286.5 0.0 copy-start.6
  286.5 1.4 copy.95
  287.8 0.0 copy-done.6
  287.8 2.6 fusion.17
  290.4 0.7 copy.98
  291.1 0.0 all-gather.5.cloned.1.call-done
  291.2 9.5 %convolution_convert_fusion = bf16[512,4096]{1,0:T(8,128)(2,1)} fusion(bf16[1024,4096]{0,1:T(8,128)(2,1)} %all-gather.5.cloned.1.call-done, bf16[64,8,8,128]{3,2,1,0:T(8,128)(2,1)S(1)} %bitcast.72), kind=kOutput, calls=%fused_computation.1 | convolution fusion | flops 4297064448 | bytes 13631488 | tf_op jit(solution)/shard_map/dot_general | solution.py:98
  300.7 0.0 copy-start.1
  300.7 0.0 reduce-scatter.2.cloned.1.call-update
  300.7 43.5 %reduce-scatter.2.cloned.1.call-done = bf16[512,1024]{1,0:T(8,128)(2,1)} async-done(((bf16[512,4096]{1,0:T(8,128)(2,1)}), bf16[512,1024]{1,0:T(8,128)(2,1)}) %reduce-scatter.2.cloned.1.call-update) | async-done | bytes 1048592 | tf_op jit(solution)/shard_map/reduce_scatter | solution.py:103
  344.2 0.0 copy-done.1
  (9 shorter events, 0.1 us)
Async XLA Ops:
  6.5 0.8 copy-start
  6.5 2.8 copy-start.2
  9.4 2.0 copy-start.3
  11.4 2.0 copy-start.4
  13.3 2.0 copy-start.5
  14.0 1.3 copy-start.7
  29.0 168.3 %all-to-all-start = ((bf16[3,256,16,2,128]{4,2,3,0,1:T(8,128)(2,1)}), bf16[3,256,16,2,128]{4,2,3,0,1:T(8,128)(2,1)}, u32[]{:S(2)}, u32[]{:S(2)}) async-start(bf16[3,256,16,2,128]{4,2,3,0,1:T(8,128)(2,1)} %copy.86), calls=%async_computation | async-start | bytes 12582912 | tf_op jit(solution)/shard_map/all_to_all | solution.py:75
  45.5 92.9 %all-gather.3.cloned.1.call-start = ((), (), s32[]{:S(2)}) async-start(), calls=%async_computation.3 | async-start | bytes 1064960 | tf_op jit(solution)/shard_map/all_gather | solution.py:78
  46.3 244.9 %all-gather.5.cloned.1.call-start = ((), (), s32[]{:S(2)}) async-start(), calls=%async_computation.4 | async-start | bytes 8519680 | tf_op jit(solution)/shard_map/all_gather | solution.py:100
  229.6 5.8 %copy-start.8 = (s32[8,512,1]{1,0,2:T(8,128)S(1)}, s32[8,512,1]{1,0,2:T(8,128)}, u32[]{:S(2)}) copy-start(s32[8,512,1]{1,0,2:T(8,128)} %copy.118) | copy-start | bytes 49156
  229.6 56.8 %all-to-all-start.1 = ((bf16[64,16,8,128]{3,2,1,0:T(8,128)(2,1)}), bf16[64,16,8,128]{3,2,1,0:T(8,128)(2,1)S(1)}, u32[]{:S(2)}, u32[]{:S(2)}) async-start(bf16[64,16,8,128]{3,2,1,0:T(8,128)(2,1)} %shard_map.55), calls=%async_computation.1 | async-start | bytes 4194304 | tf_op jit(solution)/shard_map/all_to_all | solution.py:89
  235.1 109.1 %reduce-scatter.2.cloned.1.call-start = ((), (), s32[]{:S(2)}) async-start(), calls=%async_computation.5 | async-start | bytes 5242880 | tf_op jit(solution)/shard_map/reduce_scatter | solution.py:103
  286.5 1.4 copy-start.6
  300.7 43.6 %copy-start.1 = (s32[32,512,1]{1,2,0:T(1,128)S(1)}, s32[32,512,1]{1,2,0:T(1,128)}, u32[]{:S(2)}) copy-start(s32[32,512,1]{1,2,0:T(1,128)} %param.8) | copy-start | bytes 196612
Sparse Core Ops, SparseCore 0:
  49.1 89.2 all-gather.2
  141.2 91.9 all-gather.4
  300.8 43.3 reduce-scatter.1

commit v9 on v8

--- a/solution.py
+++ b/solution.py
@@ -21,13 +21,13 @@
 
 def attend_kernel(q_ref, k_ref, v_ref, mask_ref, out_ref):
     scores = lax.dot_general(
-        q_ref[0], k_ref[0], (((1,), (1,)), ((), ())), preferred_element_type=jnp.float32
+        q_ref[0, 0], k_ref[0, 0], (((1,), (1,)), ((), ())), preferred_element_type=jnp.float32
     ) * HD ** (-0.5)
     scores = jnp.where(mask_ref[0] > 0, scores, -1e30)
     row_max = jnp.max(scores, axis=-1, keepdims=True)
     raised = jnp.exp(scores - row_max)
     weights = (raised / jnp.sum(raised, axis=-1, keepdims=True)).astype(jnp.bfloat16)
-    result = jnp.dot(weights, v_ref[0], preferred_element_type=jnp.float32)
+    result = jnp.dot(weights, v_ref[0, 0], preferred_element_type=jnp.float32)
     out_ref[:, 0] = result.reshape(out_ref.shape[0], out_ref.shape[2], HD).astype(out_ref.dtype)
 
 
@@ -35,11 +35,11 @@
     items, slots, _ = packed.shape[1:]
     lanes = slots // n_dest
     mask = validity.astype(jnp.float32).reshape(items, 1, slots)
-    row_spec = pl.BlockSpec((1, slots, HD), lambda i: (i, 0, 0))
+    specs = [pl.BlockSpec((1, 1, slots, HD), lambda i, x=x: (x, i, 0, 0)) for x in range(3)]
     return pl.pallas_call(
         attend_kernel,
         grid=(items,),
-        in_specs=[row_spec, row_spec, row_spec, pl.BlockSpec((1, 1, slots), lambda i: (i, 0, 0))],
+        in_specs=specs + [pl.BlockSpec((1, 1, slots), lambda i: (i, 0, 0))],
         out_specs=pl.BlockSpec((n_dest, 1, lanes, HD), lambda i: (0, i, 0, 0)),
         out_shape=jax.ShapeDtypeStruct((n_dest, items, lanes, HD), jnp.bfloat16),
         cost_estimate=pl.CostEstimate(
@@ -47,7 +47,7 @@
             transcendentals=10 * items * slots * slots,
             bytes_accessed=4 * items * slots * HD * 2,
         ),
-    )(packed[0], packed[1], packed[2], mask)
+    )(packed, packed, packed, mask)
 
 
 def body(queries, keys, values, cluster_ids, out_weight):

time: 352 us -> 348 us (0.989)
  local copies, waits for them, and re-layouts: 37.1 us -> 33.3 us
    slice x4 -> x0, local copies, waits for them, and re-layouts: 14.1 us -> none  [the longest x2 7.72 us: attend_blocks(): packed[2]]
    transpose x0 -> x1, local copies, waits for them, and re-layouts: none -> 10.3 us  [body(): arrived.transpose(0, 2, 1, 3, 4)]
  transfers between devices with their start and end apart: 5 -> 5, of which waited for: 4 -> 4; matrix products, arithmetic and copies ran while one was open for 7% -> 6% of each run, Pallas kernels for 5% -> 5%
where the time goes in v9:
time: 348 us; the launch traced here: 347 us
  waiting for transfers between devices  240 us (69%)
  local copies, waits for them, and re-layouts  33.3 us (10%)
  starting transfers between devices  22 us (6%)
  Pallas kernels  18.1 us (5%)
  matrix products  16.7 us (5%)
  between operations  13.4 us (4%)
    all_gather x1, waiting for transfers between devices, body(): seen_ids = lax.all_gather(group_ids, 'seq', axis=1, tiled=True)  91.2 us
    all_to_all x1, waiting for transfers between devices, body(): lax.all_to_all(packed, ('seq', 'head'), split_axis=1, concat_axis=1, tile...  55.7 us
    all_to_all x1, waiting for transfers between devices, body(): lax.all_to_all(result_block, 'seq', split_axis=0, concat_axis=0, tiled=True)  49 us
    reduce_scatter x1, waiting for transfers between devices, body(): lax.psum_scatter(partial_value.astype(jnp.bfloat16), 'head', scatter_dime...  43.5 us
    pallas_call x1, Pallas kernels, attend_blocks(): pl.pallas_call(attend_kernel, grid=(items,), in_specs=specs + [pl.BlockSp...  18.1 us
    all_to_all x1, starting transfers between devices, body(): lax.all_to_all(packed, ('seq', 'head'), split_axis=1, concat_axis=1, tile...  16.5 us
    transpose x1, local copies, waits for them, and re-layouts, body(): arrived.transpose(0, 2, 1, 3, 4)  10.3 us
    dot_general x1, matrix products, body(): jnp.dot(gathered, lax.all_gather(out_weight, 'seq', axis=1, tiled=True),...  9.52 us
  transfers between devices with their start and end apart: 5, of which 4 were waited for; matrix products, arithmetic and copies ran while one was open for 6% of the time, Pallas kernels for 5%

profile of v9, /device:TPU:1, one launch (start us, length us, event | category | flops | bytes accessed | tf_op | source)
XLA Modules:
  0.0 346.8 jit_solution(5103330275289145397)
XLA Ops:
  6.5 0.0 copy-start
  6.5 0.0 copy-start.2
  6.5 0.8 copy-done
  7.4 1.2 convert_convert_fusion.1
  8.6 0.7 fusion.5
  9.3 0.0 copy-done.2
  9.4 0.0 copy-start.3
  9.4 0.7 copy.72
  10.0 1.3 copy.75
  11.4 0.0 copy-done.3
  11.4 0.0 copy-start.4
  11.4 0.7 copy.73
  12.0 1.3 copy.76
  13.3 0.0 copy-done.4
  13.3 0.0 copy-start.5
  13.3 0.7 copy.74
  14.0 0.0 copy-start.7
  14.0 1.3 copy.77
  15.3 0.0 copy-done.5
  15.3 0.0 copy-done.7
  15.3 3.3 convert_bitcast_fusion
  18.6 2.6 copy.78
  21.3 4.0 %copy.79 = bf16[3,64,4,16,2,128]{5,3,4,2,1,0:T(8,128)(2,1)S(1)} copy(bf16[3,64,4,16,2,128]{5,1,3,2,4,0:T(8,128)(2,1)S(1)} %bitcast.58) | data formatting | bytes 12582912 | tf_op jit(solution)/shard_map/transpose | solution.py:72
  25.3 3.7 %copy.80 = bf16[3,256,16,2,128]{4,2,3,0,1:T(8,128)(2,1)} copy(bf16[3,256,16,2,128]{4,2,3,1,0:T(8,128)(2,1)S(1)} %bitcast.59) | data formatting | bytes 12582912 | tf_op jit(solution)/shard_map/reshape | solution.py:72
  29.0 16.5 %all-to-all-start = ((bf16[3,256,16,2,128]{4,2,3,0,1:T(8,128)(2,1)}), bf16[3,256,16,2,128]{4,2,3,0,1:T(8,128)(2,1)}, u32[]{:S(2)}, u32[]{:S(2)}) async-start(bf16[3,256,16,2,128]{4,2,3,0,1:T(8,128)(2,1)} %copy.80), calls=%async_computation | async-start | bytes 12582912 | tf_op jit(solution)/shard_map/all_to_all | solution.py:75
  45.5 0.0 all-gather.3.cloned.1.call-start
  45.6 0.6 copy.110
  46.2 0.1 all-gather.3.cloned.1.call-update
  46.3 0.0 all-gather.5.cloned.1.call-start
  46.3 0.7 all-gather.5.cloned.1.call-update
  47.1 0.1 gt.33
  47.2 91.2 %all-gather.3.cloned.1.call-done = s32[8,32768,1]{1,0,2:T(8,128)} async-done(((s32[8,512,1]{1,0,2:T(8,128)}), s32[8,32768,1]{1,0,2:T(8,128)}) %all-gather.3.cloned.1.call-update) | async-done | bytes 1048592 | tf_op jit(solution)/shard_map/all_gather | solution.py:78
  138.4 1.4 copy.83
  139.9 0.7 convert_reduce_fusion
  140.6 0.1 copy.84
  140.7 0.1 gt.30
  140.8 0.1 copy.85
  140.9 0.7 compare_convert_fusion.mask_ref
  141.5 55.7 %all-to-all-done = bf16[3,256,16,2,128]{4,2,3,0,1:T(8,128)(2,1)} async-done(((bf16[3,256,16,2,128]{4,2,3,0,1:T(8,128)(2,1)}), bf16[3,256,16,2,128]{4,2,3,0,1:T(8,128)(2,1)}, u32[]{:S(2)}, u32[]{:S(2)}) %all-to-all-start) | async-done | bytes 6291488 | tf_op jit(solution)/shard_map/all_to_all | solution.py:75
  197.3 10.3 %copy.81 = bf16[3,16,256,2,128]{4,3,2,1,0:T(2,128)(2,1)} copy(bf16[3,16,256,2,128]{4,1,3,0,2:T(8,128)(2,1)} %bitcast.15) | data formatting | bytes 12582912 | tf_op jit(solution)/shard_map/transpose | solution.py:76
  207.6 18.1 %shard_map.55 = bf16[64,16,8,128]{3,2,1,0:T(8,128)(2,1)} custom-call(bf16[3,16,512,128]{3,2,1,0:T(8,128)(2,1)} %bitcast.61, bf16[3,16,512,128]{3,2,1,0:T(8,128)(2,1)} %bitcast.62, bf16[3,16,512,128]{3,2,1,0:T(8,128)(2,1)} %bitcast.63, f32[16,1,512]{2,1,0:T(1,128)} %compare_convert_fusion.mask_ref), custom_call_target="tpu_custom_call" | custom-call | flops 21474836480 | bytes 8388608 | tf_op jit(solution)/shard_map/pallas_call | solution.py:39
  225.7 0.0 copy-start.8
  225.8 5.3 %all-to-all-start.1 = ((bf16[64,16,8,128]{3,2,1,0:T(8,128)(2,1)}), bf16[64,16,8,128]{3,2,1,0:T(8,128)(2,1)S(1)}, u32[]{:S(2)}, u32[]{:S(2)}) async-start(bf16[64,16,8,128]{3,2,1,0:T(8,128)(2,1)} %shard_map.55), calls=%async_computation.1 | async-start | bytes 4194304 | tf_op jit(solution)/shard_map/all_to_all | solution.py:89
  231.1 0.0 reduce-scatter.2.cloned.1.call-start
  231.1 0.0 copy-done.8
  231.1 0.3 convert_convert_fusion
  231.4 1.3 copy.88
  232.7 0.7 fusion.6
  233.4 49.0 %all-to-all-done.1 = bf16[64,16,8,128]{3,2,1,0:T(8,128)(2,1)S(1)} async-done(((bf16[64,16,8,128]{3,2,1,0:T(8,128)(2,1)}), bf16[64,16,8,128]{3,2,1,0:T(8,128)(2,1)S(1)}, u32[]{:S(2)}, u32[]{:S(2)}) %all-to-all-start.1) | async-done | bytes 2097184 | tf_op jit(solution)/shard_map/all_to_all | solution.py:89
  282.4 0.0 copy-start.6
  282.4 1.4 copy.87
  283.8 0.0 copy-done.6
  283.8 2.6 fusion.17
  286.4 0.7 copy.90
  287.1 0.0 all-gather.5.cloned.1.call-done
  287.1 9.5 %convolution_convert_fusion = bf16[512,4096]{1,0:T(8,128)(2,1)} fusion(bf16[1024,4096]{0,1:T(8,128)(2,1)} %all-gather.5.cloned.1.call-done, bf16[64,8,8,128]{3,2,1,0:T(8,128)(2,1)S(1)} %bitcast.70), kind=kOutput, calls=%fused_computation.1 | convolution fusion | flops 4297064448 | bytes 13631488 | tf_op jit(solution)/shard_map/dot_general | solution.py:98
  296.7 0.0 copy-start.1
  296.7 0.0 reduce-scatter.2.cloned.1.call-update
  296.7 43.5 %reduce-scatter.2.cloned.1.call-done = bf16[512,1024]{1,0:T(8,128)(2,1)} async-done(((bf16[512,4096]{1,0:T(8,128)(2,1)}), bf16[512,1024]{1,0:T(8,128)(2,1)}) %reduce-scatter.2.cloned.1.call-update) | async-done | bytes 1048592 | tf_op jit(solution)/shard_map/reduce_scatter | solution.py:103
  340.2 0.0 copy-done.1
  (9 shorter events, 0.1 us)
Async XLA Ops:
  6.5 0.8 copy-start
  6.5 2.8 copy-start.2
  9.4 2.0 copy-start.3
  11.4 2.0 copy-start.4
  13.3 2.0 copy-start.5
  14.0 1.3 copy-start.7
  29.0 168.3 %all-to-all-start = ((bf16[3,256,16,2,128]{4,2,3,0,1:T(8,128)(2,1)}), bf16[3,256,16,2,128]{4,2,3,0,1:T(8,128)(2,1)}, u32[]{:S(2)}, u32[]{:S(2)}) async-start(bf16[3,256,16,2,128]{4,2,3,0,1:T(8,128)(2,1)} %copy.80), calls=%async_computation | async-start | bytes 12582912 | tf_op jit(solution)/shard_map/all_to_all | solution.py:75
  45.5 92.9 %all-gather.3.cloned.1.call-start = ((), (), s32[]{:S(2)}) async-start(), calls=%async_computation.3 | async-start | bytes 1064960 | tf_op jit(solution)/shard_map/all_gather | solution.py:78
  46.3 240.9 %all-gather.5.cloned.1.call-start = ((), (), s32[]{:S(2)}) async-start(), calls=%async_computation.4 | async-start | bytes 8519680 | tf_op jit(solution)/shard_map/all_gather | solution.py:100
  225.7 5.4 %copy-start.8 = (s32[8,512,1]{1,0,2:T(8,128)S(1)}, s32[8,512,1]{1,0,2:T(8,128)}, u32[]{:S(2)}) copy-start(s32[8,512,1]{1,0,2:T(8,128)} %copy.110) | copy-start | bytes 49156
  225.8 56.7 %all-to-all-start.1 = ((bf16[64,16,8,128]{3,2,1,0:T(8,128)(2,1)}), bf16[64,16,8,128]{3,2,1,0:T(8,128)(2,1)S(1)}, u32[]{:S(2)}, u32[]{:S(2)}) async-start(bf16[64,16,8,128]{3,2,1,0:T(8,128)(2,1)} %shard_map.55), calls=%async_computation.1 | async-start | bytes 4194304 | tf_op jit(solution)/shard_map/all_to_all | solution.py:89
  231.1 109.1 %reduce-scatter.2.cloned.1.call-start = ((), (), s32[]{:S(2)}) async-start(), calls=%async_computation.5 | async-start | bytes 5242880 | tf_op jit(solution)/shard_map/reduce_scatter | solution.py:103
  282.4 1.4 copy-start.6
  296.7 43.6 %copy-start.1 = (s32[32,512,1]{1,2,0:T(1,128)S(1)}, s32[32,512,1]{1,2,0:T(1,128)}, u32[]{:S(2)}) copy-start(s32[32,512,1]{1,2,0:T(1,128)} %param.8) | copy-start | bytes 196612
Sparse Core Ops, SparseCore 0:
  49.2 89.2 all-gather.2
  141.2 91.9 all-gather.4
  296.8 43.3 reduce-scatter.1

commit v10 on v9

--- a/solution.py
+++ b/solution.py
@@ -20,27 +20,30 @@
 
 
 def attend_kernel(q_ref, k_ref, v_ref, mask_ref, out_ref):
-    scores = lax.dot_general(
-        q_ref[0, 0], k_ref[0, 0], (((1,), (1,)), ((), ())), preferred_element_type=jnp.float32
-    ) * HD ** (-0.5)
-    scores = jnp.where(mask_ref[0] > 0, scores, -1e30)
-    row_max = jnp.max(scores, axis=-1, keepdims=True)
-    raised = jnp.exp(scores - row_max)
-    weights = (raised / jnp.sum(raised, axis=-1, keepdims=True)).astype(jnp.bfloat16)
-    result = jnp.dot(weights, v_ref[0, 0], preferred_element_type=jnp.float32)
-    out_ref[:, 0] = result.reshape(out_ref.shape[0], out_ref.shape[2], HD).astype(out_ref.dtype)
+    for item in range(q_ref.shape[1]):
+        scores = lax.dot_general(
+            q_ref[0, item], k_ref[0, item], (((1,), (1,)), ((), ())),
+            preferred_element_type=jnp.float32,
+        ) * HD ** (-0.5)
+        scores = jnp.where(mask_ref[item] > 0, scores, -1e30)
+        row_max = jnp.max(scores, axis=-1, keepdims=True)
+        raised = jnp.exp(scores - row_max)
+        weights = (raised / jnp.sum(raised, axis=-1, keepdims=True)).astype(jnp.bfloat16)
+        result = jnp.dot(weights, v_ref[0, item], preferred_element_type=jnp.float32)
+        out_ref[:, item] = result.reshape(out_ref.shape[0], out_ref.shape[2], HD).astype(out_ref.dtype)
 
 
 def attend_blocks(packed, validity, n_dest):
     items, slots, _ = packed.shape[1:]
     lanes = slots // n_dest
     mask = validity.astype(jnp.float32).reshape(items, 1, slots)
-    specs = [pl.BlockSpec((1, 1, slots, HD), lambda i, x=x: (x, i, 0, 0)) for x in range(3)]
+    step = 2
+    specs = [pl.BlockSpec((1, step, slots, HD), lambda i, x=x: (x, i, 0, 0)) for x in range(3)]
     return pl.pallas_call(
         attend_kernel,
-        grid=(items,),
-        in_specs=specs + [pl.BlockSpec((1, 1, slots), lambda i: (i, 0, 0))],
-        out_specs=pl.BlockSpec((n_dest, 1, lanes, HD), lambda i: (0, i, 0, 0)),
+        grid=(items // step,),
+        in_specs=specs + [pl.BlockSpec((step, 1, slots), lambda i: (i, 0, 0))],
+        out_specs=pl.BlockSpec((n_dest, step, lanes, HD), lambda i: (0, i, 0, 0)),
         out_shape=jax.ShapeDtypeStruct((n_dest, items, lanes, HD), jnp.bfloat16),
         cost_estimate=pl.CostEstimate(
             flops=40 * items * slots * slots * HD,

time: 348 us -> 343 us (0.986)
  Pallas kernels: 18.1 us -> 12.5 us
    pallas_call x1, Pallas kernels: 18.1 us -> 12.5 us  [attend_blocks(): pl.pallas_call(attend_kernel, grid=(items // step,), in_specs=specs + [pl...]
  transfers between devices with their start and end apart: 5 -> 5, of which waited for: 4 -> 4; matrix products, arithmetic and copies ran while one was open for 6% -> 6% of each run, Pallas kernels for 5% -> 4%
where the time goes in v10:
time: 343 us
  waiting for transfers between devices  242 us (71%)
  local copies, waits for them, and re-layouts  33.3 us (10%)
  starting transfers between devices  22 us (6%)
  matrix products  16.7 us (5%)
  between operations  13.4 us (4%)
  Pallas kernels  12.5 us (4%)
    all_gather x1, waiting for transfers between devices, body(): seen_ids = lax.all_gather(group_ids, 'seq', axis=1, tiled=True)  91.2 us
    all_to_all x1, waiting for transfers between devices, body(): lax.all_to_all(packed, ('seq', 'head'), split_axis=1, concat_axis=1, tile...  55.7 us
    all_to_all x1, waiting for transfers between devices, body(): lax.all_to_all(result_block, 'seq', split_axis=0, concat_axis=0, tiled=True)  49.4 us
    reduce_scatter x1, waiting for transfers between devices, body(): lax.psum_scatter(partial_value.astype(jnp.bfloat16), 'head', scatter_dime...  44.9 us
    all_to_all x1, starting transfers between devices, body(): lax.all_to_all(packed, ('seq', 'head'), split_axis=1, concat_axis=1, tile...  16.5 us
    pallas_call x1, Pallas kernels, attend_blocks(): pl.pallas_call(attend_kernel, grid=(items // step,), in_specs=specs + [pl...  12.5 us
    transpose x1, local copies, waits for them, and re-layouts, body(): arrived.transpose(0, 2, 1, 3, 4)  10.3 us
    dot_general x1, matrix products, body(): jnp.dot(gathered, lax.all_gather(out_weight, 'seq', axis=1, tiled=True),...  9.51 us
  transfers between devices with their start and end apart: 5, of which 4 were waited for; matrix products, arithmetic and copies ran while one was open for 6% of the time, Pallas kernels for 4%

profile of v10, /device:TPU:1, one launch (start us, length us, event | category | flops | bytes accessed | tf_op | source)
XLA Modules:
  0.0 342.9 jit_solution(14124490380851020363)
XLA Ops:
  6.5 0.0 copy-start
  6.5 0.0 copy-start.2
  6.5 0.8 copy-done
  7.4 1.2 convert_convert_fusion.1
  8.6 0.7 fusion.5
  9.3 0.0 copy-done.2
  9.4 0.0 copy-start.3
  9.4 0.7 copy.72
  10.0 1.3 copy.75
  11.4 0.0 copy-done.3
  11.4 0.0 copy-start.4
  11.4 0.7 copy.73
  12.0 1.3 copy.76
  13.3 0.0 copy-done.4
  13.3 0.0 copy-start.5
  13.3 0.7 copy.74
  14.0 0.0 copy-start.7
  14.0 1.3 copy.77
  15.3 0.0 copy-done.5
  15.3 0.0 copy-done.7
  15.3 3.3 convert_bitcast_fusion
  18.6 2.6 copy.78
  21.3 4.0 %copy.79 = bf16[3,64,4,16,2,128]{5,3,4,2,1,0:T(8,128)(2,1)S(1)} copy(bf16[3,64,4,16,2,128]{5,1,3,2,4,0:T(8,128)(2,1)S(1)} %bitcast.58) | data formatting | bytes 12582912 | tf_op jit(solution)/shard_map/transpose | solution.py:75
  25.3 3.7 %copy.80 = bf16[3,256,16,2,128]{4,2,3,0,1:T(8,128)(2,1)} copy(bf16[3,256,16,2,128]{4,2,3,1,0:T(8,128)(2,1)S(1)} %bitcast.59) | data formatting | bytes 12582912 | tf_op jit(solution)/shard_map/reshape | solution.py:75
  29.0 16.5 %all-to-all-start = ((bf16[3,256,16,2,128]{4,2,3,0,1:T(8,128)(2,1)}), bf16[3,256,16,2,128]{4,2,3,0,1:T(8,128)(2,1)}, u32[]{:S(2)}, u32[]{:S(2)}) async-start(bf16[3,256,16,2,128]{4,2,3,0,1:T(8,128)(2,1)} %copy.80), calls=%async_computation | async-start | bytes 12582912 | tf_op jit(solution)/shard_map/all_to_all | solution.py:78
  45.5 0.0 all-gather.3.cloned.1.call-start
  45.6 0.6 copy.110
  46.2 0.1 all-gather.3.cloned.1.call-update
  46.3 0.0 all-gather.5.cloned.1.call-start
  46.3 0.7 all-gather.5.cloned.1.call-update
  47.1 0.1 gt.33
  47.2 91.2 %all-gather.3.cloned.1.call-done = s32[8,32768,1]{1,0,2:T(8,128)} async-done(((s32[8,512,1]{1,0,2:T(8,128)}), s32[8,32768,1]{1,0,2:T(8,128)}) %all-gather.3.cloned.1.call-update) | async-done | bytes 1048592 | tf_op jit(solution)/shard_map/all_gather | solution.py:81
  138.4 1.4 copy.83
  139.9 0.7 convert_reduce_fusion
  140.6 0.1 copy.84
  140.7 0.1 gt.30
  140.8 0.1 copy.85
  140.9 0.7 compare_convert_fusion.mask_ref
  141.5 55.7 %all-to-all-done = bf16[3,256,16,2,128]{4,2,3,0,1:T(8,128)(2,1)} async-done(((bf16[3,256,16,2,128]{4,2,3,0,1:T(8,128)(2,1)}), bf16[3,256,16,2,128]{4,2,3,0,1:T(8,128)(2,1)}, u32[]{:S(2)}, u32[]{:S(2)}) %all-to-all-start) | async-done | bytes 6291488 | tf_op jit(solution)/shard_map/all_to_all | solution.py:78
  197.3 10.3 %copy.81 = bf16[3,16,256,2,128]{4,3,2,1,0:T(2,128)(2,1)} copy(bf16[3,16,256,2,128]{4,1,3,0,2:T(8,128)(2,1)} %bitcast.15) | data formatting | bytes 12582912 | tf_op jit(solution)/shard_map/transpose | solution.py:79
  207.6 12.5 %shard_map.55 = bf16[64,16,8,128]{3,2,1,0:T(8,128)(2,1)} custom-call(bf16[3,16,512,128]{3,2,1,0:T(8,128)(2,1)} %bitcast.61, bf16[3,16,512,128]{3,2,1,0:T(8,128)(2,1)} %bitcast.62, bf16[3,16,512,128]{3,2,1,0:T(8,128)(2,1)} %bitcast.63, f32[16,1,512]{2,1,0:T(1,128)} %compare_convert_fusion.mask_ref), custom_call_target="tpu_custom_call" | custom-call | flops 21474836480 | bytes 8388608 | tf_op jit(solution)/shard_map/pallas_call | solution.py:42
  220.1 0.0 copy-start.8
  220.1 5.3 %all-to-all-start.1 = ((bf16[64,16,8,128]{3,2,1,0:T(8,128)(2,1)}), bf16[64,16,8,128]{3,2,1,0:T(8,128)(2,1)S(1)}, u32[]{:S(2)}, u32[]{:S(2)}) async-start(bf16[64,16,8,128]{3,2,1,0:T(8,128)(2,1)} %shard_map.55), calls=%async_computation.1 | async-start | bytes 4194304 | tf_op jit(solution)/shard_map/all_to_all | solution.py:92
  225.5 0.0 reduce-scatter.2.cloned.1.call-start
  225.5 0.0 copy-done.8
  225.5 0.3 convert_convert_fusion
  225.8 1.3 copy.88
  227.1 0.7 fusion.6
  227.8 49.4 %all-to-all-done.1 = bf16[64,16,8,128]{3,2,1,0:T(8,128)(2,1)S(1)} async-done(((bf16[64,16,8,128]{3,2,1,0:T(8,128)(2,1)}), bf16[64,16,8,128]{3,2,1,0:T(8,128)(2,1)S(1)}, u32[]{:S(2)}, u32[]{:S(2)}) %all-to-all-start.1) | async-done | bytes 2097184 | tf_op jit(solution)/shard_map/all_to_all | solution.py:92
  277.2 0.0 copy-start.6
  277.2 1.4 copy.87
  278.6 0.0 copy-done.6
  278.6 2.6 fusion.17
  281.2 0.7 copy.90
  281.9 0.0 all-gather.5.cloned.1.call-done
  281.9 9.5 %convolution_convert_fusion = bf16[512,4096]{1,0:T(8,128)(2,1)} fusion(bf16[1024,4096]{0,1:T(8,128)(2,1)} %all-gather.5.cloned.1.call-done, bf16[64,8,8,128]{3,2,1,0:T(8,128)(2,1)S(1)} %bitcast.70), kind=kOutput, calls=%fused_computation.1 | convolution fusion | flops 4297064448 | bytes 13631488 | tf_op jit(solution)/shard_map/dot_general | solution.py:101
  291.4 0.0 copy-start.1
  291.4 0.0 reduce-scatter.2.cloned.1.call-update
  291.5 44.9 %reduce-scatter.2.cloned.1.call-done = bf16[512,1024]{1,0:T(8,128)(2,1)} async-done(((bf16[512,4096]{1,0:T(8,128)(2,1)}), bf16[512,1024]{1,0:T(8,128)(2,1)}) %reduce-scatter.2.cloned.1.call-update) | async-done | bytes 1048592 | tf_op jit(solution)/shard_map/reduce_scatter | solution.py:106
  336.4 0.0 copy-done.1
  (9 shorter events, 0.1 us)
Async XLA Ops:
  6.5 0.8 copy-start
  6.5 2.8 copy-start.2
  9.4 2.0 copy-start.3
  11.4 2.0 copy-start.4
  13.3 2.0 copy-start.5
  14.0 1.3 copy-start.7
  29.0 168.3 %all-to-all-start = ((bf16[3,256,16,2,128]{4,2,3,0,1:T(8,128)(2,1)}), bf16[3,256,16,2,128]{4,2,3,0,1:T(8,128)(2,1)}, u32[]{:S(2)}, u32[]{:S(2)}) async-start(bf16[3,256,16,2,128]{4,2,3,0,1:T(8,128)(2,1)} %copy.80), calls=%async_computation | async-start | bytes 12582912 | tf_op jit(solution)/shard_map/all_to_all | solution.py:78
  45.5 92.9 %all-gather.3.cloned.1.call-start = ((), (), s32[]{:S(2)}) async-start(), calls=%async_computation.3 | async-start | bytes 1064960 | tf_op jit(solution)/shard_map/all_gather | solution.py:81
  46.3 235.6 %all-gather.5.cloned.1.call-start = ((), (), s32[]{:S(2)}) async-start(), calls=%async_computation.4 | async-start | bytes 8519680 | tf_op jit(solution)/shard_map/all_gather | solution.py:103
  220.1 5.4 %copy-start.8 = (s32[8,512,1]{1,0,2:T(8,128)S(1)}, s32[8,512,1]{1,0,2:T(8,128)}, u32[]{:S(2)}) copy-start(s32[8,512,1]{1,0,2:T(8,128)} %copy.110) | copy-start | bytes 49156
  220.1 57.1 %all-to-all-start.1 = ((bf16[64,16,8,128]{3,2,1,0:T(8,128)(2,1)}), bf16[64,16,8,128]{3,2,1,0:T(8,128)(2,1)S(1)}, u32[]{:S(2)}, u32[]{:S(2)}) async-start(bf16[64,16,8,128]{3,2,1,0:T(8,128)(2,1)} %shard_map.55), calls=%async_computation.1 | async-start | bytes 4194304 | tf_op jit(solution)/shard_map/all_to_all | solution.py:92
  225.5 110.9 %reduce-scatter.2.cloned.1.call-start = ((), (), s32[]{:S(2)}) async-start(), calls=%async_computation.5 | async-start | bytes 5242880 | tf_op jit(solution)/shard_map/reduce_scatter | solution.py:106
  277.2 1.4 copy-start.6
  291.4 45.0 %copy-start.1 = (s32[32,512,1]{1,2,0:T(1,128)S(1)}, s32[32,512,1]{1,2,0:T(1,128)}, u32[]{:S(2)}) copy-start(s32[32,512,1]{1,2,0:T(1,128)} %param.8) | copy-start | bytes 196612
Sparse Core Ops, SparseCore 0:
  49.2 89.2 all-gather.2
  141.2 95.9 all-gather.4
  291.6 44.7 reduce-scatter.1

commit v11 on v10

--- a/solution.py
+++ b/solution.py
@@ -37,7 +37,7 @@
     items, slots, _ = packed.shape[1:]
     lanes = slots // n_dest
     mask = validity.astype(jnp.float32).reshape(items, 1, slots)
-    step = 2
+    step = 4
     specs = [pl.BlockSpec((1, step, slots, HD), lambda i, x=x: (x, i, 0, 0)) for x in range(3)]
     return pl.pallas_call(
         attend_kernel,

time: 343 us -> 343 us (level)
  transfers between devices with their start and end apart: 5 -> 5, of which waited for: 4 -> 4; matrix products, arithmetic and copies ran while one was open for 6% -> 6% of each run, Pallas kernels for 4% -> 3%
where the time goes in v11:
time: 343 us; the launch traced here: 342 us
  waiting for transfers between devices  244 us (71%)
  local copies, waits for them, and re-layouts  33.3 us (10%)
  starting transfers between devices  22 us (6%)
  matrix products  16.7 us (5%)
  between operations  13.4 us (4%)
  Pallas kernels  10.6 us (3%)
    all_gather x1, waiting for transfers between devices, body(): seen_ids = lax.all_gather(group_ids, 'seq', axis=1, tiled=True)  91.2 us
    all_to_all x1, waiting for transfers between devices, body(): lax.all_to_all(packed, ('seq', 'head'), split_axis=1, concat_axis=1, tile...  55.7 us
    all_to_all x1, waiting for transfers between devices, body(): lax.all_to_all(result_block, 'seq', split_axis=0, concat_axis=0, tiled=True)  50.1 us
    reduce_scatter x1, waiting for transfers between devices, body(): lax.psum_scatter(partial_value.astype(jnp.bfloat16), 'head', scatter_dime...  45.8 us
    all_to_all x1, starting transfers between devices, body(): lax.all_to_all(packed, ('seq', 'head'), split_axis=1, concat_axis=1, tile...  16.5 us
    pallas_call x1, Pallas kernels, attend_blocks(): pl.pallas_call(attend_kernel, grid=(items // step,), in_specs=specs + [pl...  10.6 us
    transpose x1, local copies, waits for them, and re-layouts, body(): arrived.transpose(0, 2, 1, 3, 4)  10.3 us
    dot_general x1, matrix products, body(): jnp.dot(gathered, lax.all_gather(out_weight, 'seq', axis=1, tiled=True),...  9.52 us
  transfers between devices with their start and end apart: 5, of which 4 were waited for; matrix products, arithmetic and copies ran while one was open for 6% of the time, Pallas kernels for 3%

profile of v11, /device:TPU:1, one launch (start us, length us, event | category | flops | bytes accessed | tf_op | source)
XLA Modules:
  0.0 342.5 jit_solution(1717481614773267669)
XLA Ops:
  6.5 0.0 copy-start
  6.5 0.0 copy-start.2
  6.5 0.8 copy-done
  7.4 1.2 convert_convert_fusion.1
  8.6 0.7 fusion.5
  9.3 0.0 copy-done.2
  9.4 0.0 copy-start.3
  9.4 0.7 copy.72
  10.0 1.3 copy.75
  11.4 0.0 copy-done.3
  11.4 0.0 copy-start.4
  11.4 0.7 copy.73
  12.0 1.3 copy.76
  13.3 0.0 copy-done.4
  13.3 0.0 copy-start.5
  13.3 0.7 copy.74
  14.0 0.0 copy-start.7
  14.0 1.3 copy.77
  15.3 0.0 copy-done.5
  15.3 0.0 copy-done.7
  15.3 3.3 convert_bitcast_fusion
  18.6 2.6 copy.78
  21.3 4.0 %copy.79 = bf16[3,64,4,16,2,128]{5,3,4,2,1,0:T(8,128)(2,1)S(1)} copy(bf16[3,64,4,16,2,128]{5,1,3,2,4,0:T(8,128)(2,1)S(1)} %bitcast.58) | data formatting | bytes 12582912 | tf_op jit(solution)/shard_map/transpose | solution.py:75
  25.3 3.7 %copy.80 = bf16[3,256,16,2,128]{4,2,3,0,1:T(8,128)(2,1)} copy(bf16[3,256,16,2,128]{4,2,3,1,0:T(8,128)(2,1)S(1)} %bitcast.59) | data formatting | bytes 12582912 | tf_op jit(solution)/shard_map/reshape | solution.py:75
  29.0 16.5 %all-to-all-start = ((bf16[3,256,16,2,128]{4,2,3,0,1:T(8,128)(2,1)}), bf16[3,256,16,2,128]{4,2,3,0,1:T(8,128)(2,1)}, u32[]{:S(2)}, u32[]{:S(2)}) async-start(bf16[3,256,16,2,128]{4,2,3,0,1:T(8,128)(2,1)} %copy.80), calls=%async_computation | async-start | bytes 12582912 | tf_op jit(solution)/shard_map/all_to_all | solution.py:78
  45.5 0.0 all-gather.3.cloned.1.call-start
  45.6 0.6 copy.110
  46.2 0.1 all-gather.3.cloned.1.call-update
  46.3 0.0 all-gather.5.cloned.1.call-start
  46.3 0.7 all-gather.5.cloned.1.call-update
  47.1 0.1 gt.33
  47.2 91.2 %all-gather.3.cloned.1.call-done = s32[8,32768,1]{1,0,2:T(8,128)} async-done(((s32[8,512,1]{1,0,2:T(8,128)}), s32[8,32768,1]{1,0,2:T(8,128)}) %all-gather.3.cloned.1.call-update) | async-done | bytes 1048592 | tf_op jit(solution)/shard_map/all_gather | solution.py:81
  138.4 1.4 copy.83
  139.9 0.7 convert_reduce_fusion
  140.6 0.1 copy.84
  140.7 0.1 gt.30
  140.8 0.1 copy.85
  140.9 0.7 compare_convert_fusion.mask_ref
  141.5 55.7 %all-to-all-done = bf16[3,256,16,2,128]{4,2,3,0,1:T(8,128)(2,1)} async-done(((bf16[3,256,16,2,128]{4,2,3,0,1:T(8,128)(2,1)}), bf16[3,256,16,2,128]{4,2,3,0,1:T(8,128)(2,1)}, u32[]{:S(2)}, u32[]{:S(2)}) %all-to-all-start) | async-done | bytes 6291488 | tf_op jit(solution)/shard_map/all_to_all | solution.py:78
  197.3 10.3 %copy.81 = bf16[3,16,256,2,128]{4,3,2,1,0:T(2,128)(2,1)} copy(bf16[3,16,256,2,128]{4,1,3,0,2:T(8,128)(2,1)} %bitcast.15) | data formatting | bytes 12582912 | tf_op jit(solution)/shard_map/transpose | solution.py:79
  207.6 10.6 %shard_map.55 = bf16[64,16,8,128]{3,2,1,0:T(8,128)(2,1)} custom-call(bf16[3,16,512,128]{3,2,1,0:T(8,128)(2,1)} %bitcast.61, bf16[3,16,512,128]{3,2,1,0:T(8,128)(2,1)} %bitcast.62, bf16[3,16,512,128]{3,2,1,0:T(8,128)(2,1)} %bitcast.63, f32[16,1,512]{2,1,0:T(1,128)} %compare_convert_fusion.mask_ref), custom_call_target="tpu_custom_call" | custom-call | flops 21474836480 | bytes 8388608 | tf_op jit(solution)/shard_map/pallas_call | solution.py:42
  218.2 0.0 copy-start.8
  218.2 5.3 %all-to-all-start.1 = ((bf16[64,16,8,128]{3,2,1,0:T(8,128)(2,1)}), bf16[64,16,8,128]{3,2,1,0:T(8,128)(2,1)S(1)}, u32[]{:S(2)}, u32[]{:S(2)}) async-start(bf16[64,16,8,128]{3,2,1,0:T(8,128)(2,1)} %shard_map.55), calls=%async_computation.1 | async-start | bytes 4194304 | tf_op jit(solution)/shard_map/all_to_all | solution.py:92
  223.5 0.0 reduce-scatter.2.cloned.1.call-start
  223.6 0.0 copy-done.8
  223.6 0.3 convert_convert_fusion
  223.8 1.3 copy.88
  225.2 0.7 fusion.6
  225.9 50.1 %all-to-all-done.1 = bf16[64,16,8,128]{3,2,1,0:T(8,128)(2,1)S(1)} async-done(((bf16[64,16,8,128]{3,2,1,0:T(8,128)(2,1)}), bf16[64,16,8,128]{3,2,1,0:T(8,128)(2,1)S(1)}, u32[]{:S(2)}, u32[]{:S(2)}) %all-to-all-start.1) | async-done | bytes 2097184 | tf_op jit(solution)/shard_map/all_to_all | solution.py:92
  275.9 0.0 copy-start.6
  275.9 1.4 copy.87
  277.3 0.0 copy-done.6
  277.3 2.6 fusion.17
  279.9 0.7 copy.90
  280.6 0.0 all-gather.5.cloned.1.call-done
  280.6 9.5 %convolution_convert_fusion = bf16[512,4096]{1,0:T(8,128)(2,1)} fusion(bf16[1024,4096]{0,1:T(8,128)(2,1)} %all-gather.5.cloned.1.call-done, bf16[64,8,8,128]{3,2,1,0:T(8,128)(2,1)S(1)} %bitcast.70), kind=kOutput, calls=%fused_computation.1 | convolution fusion | flops 4297064448 | bytes 13631488 | tf_op jit(solution)/shard_map/dot_general | solution.py:101
  290.1 0.0 copy-start.1
  290.1 0.0 reduce-scatter.2.cloned.1.call-update
  290.2 45.8 %reduce-scatter.2.cloned.1.call-done = bf16[512,1024]{1,0:T(8,128)(2,1)} async-done(((bf16[512,4096]{1,0:T(8,128)(2,1)}), bf16[512,1024]{1,0:T(8,128)(2,1)}) %reduce-scatter.2.cloned.1.call-update) | async-done | bytes 1048592 | tf_op jit(solution)/shard_map/reduce_scatter | solution.py:106
  336.0 0.0 copy-done.1
  (9 shorter events, 0.1 us)
Async XLA Ops:
  6.5 0.8 copy-start
  6.5 2.8 copy-start.2
  9.4 2.0 copy-start.3
  11.4 2.0 copy-start.4
  13.3 2.0 copy-start.5
  14.0 1.3 copy-start.7
  29.0 168.3 %all-to-all-start = ((bf16[3,256,16,2,128]{4,2,3,0,1:T(8,128)(2,1)}), bf16[3,256,16,2,128]{4,2,3,0,1:T(8,128)(2,1)}, u32[]{:S(2)}, u32[]{:S(2)}) async-start(bf16[3,256,16,2,128]{4,2,3,0,1:T(8,128)(2,1)} %copy.80), calls=%async_computation | async-start | bytes 12582912 | tf_op jit(solution)/shard_map/all_to_all | solution.py:78
  45.5 92.9 %all-gather.3.cloned.1.call-start = ((), (), s32[]{:S(2)}) async-start(), calls=%async_computation.3 | async-start | bytes 1064960 | tf_op jit(solution)/shard_map/all_gather | solution.py:81
  46.3 234.3 %all-gather.5.cloned.1.call-start = ((), (), s32[]{:S(2)}) async-start(), calls=%async_computation.4 | async-start | bytes 8519680 | tf_op jit(solution)/shard_map/all_gather | solution.py:103
  218.2 5.4 %copy-start.8 = (s32[8,512,1]{1,0,2:T(8,128)S(1)}, s32[8,512,1]{1,0,2:T(8,128)}, u32[]{:S(2)}) copy-start(s32[8,512,1]{1,0,2:T(8,128)} %copy.110) | copy-start | bytes 49156
  218.2 57.7 %all-to-all-start.1 = ((bf16[64,16,8,128]{3,2,1,0:T(8,128)(2,1)}), bf16[64,16,8,128]{3,2,1,0:T(8,128)(2,1)S(1)}, u32[]{:S(2)}, u32[]{:S(2)}) async-start(bf16[64,16,8,128]{3,2,1,0:T(8,128)(2,1)} %shard_map.55), calls=%async_computation.1 | async-start | bytes 4194304 | tf_op jit(solution)/shard_map/all_to_all | solution.py:92
  223.5 112.4 %reduce-scatter.2.cloned.1.call-start = ((), (), s32[]{:S(2)}) async-start(), calls=%async_computation.5 | async-start | bytes 5242880 | tf_op jit(solution)/shard_map/reduce_scatter | solution.py:106
  275.9 1.4 copy-start.6
  290.1 45.8 %copy-start.1 = (s32[32,512,1]{1,2,0:T(1,128)S(1)}, s32[32,512,1]{1,2,0:T(1,128)}, u32[]{:S(2)}) copy-start(s32[32,512,1]{1,2,0:T(1,128)} %param.8) | copy-start | bytes 196612
Sparse Core Ops, SparseCore 0:
  49.2 89.2 all-gather.2
  141.2 101.0 all-gather.4
  290.3 45.6 reduce-scatter.1
